TPU v7x, 256 devices: a whole 4x4x8 slice. The times are simulated.
256 devices in a mesh: exp: 64 (over y, z, core), grp: 4 (over x).
Axes of the slice: x: 4, y: 4, z: 8, core: 2. Of those that a mesh axis runs over, the one named last changes fastest.
Arguments:
- tiles: bfloat16 [1024, 256, 256], P(('exp', 'grp')), may hold values from -6 to 6
- tile_exposure: int32 [1024], P(('exp', 'grp')), may hold values from 0 to 511, as said below
- tile_patch: int32 [1024, 4], P(('exp', 'grp')), may hold values from 0 to 63, all different within a row; in each aligned block of 4 rows (0 to 3, 4 to 7, ...) at most 2 rows name the same one
- tile_offset: int32 [1024, 4, 2], P(('exp', 'grp')), may hold values from 0 to 256
- coeffs: bfloat16 [512, 10], P(('exp', 'grp')), may hold values from -2 to 2
- inv_var: bfloat16 [512], P(('exp', 'grp')), may hold values from 0.25 to 4
- vert_taps: bfloat16 [10, 41], replicated, may hold values from -1 to 1
- horiz_taps: bfloat16 [10, 41], replicated, may hold values from -1 to 1
Outputs:
- coadd: float32 [64, 512, 512], P('exp', 'grp')
Inputs may be any that keep to these rules, and one draw needn't show every extreme that they name: `tile_exposure`: each exposure is named by exactly 1024 / 512 tiles. `tile_patch`: the entries of a row differ; among the rows of one device no patch is named by more than 2 rows. `tile_offset`: each tile lies wholly inside each patch listed for it.
All inputs are finite; a program needn't handle non-finite values.
Results may differ from a plain program's by a relative error of at most 0.0041.
Values may be sent and summed in bfloat16 or wider, within the bound.
No kernel may reach another device: no remote copies, remote signals or barrier semaphores. Data moves between devices by JAX's collectives and lax.ppermute only.
A program may use at most 128 MiB of HBM per device.

v0:
```python
import math

import jax
import jax.numpy as jnp
from jax import lax
from jax.sharding import PartitionSpec as P

PS = 512


def band_matrix(filters, tile_side):
    terms, kernel_width = filters.shape
    half_width = (kernel_width - 1) // 2
    padding = tile_side - 1 - half_width
    padded = jnp.concatenate(
        [
            jnp.zeros((terms, padding), jnp.float32),
            filters.astype(jnp.float32),
            jnp.zeros((terms, padding + 1), jnp.float32),
        ],
        axis=1,
    )
    tiled = jnp.tile(padded, (1, tile_side + 1))[:, : tile_side * (2 * tile_side + 1)]
    window = tiled.reshape(terms, tile_side, 2 * tile_side + 1)[:, :, :tile_side]
    return window[:, ::-1, :].astype(jnp.bfloat16)


def coverage_rows(tags, row_count, tile_side, patch_side):
    weights = tags[:, 0].astype(jnp.float32)
    row_off = tags[:, 1].astype(jnp.int32)
    col_off = tags[:, 2].astype(jnp.int32)
    row_index = jnp.arange(row_count, dtype=jnp.int32)
    col_index = jnp.arange(patch_side, dtype=jnp.int32)
    row_mask = (
        (row_index[None, :] >= row_off[:, None])
        & (row_index[None, :] < row_off[:, None] + tile_side)
    ).astype(jnp.float32) * weights[:, None]
    col_mask = (
        (col_index[None, :] >= col_off[:, None])
        & (col_index[None, :] < col_off[:, None] + tile_side)
    ).astype(jnp.float32)
    return jnp.einsum("sy,sx->yx", row_mask, col_mask, precision=lax.Precision.HIGHEST)


def per_device(
    tiles, tile_exposure, tile_patch, tile_offset, coeffs, inv_var, vert_taps, horiz_taps
):
    n_owners = lax.axis_size("exp")
    tile_count = tiles.shape[0]
    tile_side = tiles.shape[1]
    listed = tile_patch.shape[1]
    entries = tile_count * listed
    capacity = max(2, (entries + n_owners - 1) // n_owners)
    slot_total = n_owners * capacity
    coef_all, weight_all = (
        lax.all_gather(coeffs, ("exp", "grp"), axis=0, tiled=True),
        lax.all_gather(inv_var, ("exp", "grp"), axis=0, tiled=True),
    )
    exposures = coef_all.shape[0]
    picker = (tile_exposure[:, None] == jnp.arange(exposures, dtype=jnp.int32)[None, :]).astype(
        jnp.bfloat16
    )
    coef_tile = jnp.dot(picker, coef_all, preferred_element_type=jnp.float32)
    weight_tile = jnp.dot(picker, weight_all[:, None], preferred_element_type=jnp.float32)[:, 0]
    vband = band_matrix(vert_taps, tile_side)
    hband = band_matrix(horiz_taps, tile_side)

    def convolve_one(inputs):
        one_tile, coef_row, weight = inputs
        rows_pass = jnp.einsum("yk,bxk->ybx", one_tile, hband, preferred_element_type=jnp.float32)
        partial_value = (rows_pass * coef_row[None, :, None]).astype(jnp.bfloat16)
        smoothed = jnp.einsum(
            "byk,kbx->yx", vband, partial_value, preferred_element_type=jnp.float32
        )
        return (weight * smoothed).astype(jnp.bfloat16)

    weighted = lax.map(convolve_one, (tiles, coef_tile, weight_tile))
    owners = tile_patch.reshape(entries)
    onehot = (owners[:, None] == jnp.arange(n_owners, dtype=jnp.int32)[None, :]).astype(jnp.int32)
    before = jnp.cumsum(onehot, axis=0) - onehot
    rank = jnp.sum(before * onehot, axis=1)
    target = owners * capacity + rank
    offsets = tile_offset.reshape(entries, 2)
    entry_tiles = jnp.repeat(weighted, listed, axis=0)
    entry_tags = jnp.stack(
        [
            jnp.repeat(weight_tile, listed),
            offsets[:, 0].astype(jnp.float32),
            offsets[:, 1].astype(jnp.float32),
        ],
        axis=1,
    ).astype(jnp.bfloat16)
    send_tiles = (
        jnp.zeros((slot_total, tile_side, tile_side), jnp.bfloat16).at[target].set(entry_tiles)
    )
    send_tags = jnp.zeros((slot_total, 3), jnp.bfloat16).at[target].set(entry_tags)
    got_tiles, got_tags = (
        lax.all_to_all(send_tiles, "exp", split_axis=0, concat_axis=0, tiled=True),
        lax.all_to_all(send_tags, "exp", split_axis=0, concat_axis=0, tiled=True),
    )
    got_rows = got_tags[:, 1].astype(jnp.int32)
    got_cols = got_tags[:, 2].astype(jnp.int32)
    block_slots = math.gcd(slot_total, 32)
    block_count = slot_total // block_slots
    inner = jnp.arange(tile_side, dtype=jnp.int32)
    col_index = jnp.arange(PS, dtype=jnp.int32)

    def place_block(canvas, inputs):
        block_tiles, block_rows, block_cols = inputs
        shifter = (
            col_index[None, None, :] == block_cols[:, None, None] + inner[None, :, None]
        ).astype(jnp.bfloat16)
        shifted = jnp.einsum(
            "syk,skx->syx", block_tiles, shifter, preferred_element_type=jnp.float32
        )
        row_index = (block_rows[:, None] + inner[None, :]).reshape(-1)
        canvas = canvas.at[row_index].add(shifted.reshape(-1, PS))
        return (canvas, None)

    flux, _ = lax.scan(
        place_block,
        jnp.zeros((PS, PS), jnp.float32),
        (
            got_tiles.reshape(block_count, block_slots, tile_side, tile_side),
            got_rows.reshape(block_count, block_slots),
            got_cols.reshape(block_count, block_slots),
        ),
    )
    cover = coverage_rows(got_tags, PS, tile_side, PS)
    flux_band, cover_band = (
        lax.psum_scatter(flux, "grp", scatter_dimension=0, tiled=True),
        lax.psum_scatter(cover, "grp", scatter_dimension=0, tiled=True),
    )
    coadd = flux_band / jnp.maximum(cover_band, 1.0)
    return coadd[None]


def solution(mesh):
    in_specs = (
        P(("exp", "grp"), None, None),
        P(("exp", "grp")),
        P(("exp", "grp"), None),
        P(("exp", "grp"), None, None),
        P(("exp", "grp"), None),
        P(("exp", "grp")),
        P(),
        P(),
    )
    out_specs = P("exp", "grp", None)
    return jax.shard_map(
        per_device, mesh=mesh, in_specs=in_specs, out_specs=out_specs, check_vma=False
    )
```

profile of v0, /device:TPU:8, one launch (start us, length us, event | category | flops | bytes accessed | tf_op | source)
XLA Modules:
  0.0 925.6 jit_solution(5432011449631272837)
XLA Ops:
  6.5 0.8 eq.20
  7.3 0.7 broadcast_multiply_fusion
  8.4 0.8 dynamic-update-slice
  9.2 78.6 %all-reduce = bf16[512]{0:T(512)(128)(2,1)S(1)} all-reduce(bf16[512]{0:T(512)(128)(2,1)S(1)} %dynamic-update-slice), channel_id=1, replica_groups=mesh['exp'=64,'grp'=4] {'exp','grp'}, use_global_device_ids=true, to_apply=%add | all-reduce | flops 512 | bytes 2048
  87.8 0.8 fusion.48
  88.8 0.7 copy.16
  89.7 1.2 scatter_custom_fusion.1
  90.9 8.2 all-to-all-start
  99.3 0.8 maximum_maximum_fusion.1
  100.5 1.6 copy.31
  102.1 2.1 slice.39
  104.2 8.3 reshape.146
  112.5 1.2 slice.40
  113.7 19.4 %rev.6 = bf16[10,256,256]{2,1,0:T(8,128)(2,1)} reverse(bf16[10,256,256]{2,1,0:T(8,128)(2,1)} %slice.40), dimensions={1} | reverse | bytes 2621440 | tf_op jit(solution)/shard_map/rev | solution.py:25
  133.5 1.6 copy.32
  135.1 2.1 slice.41
  137.2 8.3 reshape.147
  145.6 1.2 slice.42
  146.7 15.8 %rev.7 = bf16[10,256,256]{2,1,0:T(8,128)(2,1)S(1)} reverse(bf16[10,256,256]{2,1,0:T(8,128)(2,1)} %slice.42), dimensions={1} | reverse | bytes 2621440 | tf_op jit(solution)/shard_map/rev | solution.py:25
  162.5 89.8 %all-gather = bf16[256,2,10]{2,1,0:T(2,128)(2,1)S(1)} all-gather(bf16[1,2,10]{2,1,0:T(2,128)(2,1)S(1)} %bitcast.109), channel_id=1, replica_groups=mesh['exp'=64,'grp'=4] {'exp','grp'}, dimensions={0}, use_global_device_ids=true | all-gather | bytes 10280 | tf_op jit(solution)/shard_map/all_gather | solution.py:56
  252.5 19.2 %while.22 = (s32[]{:T(128)}, bf16[4,256,256]{2,1,0:T(8,128)(2,1)}, f32[4]{0:T(128)S(1)}, bf16[4,256,256]{2,1,0:T(8,128)(2,1)}, bf16[10,256,256]{2,1,0:T(8,128)(2...) while((s32[]{:T(128)}, bf16[4,256,256]{2,1,0:T(8,128)(2,1)}, f32[4]{0:T(128)S(1)}, ...), condition=%wide.region_3.4_spmd, body=%wide.region_2.3_spmd.sunk | while | flops 672530432 | bytes 3409629 | solution.py:77
  252.5 0.7 dynamic_slice.54
  253.2 3.3 fusion.66
  256.6 0.7 constant_dynamic-update-slice_fusion.2
  258.0 3.3 fusion.66
  261.5 0.7 constant_dynamic-update-slice_fusion.2
  262.8 3.3 fusion.66
  266.3 0.7 constant_dynamic-update-slice_fusion.2
  267.6 3.3 fusion.66
  271.1 0.7 constant_dynamic-update-slice_fusion.2
  271.7 1.2 broadcast_in_dim.30
  273.0 5.9 broadcast_in_dim.28
  278.9 5.2 scatter_fusion.1
  284.1 9.3 %all-to-all-start.1 = ((bf16[128,256,256]{2,1,0:T(8,128)(2,1)}), bf16[128,256,256]{2,1,0:T(8,128)(2,1)}, u32[]{:S(2)}, u32[]{:S(2)}) async-start(bf16[128,256,256]{2,1,0:T(8,128)(2,1)} %scatter_fusion.1), calls=%async_computation.1 | async-start | bytes 33554432 | tf_op jit(solution)/shard_map/all_to_all | solution.py:98
  294.0 1.7 fusion.25
  295.9 363.0 %all-to-all-done.1 = bf16[128,256,256]{2,1,0:T(8,128)(2,1)} async-done(((bf16[128,256,256]{2,1,0:T(8,128)(2,1)}), bf16[128,256,256]{2,1,0:T(8,128)(2,1)}, u32[]{:S(2)}, u32[]{:S(2)}) %all-to-all-start.1) | async-done | bytes 16777248 | tf_op jit(solution)/shard_map/all_to_all | solution.py:98
  659.0 234.5 %while.23 = (s32[]{:T(128)}, f32[512,512]{1,0:T(8,128)S(1)}, s32[4,32]{1,0:T(4,128)S(1)}, bf16[4,32,256,256]{3,2,1,0:T(8,128)(2,1)}, s32[4,32]{1,0:T(4,128)S(1)}, /*index=5*/s32[]{:T(128)}) while((s32[]{:T(128)}, f32[512,512]{1,0:T(8,128)S(1)}, s32[4,32]{1,0:T(4,128)S(1)}, bf16[4,32,256,256]{3,2,1,0:T(8,128)(2,1)}, ...), condition=%wide.region_8.9_spmd.clone.clone, body=%wide.region_6.8_spmd.clone.clone.sunk | while | flops 2155913216 | bytes 71566664 | solution.py:120
  659.4 8.8 fusion.70
  668.3 49.5 %scatter_fusion = f32[512,512]{1,0:T(8,128)S(1)} fusion(f32[512,512]{1,0:T(8,128)S(1)} %get-tuple-element.267, s32[8192]{0:T(1024)S(1)} %bitcast.105, f32[8192,512]{1,0:T(8,128)} %bitcast.99), kind=kCustom, calls=%fused_computation.clone.clone.1 | custom fusion | flops 4194304 | bytes 50364416 | tf_op jit(solution)/shard_map/while/body/eval_jaxpr/scatter-add | solution.py:117
  717.9 8.8 fusion.70
  726.9 49.5 %scatter_fusion = f32[512,512]{1,0:T(8,128)S(1)} fusion(f32[512,512]{1,0:T(8,128)S(1)} %get-tuple-element.267, s32[8192]{0:T(1024)S(1)} %bitcast.105, f32[8192,512]{1,0:T(8,128)} %bitcast.99), kind=kCustom, calls=%fused_computation.clone.clone.1 | custom fusion | flops 4194304 | bytes 50364416 | tf_op jit(solution)/shard_map/while/body/eval_jaxpr/scatter-add | solution.py:117
  776.5 8.8 fusion.70
  785.5 49.5 %scatter_fusion = f32[512,512]{1,0:T(8,128)S(1)} fusion(f32[512,512]{1,0:T(8,128)S(1)} %get-tuple-element.267, s32[8192]{0:T(1024)S(1)} %bitcast.105, f32[8192,512]{1,0:T(8,128)} %bitcast.99), kind=kCustom, calls=%fused_computation.clone.clone.1 | custom fusion | flops 4194304 | bytes 50364416 | tf_op jit(solution)/shard_map/while/body/eval_jaxpr/scatter-add | solution.py:117
  835.1 8.8 fusion.70
  844.1 49.5 %scatter_fusion = f32[512,512]{1,0:T(8,128)S(1)} fusion(f32[512,512]{1,0:T(8,128)S(1)} %get-tuple-element.267, s32[8192]{0:T(1024)S(1)} %bitcast.105, f32[8192,512]{1,0:T(8,128)} %bitcast.99), kind=kCustom, calls=%fused_computation.clone.clone.1 | custom fusion | flops 4194304 | bytes 50364416 | tf_op jit(solution)/shard_map/while/body/eval_jaxpr/scatter-add | solution.py:117
  893.6 1.0 copy-done
  894.6 22.4 %reduce-scatter.3.cloned.1.call-done = f32[128,512]{1,0:T(8,128)} async-done(((f32[512,512]{1,0:T(8,128)}), f32[128,512]{1,0:T(8,128)}) %reduce-scatter.3.cloned.1.call-update) | async-done | bytes 262160 | tf_op jit(solution)/shard_map/reduce_scatter | solution.py:131
  917.0 1.8 divide_bitcast_fusion
  (75 shorter events, 6.1 us)
Async XLA Ops:
  90.9 193.2 %all-to-all-start = ((bf16[64,2,3]{2,1,0:T(2,128)(2,1)}), bf16[64,2,3]{2,1,0:T(2,128)(2,1)S(1)}, u32[]{:S(2)}, u32[]{:S(2)}) async-start(bf16[64,2,3]{2,1,0:T(2,128)(2,1)} %bitcast.10), calls=%async_computation | async-start | bytes 65536 | tf_op jit(solution)/shard_map/all_to_all | solution.py:99
  145.5 17.0 %copy-start.1 = (bf16[2,10]{1,0:T(2,128)(2,1)S(1)}, bf16[2,10]{1,0:T(2,128)(2,1)}, u32[]{:S(2)}) copy-start(bf16[2,10]{1,0:T(2,128)(2,1)} %param.16) | copy-start | bytes 124
  145.5 106.8 %copy-start.2 = (s32[4]{0:T(128)S(1)}, s32[4]{0:T(128)}, u32[]{:S(2)}) copy-start(s32[4]{0:T(128)} %param.13) | copy-start | bytes 52
  284.1 374.7 %all-to-all-start.1 = ((bf16[128,256,256]{2,1,0:T(8,128)(2,1)}), bf16[128,256,256]{2,1,0:T(8,128)(2,1)}, u32[]{:S(2)}, u32[]{:S(2)}) async-start(bf16[128,256,256]{2,1,0:T(8,128)(2,1)} %scatter_fusion.1), calls=%async_computation.1 | async-start | bytes 33554432 | tf_op jit(solution)/shard_map/all_to_all | solution.py:98
  293.5 601.1 %reduce-scatter.5.cloned.1.call-start = ((), (), s32[]{:S(2)}) async-start(), calls=%async_computation.5 | async-start | bytes 1310720 | tf_op jit(solution)/shard_map/reduce_scatter | solution.py:132
  295.7 621.3 %reduce-scatter.3.cloned.1.call-start = ((), (), s32[]{:S(2)}) async-start(), calls=%async_computation.4 | async-start | bytes 1310720 | tf_op jit(solution)/shard_map/reduce_scatter | solution.py:131
  893.6 1.0 copy-start
Sparse Core Ops, SparseCore 0:
  296.9 26.3 reduce-scatter.4
  894.7 22.2 reduce-scatter.2
where the time goes:
time: 930 us; the launch traced here: 926 us
  waiting for transfers between devices  385 us (41%)
  other arithmetic  202 us (22%)
  blocking collectives  168 us (18%)
  local copies, waits for them, and re-layouts  86.4 us (9%)
  matrix products  51.4 us (6%)
  starting transfers between devices  17.7 us (2%)
  between operations  13.6 us (1%)
    all_to_all x1, waiting for transfers between devices, per_device(): lax.all_to_all(send_tiles, 'exp', split_axis=0, concat_axis=0, tiled=True)  363 us
    scatter-add x4, other arithmetic, place_block(): canvas = canvas.at[row_index].add(shifted.reshape(-1, PS))  198 us
    all_gather x1, blocking collectives, per_device(): lax.all_gather(coeffs, ('exp', 'grp'), axis=0, tiled=True)  89.8 us
    unnamed x1, blocking collectives  78.6 us
    dot_general x4, matrix products, place_block(): jnp.einsum('syk,skx->syx', block_tiles, shifter, preferred_element_type=j...  35.3 us
    rev x2, local copies, waits for them, and re-layouts, band_matrix(): return window[:, ::-1, :].astype(jnp.bfloat16)  35.2 us
    reduce_scatter x1, waiting for transfers between devices, per_device(): lax.psum_scatter(flux, 'grp', scatter_dimension=0, tiled=True)  22.4 us
  transfers between devices with their start and end apart: 4, of which 2 were waited for; matrix products, arithmetic and copies ran while one was open for 36% of the time, Pallas kernels for 0%

commit v1 on v0

v1 whole, which is shorter than its diff:
```python
import jax
import jax.numpy as jnp
from jax import lax
from jax.sharding import PartitionSpec as P

PS = 512


def band_matrix(filters, tile_side):
    terms, kernel_width = filters.shape
    half_width = (kernel_width - 1) // 2
    row = lax.broadcasted_iota(jnp.int32, (kernel_width, tile_side, tile_side), 1)
    col = lax.broadcasted_iota(jnp.int32, (kernel_width, tile_side, tile_side), 2)
    tap = lax.broadcasted_iota(jnp.int32, (kernel_width, tile_side, tile_side), 0)
    onehot = (col - row + half_width == tap).astype(jnp.bfloat16)
    band = jnp.einsum("bd,dij->bij", filters, onehot, preferred_element_type=jnp.float32)
    return band.astype(jnp.bfloat16)


def per_device(
    tiles, tile_exposure, tile_patch, tile_offset, coeffs, inv_var, vert_taps, horiz_taps
):
    n_owners = lax.axis_size("exp")
    n_bands = lax.axis_size("grp")
    tile_count, tile_side, _ = tiles.shape
    listed = tile_patch.shape[1]
    terms = coeffs.shape[1]
    band_rows = PS // n_bands
    g = lax.axis_index("grp")

    packed = jnp.concatenate([coeffs, inv_var[:, None]], axis=1)
    packed = lax.all_gather(packed, "grp", axis=0, tiled=True)
    packed = lax.all_gather(packed, "exp", axis=0, tiled=True)

    vband = band_matrix(vert_taps, tile_side)
    hband = band_matrix(horiz_taps, tile_side)

    rows_pass = jnp.einsum("tyk,bxk->tybx", tiles, hband, preferred_element_type=jnp.float32)

    exposures = packed.shape[0]
    picker = (tile_exposure[:, None] == jnp.arange(exposures, dtype=jnp.int32)[None, :]).astype(
        jnp.bfloat16
    )
    picked = jnp.dot(picker, packed, preferred_element_type=jnp.float32)
    coef_tile = picked[:, :terms]
    weight_tile = picked[:, terms]

    partial_value = (rows_pass * coef_tile[:, None, :, None]).astype(jnp.bfloat16)
    smoothed = jnp.einsum(
        "byk,tkbx->tyx", vband, partial_value, preferred_element_type=jnp.float32
    )
    weighted = (weight_tile[:, None, None] * smoothed).astype(jnp.bfloat16)

    row_off = tile_offset[:, :, 0]
    col_off = tile_offset[:, :, 1]
    band_i = lax.broadcasted_iota(jnp.int32, (n_bands, tile_count, listed, band_rows, tile_side), 0)
    inner = lax.broadcasted_iota(jnp.int32, (n_bands, tile_count, listed, band_rows, tile_side), 3)
    src = lax.broadcasted_iota(jnp.int32, (n_bands, tile_count, listed, band_rows, tile_side), 4)
    picks = (src == band_i * band_rows + inner - row_off[None, :, :, None, None]).astype(
        jnp.bfloat16
    )
    slabs = jnp.einsum("gtjiy,tyx->gtjix", picks, weighted, preferred_element_type=jnp.float32)
    slabs = slabs.astype(jnp.bfloat16).reshape(n_bands * tile_count * listed, band_rows, tile_side)
    meta = jnp.stack(
        [
            tile_patch.astype(jnp.float32),
            row_off.astype(jnp.float32),
            col_off.astype(jnp.float32),
            jnp.broadcast_to(weight_tile[:, None], (tile_count, listed)),
        ],
        axis=-1,
    ).reshape(tile_count * listed, 4)
    meta_send = jnp.broadcast_to(meta[None], (n_bands,) + meta.shape).reshape(-1, 4)
    got_slabs = lax.all_to_all(slabs, "grp", split_axis=0, concat_axis=0, tiled=True)
    got_meta = lax.all_to_all(meta_send, "grp", split_axis=0, concat_axis=0, tiled=True)
    entries = got_meta.shape[0]
    got_patch = got_meta[:, 0].astype(jnp.int32)
    got_row = got_meta[:, 1].astype(jnp.int32)
    got_col = got_meta[:, 2].astype(jnp.int32)

    x_in = lax.broadcasted_iota(jnp.int32, (entries, tile_side, PS), 1)
    x_out = lax.broadcasted_iota(jnp.int32, (entries, tile_side, PS), 2)
    shifter = (x_out == got_col[:, None, None] + x_in).astype(jnp.bfloat16)
    shifted = jnp.einsum("kyx,kxX->kyX", got_slabs, shifter, preferred_element_type=jnp.float32)
    shifted = shifted.astype(jnp.bfloat16)
    owner_of = (
        got_patch[None, :] == jnp.arange(n_owners, dtype=jnp.int32)[:, None]
    ).astype(jnp.bfloat16)
    bands = jnp.einsum("pk,kyX->pyX", owner_of, shifted, preferred_element_type=jnp.float32)
    bands = bands.astype(jnp.bfloat16)

    per_owner = n_bands * 2
    onehot = (got_patch[:, None] == jnp.arange(n_owners, dtype=jnp.int32)[None, :]).astype(
        jnp.int32
    )
    before = jnp.cumsum(onehot, axis=0) - onehot
    rank = jnp.sum(before * onehot, axis=1)
    target = got_patch * per_owner + rank
    meta_slots = (
        jnp.zeros((n_owners * per_owner, 3), jnp.float32)
        .at[target]
        .set(got_meta[:, 1:], mode="drop")
    )

    recv_bands = lax.all_to_all(bands, "exp", split_axis=0, concat_axis=0, tiled=True)
    recv_meta = lax.all_to_all(meta_slots, "exp", split_axis=0, concat_axis=0, tiled=True)

    rows = recv_meta[:, 0].astype(jnp.int32)
    cols = recv_meta[:, 1].astype(jnp.int32)
    wts = recv_meta[:, 2]
    y_index = g * band_rows + jnp.arange(band_rows, dtype=jnp.int32)
    x_index = jnp.arange(PS, dtype=jnp.int32)
    row_mask = (
        (y_index[None, :] >= rows[:, None]) & (y_index[None, :] < rows[:, None] + tile_side)
    ).astype(jnp.float32) * wts[:, None]
    col_mask = (
        (x_index[None, :] >= cols[:, None]) & (x_index[None, :] < cols[:, None] + tile_side)
    ).astype(jnp.float32)
    cover = jnp.einsum("my,mx->yx", row_mask, col_mask, precision=lax.Precision.HIGHEST)
    flux = jnp.sum(recv_bands.astype(jnp.float32), axis=0)
    coadd = flux / jnp.maximum(cover, 1.0)
    return coadd[None]


def solution(mesh):
    in_specs = (
        P(("exp", "grp"), None, None),
        P(("exp", "grp")),
        P(("exp", "grp"), None),
        P(("exp", "grp"), None, None),
        P(("exp", "grp"), None),
        P(("exp", "grp")),
        P(),
        P(),
    )
    out_specs = P("exp", "grp", None)
    return jax.shard_map(
        per_device, mesh=mesh, in_specs=in_specs, out_specs=out_specs, check_vma=False
    )
```

time: 930 us -> 391 us (0.42)
  other arithmetic: 202 us -> 7.38 us
  waiting for transfers between devices: 385 us -> 231 us
  blocking collectives: 168 us -> 62.1 us
  local copies, waits for them, and re-layouts: 86.4 us -> 23 us
  between operations: 13.6 us -> 0.14 us
  matrix products: 51.4 us -> 38.2 us
    scatter-add x4 -> x0, other arithmetic: 198 us -> none  [place_block(): canvas = canvas.at[row_index].add(shifted.reshape(-1, PS))]
    all_to_all x2 -> x4, waiting for transfers between devices: 363 us -> 231 us  [the longest x1 184 us: per_device(): lax.all_to_all(bands, 'exp', split_axis=0, concat_axis=0, tiled=True)]
    unnamed x1 -> x0, blocking collectives: 78.6 us -> none
    rev x2 -> x0, local copies, waits for them, and re-layouts: 35.2 us -> none  [band_matrix(): return window[:, ::-1, :].astype(jnp.bfloat16)]
    all_gather x1 -> x2, blocking collectives: 89.8 us -> 62.1 us  [the longest x1 52.4 us: per_device(): packed = lax.all_gather(packed, 'exp', axis=0, tiled=True)]
    reduce_scatter x2 -> x0, waiting for transfers between devices: 22.4 us -> none  [the longest x1 22.4 us: per_device(): lax.psum_scatter(flux, 'grp', scatter_dimension=0, tiled=True)]
    convert_element_type x2, local copies, waits for them, and re-layouts: 0.16 us -> 18.6 us  [the longest x1 11.3 us: per_device(): bands = bands.astype(jnp.bfloat16)]
    reshape x3 -> x0, local copies, waits for them, and re-layouts: 16.8 us -> none  [the longest x2 16.7 us: band_matrix(): tiled.reshape(terms, tile_side, 2 * tile_side + 1)[:, :, :tile_side]]
  transfers between devices with their start and end apart: 4 -> 4, of which waited for: 2 -> 2; matrix products, arithmetic and copies ran while one was open for 36% -> 15% of each run, Pallas kernels for 0% -> 0%
where the time goes in v1:
time: 391 us; the launch traced here: 388 us
  waiting for transfers between devices  231 us (59%)
  blocking collectives  62.1 us (16%)
  matrix products  38.2 us (10%)
  starting transfers between devices  25.9 us (7%)
  local copies, waits for them, and re-layouts  23 us (6%)
  other arithmetic  7.38 us (2%)
    all_to_all x1, waiting for transfers between devices, per_device(): lax.all_to_all(bands, 'exp', split_axis=0, concat_axis=0, tiled=True)  184 us
    all_gather x1, blocking collectives, per_device(): packed = lax.all_gather(packed, 'exp', axis=0, tiled=True)  52.4 us
    all_to_all x1, waiting for transfers between devices, per_device(): lax.all_to_all(slabs, 'grp', split_axis=0, concat_axis=0, tiled=True)  47.2 us
    convert_element_type x1, local copies, waits for them, and re-layouts, per_device(): bands = bands.astype(jnp.bfloat16)  11.3 us
    all_to_all x1, starting transfers between devices, per_device(): lax.all_to_all(bands, 'exp', split_axis=0, concat_axis=0, tiled=True)  10.5 us
    dot_general x1, matrix products, per_device(): jnp.einsum('kyx,kxX->kyX', got_slabs, shifter, preferred_element_type=jnp...  10.5 us
    all_gather x1, blocking collectives, per_device(): packed = lax.all_gather(packed, 'grp', axis=0, tiled=True)  9.65 us
    dot_general x1, matrix products, per_device(): jnp.einsum('pk,kyX->pyX', owner_of, shifted, preferred_element_type=jnp.f...  8.35 us
  transfers between devices with their start and end apart: 4, of which 2 were waited for; matrix products, arithmetic and copies ran while one was open for 15% of the time, Pallas kernels for 0%

profile of v1, /device:TPU:8, one launch (start us, length us, event | category | flops | bytes accessed | tf_op | source)
XLA Modules:
  0.0 388.0 jit_solution(9471603054022676226)
XLA Ops:
  0.0 0.0 copy-start
  0.0 0.0 copy-start.1
  0.0 0.8 copy.25
  0.8 0.7 maximum_bitcast_fusion.1
  1.6 9.7 %all-gather = bf16[4,2,11]{2,1,0:T(2,128)(2,1)S(1)} all-gather(bf16[1,2,11]{2,1,0:T(2,128)(2,1)S(1)} %maximum_bitcast_fusion.1), channel_id=1, replica_groups=mesh['exp'=64,'grp'=4] {'grp'}, dimensions={0}, use_global_device_ids=true | all-gather | bytes 220 | tf_op jit(solution)/shard_map/all_gather | solution.py:32
  11.2 52.4 %all_gather.7 = bf16[512,11]{1,0:T(8,128)(2,1)S(1)} all-gather(bf16[8,11]{1,0:T(8,128)(2,1)S(1)} %bitcast.85), channel_id=1, replica_groups=mesh['exp'=64,'grp'=4] {'exp'}, dimensions={0}, use_global_device_ids=true | all-gather | bytes 11440 | tf_op jit(solution)/shard_map/all_gather | solution.py:33
  63.6 0.8 fusion.67
  64.5 0.2 slice_reduce_fusion
  64.6 0.1 stack_broadcast_in_dim.7
  64.7 0.1 stack_broadcast_in_dim.8
  64.8 0.8 convert_reduce_fusion.2
  65.6 0.1 stack.14
  65.7 0.1 stack.13
  65.8 0.7 convert_element_type.88
  66.4 0.1 stack.12
  66.5 0.6 broadcast_in_dim.12
  67.2 3.2 all-to-all-start
  70.4 2.6 convert_bitcast_fusion.1
  73.0 0.1 copy.28
  73.1 0.0 copy-done.1
  73.1 3.3 convert_bitcast_fusion.2
  76.4 0.0 copy-done
  76.4 0.0 slice-start
  76.4 6.7 %fusion.37 = bf16[4,256,256,1,1]{2,1,4,3,0:T(8,128)(2,1)S(1)} fusion(bf16[10,256,256,1]{2,0,1,3:T(8,128)(2,1)S(1)} %convert_bitcast_fusion.1, f32[4,10]{0,1:T(8,128)S(1)} %copy.28, bf16[10,256,256,1]{2,0,1,3:T(8,128)(2,1)} %convert_bitcast_fusion.2, bf16[4,256,256]{2,1,0:T(8,128)(2,1)S(1)} %copy-done, f32[4]{0:T(128)S(1)} %slice_reduce_fusion), kind=kOutput, calls=%fused_computation.31 | convolution fusion | flops 2690121728 | bytes 3670192 | tf_op jit(solution)/shard_map/byk,tkbx->tyx/dot_general | solution.py:49
  83.1 0.0 slice-done
  83.1 4.3 %convert_bitcast_fusion = bf16[4,4,4,128,256]{3,4,2,0,1:T(8,128)(2,1)} fusion(bf16[4,256,256,1,1]{2,1,4,3,0:T(8,128)(2,1)S(1)} %fusion.37, s32[4,4]{1,0:T(4,128)S(1)} %bitcast.84, s32[4]{0:T(128)S(1)} %iota_multiply_fusion), kind=kOutput, calls=%fused_computation.20 | convolution fusion | flops 1082130432 | bytes 4718672 | tf_op jit(solution)/shard_map/gtjiy,tyx->gtjix/dot_general | solution.py:62
  87.5 7.3 %copy.30 = bf16[4,4,4,128,256]{4,3,2,1,0:T(8,128)(2,1)} copy(bf16[4,4,4,128,256]{3,4,2,0,1:T(8,128)(2,1)} %convert_bitcast_fusion) | data formatting | bytes 8388608 | tf_op jit(solution)/shard_map/convert_element_type | solution.py:63
  94.7 0.0 all-to-all-done
  94.7 4.8 %all-to-all-start.1 = ((bf16[64,128,256]{2,1,0:T(8,128)(2,1)}), bf16[64,128,256]{2,1,0:T(8,128)(2,1)}, u32[]{:S(2)}, u32[]{:S(2)}) async-start(bf16[64,128,256]{2,1,0:T(8,128)(2,1)} %bitcast.82), calls=%async_computation.1 | async-start | bytes 8388608 | tf_op jit(solution)/shard_map/all_to_all | solution.py:74
  99.6 0.1 all_to_all.21
  99.7 0.1 copy.33
  99.8 0.1 fusion.63
  99.9 0.1 reduce_window_sum.11
  100.0 0.2 select_reduce_fusion
  100.2 0.8 scatter_custom_fusion
  101.0 1.1 copy.34
  102.1 47.2 %all-to-all-done.1 = bf16[64,128,256]{2,1,0:T(8,128)(2,1)} async-done(((bf16[64,128,256]{2,1,0:T(8,128)(2,1)}), bf16[64,128,256]{2,1,0:T(8,128)(2,1)}, u32[]{:S(2)}, u32[]{:S(2)}) %all-to-all-start.1) | async-done | bytes 4194336 | tf_op jit(solution)/shard_map/all_to_all | solution.py:74
  149.2 7.3 %all-to-all-start.3 = ((f32[64,8,3]{1,2,0:T(4,128)}), f32[64,8,3]{1,2,0:T(4,128)S(1)}, u32[]{:S(2)}, u32[]{:S(2)}) async-start(f32[64,8,3]{1,2,0:T(4,128)} %copy.34), calls=%async_computation.3 | async-start | bytes 262144 | tf_op jit(solution)/shard_map/all_to_all | solution.py:106
  156.6 10.5 %fusion.11 = bf16[64,128,512]{2,1,0:T(8,128)(2,1)S(1)} fusion(bf16[64,128,256]{2,1,0:T(8,128)(2,1)} %all-to-all-done.1, s32[64]{0:T(128)S(1)} %get-tuple-element.13), kind=kOutput, calls=%fused_computation.15 | convolution fusion | flops 2168455168 | bytes 12583168 | tf_op jit(solution)/shard_map/kyx,kxX->kyX/dot_general | solution.py:84
  167.1 8.4 %fusion.8 = bf16[64,128,512]{2,0,1:T(8,128)(2,1)} fusion(bf16[64,128,512]{2,1,0:T(8,128)(2,1)S(1)} %fusion.11, s32[64]{0:T(128)S(1)} %get-tuple-element.12), kind=kOutput, calls=%fused_computation.14 | convolution fusion | flops 541069312 | bytes 16777472 | tf_op jit(solution)/shard_map/pk,kyX->pyX/dot_general | solution.py:89
  175.4 11.3 %copy.32 = bf16[64,128,512]{2,1,0:T(8,128)(2,1)} copy(bf16[64,128,512]{2,0,1:T(8,128)(2,1)} %fusion.8) | data formatting | bytes 16777216 | tf_op jit(solution)/shard_map/convert_element_type | solution.py:90
  186.8 0.0 all-to-all-done.3
  186.8 10.5 %all-to-all-start.2 = ((bf16[64,128,512]{2,1,0:T(8,128)(2,1)}), bf16[64,128,512]{2,1,0:T(8,128)(2,1)}, u32[]{:S(2)}, u32[]{:S(2)}) async-start(bf16[64,128,512]{2,1,0:T(8,128)(2,1)} %copy.32), calls=%async_computation.2 | async-start | bytes 16777216 | tf_op jit(solution)/shard_map/all_to_all | solution.py:105
  197.3 0.1 all_to_all.26
  197.5 184.2 %all-to-all-done.2 = bf16[64,128,512]{2,1,0:T(8,128)(2,1)} async-done(((bf16[64,128,512]{2,1,0:T(8,128)(2,1)}), bf16[64,128,512]{2,1,0:T(8,128)(2,1)}, u32[]{:S(2)}, u32[]{:S(2)}) %all-to-all-start.2) | async-done | bytes 8388640 | tf_op jit(solution)/shard_map/all_to_all | solution.py:105
  381.6 4.8 %convert_reduce_fusion = f32[128,512]{1,0:T(8,128)S(1)} fusion(bf16[64,128,512]{2,1,0:T(8,128)(2,1)} %all-to-all-done.2), kind=kLoop, calls=%fused_computation.3 | loop fusion | flops 8323072 | bytes 8650752 | tf_op jit(solution)/shard_map/reduce_sum | solution.py:120
  386.4 1.6 fusion.45
  (10 shorter events, 0.1 us)
Async XLA Ops:
  0.0 76.4 %copy-start = (bf16[4,256,256]{2,1,0:T(8,128)(2,1)S(1)}, bf16[4,256,256]{2,1,0:T(8,128)(2,1)}, u32[]{:S(2)}) copy-start(bf16[4,256,256]{2,1,0:T(8,128)(2,1)} %param.8) | copy-start | bytes 1572868
  0.0 73.1 %copy-start.1 = (bf16[10,41]{1,0:T(8,128)(2,1)S(1)}, bf16[10,41]{1,0:T(8,128)(2,1)}, u32[]{:S(2)}) copy-start(bf16[10,41]{1,0:T(8,128)(2,1)} %param.15) | copy-start | bytes 2464
  67.2 27.6 %all-to-all-start = ((f32[4,16,4]{1,2,0:T(4,128)}), f32[4,16,4]{1,2,0:T(4,128)S(1)}, u32[]{:S(2)}, u32[]{:S(2)}) async-start(f32[4,16,4]{1,2,0:T(4,128)} %broadcast_in_dim.12), calls=%async_computation | async-start | bytes 16384 | tf_op jit(solution)/shard_map/all_to_all | solution.py:75
  76.4 6.7 %slice-start = ((s32[4,4,2]{1,2,0:T(2,128)}), s32[4,4,1]{1,2,0:T(1,128)S(1)}, s32[]{:S(2)}) async-start(s32[4,4,2]{1,2,0:T(2,128)} %param.11), calls=%async_computation.4 | async-start | bytes 4096 | tf_op jit(solution)/shard_map/slice | solution.py:54
  94.7 54.5 %all-to-all-start.1 = ((bf16[64,128,256]{2,1,0:T(8,128)(2,1)}), bf16[64,128,256]{2,1,0:T(8,128)(2,1)}, u32[]{:S(2)}, u32[]{:S(2)}) async-start(bf16[64,128,256]{2,1,0:T(8,128)(2,1)} %bitcast.82), calls=%async_computation.1 | async-start | bytes 8388608 | tf_op jit(solution)/shard_map/all_to_all | solution.py:74
  149.2 37.5 %all-to-all-start.3 = ((f32[64,8,3]{1,2,0:T(4,128)}), f32[64,8,3]{1,2,0:T(4,128)S(1)}, u32[]{:S(2)}, u32[]{:S(2)}) async-start(f32[64,8,3]{1,2,0:T(4,128)} %copy.34), calls=%async_computation.3 | async-start | bytes 262144 | tf_op jit(solution)/shard_map/all_to_all | solution.py:106
  186.8 194.9 %all-to-all-start.2 = ((bf16[64,128,512]{2,1,0:T(8,128)(2,1)}), bf16[64,128,512]{2,1,0:T(8,128)(2,1)}, u32[]{:S(2)}, u32[]{:S(2)}) async-start(bf16[64,128,512]{2,1,0:T(8,128)(2,1)} %copy.32), calls=%async_computation.2 | async-start | bytes 16777216 | tf_op jit(solution)/shard_map/all_to_all | solution.py:105

commit v2 on v1

--- a/solution.py
+++ b/solution.py
@@ -29,8 +29,12 @@
     g = lax.axis_index("grp")
 
     packed = jnp.concatenate([coeffs, inv_var[:, None]], axis=1)
-    packed = lax.all_gather(packed, "grp", axis=0, tiled=True)
-    packed = lax.all_gather(packed, "exp", axis=0, tiled=True)
+    packed = jnp.broadcast_to(packed[None], (n_bands,) + packed.shape)
+    packed = lax.all_to_all(packed, "grp", split_axis=0, concat_axis=0, tiled=True)
+    packed = packed.reshape(1, -1, terms + 1)
+    packed = jnp.broadcast_to(packed, (n_owners,) + packed.shape[1:])
+    packed = lax.all_to_all(packed, "exp", split_axis=0, concat_axis=0, tiled=True)
+    packed = packed.reshape(-1, terms + 1)
 
     vband = band_matrix(vert_taps, tile_side)
     hband = band_matrix(horiz_taps, tile_side)
@@ -87,7 +91,6 @@
         got_patch[None, :] == jnp.arange(n_owners, dtype=jnp.int32)[:, None]
     ).astype(jnp.bfloat16)
     bands = jnp.einsum("pk,kyX->pyX", owner_of, shifted, preferred_element_type=jnp.float32)
-    bands = bands.astype(jnp.bfloat16)
 
     per_owner = n_bands * 2
     onehot = (got_patch[:, None] == jnp.arange(n_owners, dtype=jnp.int32)[None, :]).astype(
@@ -102,7 +105,7 @@
         .set(got_meta[:, 1:], mode="drop")
     )
 
-    recv_bands = lax.all_to_all(bands, "exp", split_axis=0, concat_axis=0, tiled=True)
+    flux = lax.psum_scatter(bands, "exp", scatter_dimension=0, tiled=True)[0]
     recv_meta = lax.all_to_all(meta_slots, "exp", split_axis=0, concat_axis=0, tiled=True)
 
     rows = recv_meta[:, 0].astype(jnp.int32)
@@ -117,7 +120,6 @@
         (x_index[None, :] >= cols[:, None]) & (x_index[None, :] < cols[:, None] + tile_side)
     ).astype(jnp.float32)
     cover = jnp.einsum("my,mx->yx", row_mask, col_mask, precision=lax.Precision.HIGHEST)
-    flux = jnp.sum(recv_bands.astype(jnp.float32), axis=0)
     coadd = flux / jnp.maximum(cover, 1.0)
     return coadd[None]
 

time: 391 us -> 360 us (0.921)
  blocking collectives: 62.1 us -> 0 us
  between operations: 0.14 us -> 13.6 us
  local copies, waits for them, and re-layouts: 23 us -> 32.3 us
  matrix products: 38.2 us -> 46.2 us
  other arithmetic: 7.38 us -> 1.16 us
  starting transfers between devices: 25.9 us -> 32.1 us
    all_to_all x1 -> x2, waiting for transfers between devices: 184 us -> 9.14 us  [the longest x1 9.13 us: per_device(): lax.all_to_all(packed, 'exp', split_axis=0, concat_axis=0, tiled=True)]
    reduce_scatter x0 -> x1, waiting for transfers between devices: none -> 166 us  [per_device(): flux = lax.psum_scatter(bands, 'exp', scatter_dimension=0, tiled=True)[0]]
    all_gather x2 -> x0, blocking collectives: 62.1 us -> none  [the longest x1 52.4 us: per_device(): packed = lax.all_gather(packed, 'exp', axis=0, tiled=True)]
    dot_general x0 -> x1, local copies, waits for them, and re-layouts: none -> 19.5 us  [per_device(): jnp.einsum('pk,kyX->pyX', owner_of, shifted, preferred_element_type=jnp.f...]
    convert_element_type x1 -> x0, local copies, waits for them, and re-layouts: 11.3 us -> none  [per_device(): bands = bands.astype(jnp.bfloat16)]
    all_to_all x1, waiting for transfers between devices: 0.01 us -> 9.39 us  [per_device(): lax.all_to_all(meta_slots, 'exp', split_axis=0, concat_axis=0, tiled=True)]
    dot_general x1, matrix products: 8.35 us -> 14.2 us  [per_device(): jnp.einsum('pk,kyX->pyX', owner_of, shifted, preferred_element_type=jnp.f...]
    all_to_all x1 -> x2, starting transfers between devices: 10.5 us -> 16.4 us  [the longest x1 12.1 us: per_device(): lax.all_to_all(packed, 'exp', split_axis=0, concat_axis=0, tiled=True)]
  transfers between devices with their start and end apart: 4 -> 6, of which waited for: 2 -> 4; matrix products, arithmetic and copies ran while one was open for 15% -> 8% of each run, Pallas kernels for 0% -> 0%
where the time goes in v2:
time: 360 us; the launch traced here: 359 us
  waiting for transfers between devices  233 us (65%)
  matrix products  46.2 us (13%)
  local copies, waits for them, and re-layouts  32.3 us (9%)
  starting transfers between devices  32.1 us (9%)
  between operations  13.6 us (4%)
    reduce_scatter x1, waiting for transfers between devices, per_device(): flux = lax.psum_scatter(bands, 'exp', scatter_dimension=0, tiled=True)[0]  166 us
    all_to_all x1, waiting for transfers between devices, per_device(): lax.all_to_all(slabs, 'grp', split_axis=0, concat_axis=0, tiled=True)  49 us
    dot_general x1, local copies, waits for them, and re-layouts, per_device(): jnp.einsum('pk,kyX->pyX', owner_of, shifted, preferred_element_type=jnp.f...  19.5 us
    dot_general x1, matrix products, per_device(): jnp.einsum('pk,kyX->pyX', owner_of, shifted, preferred_element_type=jnp.f...  14.2 us
    dot_general x1, matrix products, per_device(): jnp.einsum('kyx,kxX->kyX', got_slabs, shifter, preferred_element_type=jnp...  12.3 us
    all_to_all x1, starting transfers between devices, per_device(): lax.all_to_all(packed, 'exp', split_axis=0, concat_axis=0, tiled=True)  12.1 us
    all_to_all x1, waiting for transfers between devices, per_device(): lax.all_to_all(meta_slots, 'exp', split_axis=0, concat_axis=0, tiled=True)  9.39 us
    all_to_all x1, waiting for transfers between devices, per_device(): lax.all_to_all(packed, 'exp', split_axis=0, concat_axis=0, tiled=True)  9.13 us
  transfers between devices with their start and end apart: 6, of which 4 were waited for; matrix products, arithmetic and copies ran while one was open for 8% of the time, Pallas kernels for 0%

profile of v2, /device:TPU:8, one launch (start us, length us, event | category | flops | bytes accessed | tf_op | source)
XLA Modules:
  0.0 358.6 jit_solution(5687846017224385172)
XLA Ops:
  6.5 0.0 copy-start
  6.5 0.8 copy.25
  7.4 0.7 pad_maximum_fusion
  8.1 0.6 broadcast_in_dim.17
  8.7 4.3 %all-to-all-start = ((bf16[4,2,11]{2,1,0:T(2,128)(2,1)}), bf16[4,2,11]{2,1,0:T(2,128)(2,1)S(1)}, u32[]{:S(2)}, u32[]{:S(2)}) async-start(bf16[4,2,11]{2,1,0:T(2,128)(2,1)} %broadcast_in_dim.17), calls=%async_computation | async-start | bytes 4096 | tf_op jit(solution)/shard_map/all_to_all | solution.py:33
  13.0 2.6 convert_bitcast_fusion.1
  15.6 0.0 copy-done.3
  15.6 3.2 convert_bitcast_fusion.2
  18.9 0.0 copy-done.1
  18.9 0.0 all-to-all-done
  18.9 0.7 broadcast_in_dim.19
  19.6 12.1 %all-to-all-start.1 = ((bf16[64,8,11]{2,1,0:T(8,128)(2,1)}), bf16[64,8,11]{2,1,0:T(8,128)(2,1)S(1)}, u32[]{:S(2)}, u32[]{:S(2)}) async-start(bf16[64,8,11]{2,1,0:T(8,128)(2,1)} %broadcast_in_dim.19), calls=%async_computation.1 | async-start | bytes 262144 | tf_op jit(solution)/shard_map/all_to_all | solution.py:36
  31.7 0.1 stack.13
  31.8 0.1 stack.14
  31.9 0.0 copy-done.2
  31.9 0.1 stack.12
  32.0 9.1 %all-to-all-done.1 = bf16[64,8,11]{2,1,0:T(8,128)(2,1)S(1)} async-done(((bf16[64,8,11]{2,1,0:T(8,128)(2,1)}), bf16[64,8,11]{2,1,0:T(8,128)(2,1)S(1)}, u32[]{:S(2)}, u32[]{:S(2)}) %all-to-all-start.1) | async-done | bytes 11296 | tf_op jit(solution)/shard_map/all_to_all | solution.py:36
  41.1 0.0 copy-done.4
  41.1 0.2 fusion.53
  41.3 0.2 slice_reduce_fusion
  41.5 0.1 stack_broadcast_in_dim.7
  41.5 0.1 stack_broadcast_in_dim.8
  41.6 0.6 broadcast_in_dim.21
  42.2 4.8 %all-to-all-start.2 = ((f32[4,16,4]{1,2,0:T(4,128)}), f32[4,16,4]{1,2,0:T(4,128)S(1)}, u32[]{:S(2)}, u32[]{:S(2)}) async-start(f32[4,16,4]{1,2,0:T(4,128)} %broadcast_in_dim.21), calls=%async_computation.2 | async-start | bytes 16384 | tf_op jit(solution)/shard_map/all_to_all | solution.py:79
  47.0 0.1 copy.28
  47.1 6.7 %fusion.34 = bf16[4,256,256,1,1]{2,1,4,3,0:T(8,128)(2,1)S(1)} fusion(bf16[10,256,256,1]{2,0,1,3:T(8,128)(2,1)S(1)} %convert_bitcast_fusion.1, f32[4,10]{0,1:T(8,128)S(1)} %copy.28, bf16[10,256,256,1]{2,0,1,3:T(8,128)(2,1)} %convert_bitcast_fusion.2, bf16[4,256,256]{2,1,0:T(8,128)(2,1)S(1)} %copy-done, f32[4]{0:T(128)S(1)} %slice_reduce_fusion), kind=kOutput, calls=%fused_computation.29 | convolution fusion | flops 2690121728 | bytes 3670192 | tf_op jit(solution)/shard_map/byk,tkbx->tyx/dot_general | solution.py:53
  53.9 4.3 %convert_bitcast_fusion = bf16[4,4,4,128,256]{3,4,2,0,1:T(8,128)(2,1)} fusion(bf16[4,256,256,1,1]{2,1,4,3,0:T(8,128)(2,1)S(1)} %fusion.34, s32[4,4]{1,0:T(4,128)S(1)} %bitcast.86, s32[4]{0:T(128)S(1)} %iota_multiply_fusion), kind=kOutput, calls=%fused_computation.18 | convolution fusion | flops 1082130432 | bytes 4718672 | tf_op jit(solution)/shard_map/gtjiy,tyx->gtjix/dot_general | solution.py:66
  58.2 7.3 %copy.30 = bf16[4,4,4,128,256]{4,3,2,1,0:T(8,128)(2,1)} copy(bf16[4,4,4,128,256]{3,4,2,0,1:T(8,128)(2,1)} %convert_bitcast_fusion) | data formatting | bytes 8388608 | tf_op jit(solution)/shard_map/convert_element_type | solution.py:67
  65.4 0.0 all-to-all-done.2
  65.5 5.1 %all-to-all-start.3 = ((bf16[64,128,256]{2,1,0:T(8,128)(2,1)}), bf16[64,128,256]{2,1,0:T(8,128)(2,1)}, u32[]{:S(2)}, u32[]{:S(2)}) async-start(bf16[64,128,256]{2,1,0:T(8,128)(2,1)} %bitcast.84), calls=%async_computation.3 | async-start | bytes 8388608 | tf_op jit(solution)/shard_map/all_to_all | solution.py:78
  70.6 0.0 reduce-scatter.2.cloned.1.call-start
  70.6 0.1 all_to_all.26
  70.7 49.0 %all-to-all-done.3 = bf16[64,128,256]{2,1,0:T(8,128)(2,1)} async-done(((bf16[64,128,256]{2,1,0:T(8,128)(2,1)}), bf16[64,128,256]{2,1,0:T(8,128)(2,1)}, u32[]{:S(2)}, u32[]{:S(2)}) %all-to-all-start.3) | async-done | bytes 4194336 | tf_op jit(solution)/shard_map/all_to_all | solution.py:78
  119.7 12.3 %fusion.8 = bf16[64,128,512]{2,1,0:T(8,128)(2,1)} fusion(bf16[64,128,256]{2,1,0:T(8,128)(2,1)} %all-to-all-done.3, s32[64]{0:T(128)S(1)} %get-tuple-element.12), kind=kOutput, calls=%fused_computation.13 | convolution fusion | flops 2168455168 | bytes 12583168 | tf_op jit(solution)/shard_map/kyx,kxX->kyX/dot_general | solution.py:88
  132.0 14.2 %fusion.5 = f32[64,128,512]{2,0,1:T(8,128)S(1)} fusion(bf16[64,128,512]{2,1,0:T(8,128)(2,1)} %fusion.8, s32[64]{0:T(128)S(1)} %get-tuple-element.13), kind=kOutput, calls=%fused_computation.9 | convolution fusion | flops 536875008 | bytes 25166080 | tf_op jit(solution)/shard_map/pk,kyX->pyX/dot_general | solution.py:93
  146.3 19.5 %copy.32 = f32[64,128,512]{2,1,0:T(8,128)} copy(f32[64,128,512]{2,0,1:T(8,128)S(1)} %fusion.5) | data formatting | bytes 33554432 | tf_op jit(solution)/shard_map/pk,kyX->pyX/dot_general | solution.py:93
  165.7 0.0 reduce-scatter.2.cloned.1.call-update
  165.8 0.1 copy.33
  165.9 0.1 fusion.62
  165.9 0.1 reduce_window_sum.11
  166.0 0.2 select_reduce_fusion
  166.2 0.8 scatter_custom_fusion
  167.0 1.1 copy.34
  168.1 5.7 %all-to-all-start.4 = ((f32[64,8,3]{1,2,0:T(4,128)}), f32[64,8,3]{1,2,0:T(4,128)S(1)}, u32[]{:S(2)}, u32[]{:S(2)}) async-start(f32[64,8,3]{1,2,0:T(4,128)} %copy.34), calls=%async_computation.5 | async-start | bytes 262144 | tf_op jit(solution)/shard_map/all_to_all | solution.py:109
  173.9 9.4 %all-to-all-done.4 = f32[64,8,3]{1,2,0:T(4,128)S(1)} async-done(((f32[64,8,3]{1,2,0:T(4,128)}), f32[64,8,3]{1,2,0:T(4,128)S(1)}, u32[]{:S(2)}, u32[]{:S(2)}) %all-to-all-start.4) | async-done | bytes 6176 | tf_op jit(solution)/shard_map/all_to_all | solution.py:109
  183.3 0.1 all_to_all.30
  183.5 165.8 %reduce-scatter.2.cloned.1.call-done = f32[1,128,512]{2,1,0:T(8,128)} async-done(((f32[64,128,512]{2,1,0:T(8,128)}), f32[1,128,512]{2,1,0:T(8,128)}) %reduce-scatter.2.cloned.1.call-update) | async-done | bytes 262160 | tf_op jit(solution)/shard_map/reduce_scatter | solution.py:108
  349.2 2.5 fusion.42
  (19 shorter events, 0.1 us)
Async XLA Ops:
  6.5 40.6 %copy-start = (bf16[4,256,256]{2,1,0:T(8,128)(2,1)S(1)}, bf16[4,256,256]{2,1,0:T(8,128)(2,1)}, u32[]{:S(2)}) copy-start(bf16[4,256,256]{2,1,0:T(8,128)(2,1)} %param.8) | copy-start | bytes 1572868
  6.5 9.1 %copy-start.3 = (bf16[10,41]{1,0:T(8,128)(2,1)S(1)}, bf16[10,41]{1,0:T(8,128)(2,1)}, u32[]{:S(2)}) copy-start(bf16[10,41]{1,0:T(8,128)(2,1)} %param.15) | copy-start | bytes 2464
  8.7 10.2 %all-to-all-start = ((bf16[4,2,11]{2,1,0:T(2,128)(2,1)}), bf16[4,2,11]{2,1,0:T(2,128)(2,1)S(1)}, u32[]{:S(2)}, u32[]{:S(2)}) async-start(bf16[4,2,11]{2,1,0:T(2,128)(2,1)} %broadcast_in_dim.17), calls=%async_computation | async-start | bytes 4096 | tf_op jit(solution)/shard_map/all_to_all | solution.py:33
  13.0 5.9 %copy-start.1 = (s32[4,4,2]{1,2,0:T(2,128)S(1)}, s32[4,4,2]{1,2,0:T(2,128)}, u32[]{:S(2)}) copy-start(s32[4,4,2]{1,2,0:T(2,128)} %param.11) | copy-start | bytes 388
  13.0 18.9 %copy-start.2 = (s32[4,4]{1,0:T(4,128)S(1)}, s32[4,4]{1,0:T(4,128)}, u32[]{:S(2)}) copy-start(s32[4,4]{1,0:T(4,128)} %param.10) | copy-start | bytes 196
  13.0 28.1 %copy-start.4 = (s32[4]{0:T(128)S(1)}, s32[4]{0:T(128)}, u32[]{:S(2)}) copy-start(s32[4]{0:T(128)} %param.9) | copy-start | bytes 52
  18.9 35.0 %slice-start = ((s32[4,4,2]{1,2,0:T(2,128)}), s32[4,4,1]{1,2,0:T(1,128)S(1)}, s32[]{:S(2)}) async-start(s32[4,4,2]{1,2,0:T(2,128)} %param.11), calls=%async_computation.7 | async-start | bytes 4096 | tf_op jit(solution)/shard_map/slice | solution.py:58
  19.6 21.5 %all-to-all-start.1 = ((bf16[64,8,11]{2,1,0:T(8,128)(2,1)}), bf16[64,8,11]{2,1,0:T(8,128)(2,1)S(1)}, u32[]{:S(2)}, u32[]{:S(2)}) async-start(bf16[64,8,11]{2,1,0:T(8,128)(2,1)} %broadcast_in_dim.19), calls=%async_computation.1 | async-start | bytes 262144 | tf_op jit(solution)/shard_map/all_to_all | solution.py:36
  42.2 23.2 %all-to-all-start.2 = ((f32[4,16,4]{1,2,0:T(4,128)}), f32[4,16,4]{1,2,0:T(4,128)S(1)}, u32[]{:S(2)}, u32[]{:S(2)}) async-start(f32[4,16,4]{1,2,0:T(4,128)} %broadcast_in_dim.21), calls=%async_computation.2 | async-start | bytes 16384 | tf_op jit(solution)/shard_map/all_to_all | solution.py:79
  65.5 54.2 %all-to-all-start.3 = ((bf16[64,128,256]{2,1,0:T(8,128)(2,1)}), bf16[64,128,256]{2,1,0:T(8,128)(2,1)}, u32[]{:S(2)}, u32[]{:S(2)}) async-start(bf16[64,128,256]{2,1,0:T(8,128)(2,1)} %bitcast.84), calls=%async_computation.3 | async-start | bytes 8388608 | tf_op jit(solution)/shard_map/all_to_all | solution.py:78
  70.6 278.7 %reduce-scatter.2.cloned.1.call-start = ((), (), s32[]{:S(2)}) async-start(), calls=%async_computation.6 | async-start | bytes 17039360 | tf_op jit(solution)/shard_map/reduce_scatter | solution.py:108
  168.1 15.2 %all-to-all-start.4 = ((f32[64,8,3]{1,2,0:T(4,128)}), f32[64,8,3]{1,2,0:T(4,128)S(1)}, u32[]{:S(2)}, u32[]{:S(2)}) async-start(f32[64,8,3]{1,2,0:T(4,128)} %copy.34), calls=%async_computation.5 | async-start | bytes 262144 | tf_op jit(solution)/shard_map/all_to_all | solution.py:109
Sparse Core Ops, SparseCore 0:
  165.9 183.3 reduce-scatter.1

commit v3 on v2

--- a/solution.py
+++ b/solution.py
@@ -1,9 +1,13 @@
 import jax
 import jax.numpy as jnp
 from jax import lax
+from jax.sharding import Mesh
 from jax.sharding import PartitionSpec as P
 
 PS = 512
+EXP = ("ey", "ez", "ec")
+CHIP = ("ey", "ez")
+PAIR = ("ec", "grp")
 
 
 def band_matrix(filters, tile_side):
@@ -20,20 +24,22 @@
 def per_device(
     tiles, tile_exposure, tile_patch, tile_offset, coeffs, inv_var, vert_taps, horiz_taps
 ):
-    n_owners = lax.axis_size("exp")
+    n_owners = lax.axis_size(EXP)
     n_bands = lax.axis_size("grp")
     tile_count, tile_side, _ = tiles.shape
     listed = tile_patch.shape[1]
     terms = coeffs.shape[1]
     band_rows = PS // n_bands
     g = lax.axis_index("grp")
+    h = lax.axis_index("ec")
+    n_halves = lax.axis_size("ec")
 
     packed = jnp.concatenate([coeffs, inv_var[:, None]], axis=1)
     packed = jnp.broadcast_to(packed[None], (n_bands,) + packed.shape)
     packed = lax.all_to_all(packed, "grp", split_axis=0, concat_axis=0, tiled=True)
     packed = packed.reshape(1, -1, terms + 1)
     packed = jnp.broadcast_to(packed, (n_owners,) + packed.shape[1:])
-    packed = lax.all_to_all(packed, "exp", split_axis=0, concat_axis=0, tiled=True)
+    packed = lax.all_to_all(packed, EXP, split_axis=0, concat_axis=0, tiled=True)
     packed = packed.reshape(-1, terms + 1)
 
     vband = band_matrix(vert_taps, tile_side)
@@ -55,16 +61,18 @@
     )
     weighted = (weight_tile[:, None, None] * smoothed).astype(jnp.bfloat16)
 
+    peers = n_bands * n_halves
+    piece_rows = band_rows // n_halves
     row_off = tile_offset[:, :, 0]
     col_off = tile_offset[:, :, 1]
-    band_i = lax.broadcasted_iota(jnp.int32, (n_bands, tile_count, listed, band_rows, tile_side), 0)
-    inner = lax.broadcasted_iota(jnp.int32, (n_bands, tile_count, listed, band_rows, tile_side), 3)
-    src = lax.broadcasted_iota(jnp.int32, (n_bands, tile_count, listed, band_rows, tile_side), 4)
-    picks = (src == band_i * band_rows + inner - row_off[None, :, :, None, None]).astype(
-        jnp.bfloat16
-    )
-    slabs = jnp.einsum("gtjiy,tyx->gtjix", picks, weighted, preferred_element_type=jnp.float32)
-    slabs = slabs.astype(jnp.bfloat16).reshape(n_bands * tile_count * listed, band_rows, tile_side)
+    shape5 = (peers, tile_count, listed, piece_rows, tile_side)
+    dest = lax.broadcasted_iota(jnp.int32, shape5, 0)
+    inner = lax.broadcasted_iota(jnp.int32, shape5, 3)
+    src = lax.broadcasted_iota(jnp.int32, shape5, 4)
+    first_row = (dest % n_bands) * band_rows + (dest // n_bands) * piece_rows
+    picks = (src == first_row + inner - row_off[None, :, :, None, None]).astype(jnp.bfloat16)
+    slabs = jnp.einsum("dtjiy,tyx->dtjix", picks, weighted, preferred_element_type=jnp.float32)
+    slabs = slabs.astype(jnp.bfloat16).reshape(peers * tile_count * listed, piece_rows, tile_side)
     meta = jnp.stack(
         [
             tile_patch.astype(jnp.float32),
@@ -74,12 +82,11 @@
         ],
         axis=-1,
     ).reshape(tile_count * listed, 4)
-    meta_send = jnp.broadcast_to(meta[None], (n_bands,) + meta.shape).reshape(-1, 4)
-    got_slabs = lax.all_to_all(slabs, "grp", split_axis=0, concat_axis=0, tiled=True)
-    got_meta = lax.all_to_all(meta_send, "grp", split_axis=0, concat_axis=0, tiled=True)
+    meta_send = jnp.broadcast_to(meta[None], (peers,) + meta.shape).reshape(-1, 4)
+    got_slabs = lax.all_to_all(slabs, PAIR, split_axis=0, concat_axis=0, tiled=True)
+    got_meta = lax.all_to_all(meta_send, PAIR, split_axis=0, concat_axis=0, tiled=True)
     entries = got_meta.shape[0]
     got_patch = got_meta[:, 0].astype(jnp.int32)
-    got_row = got_meta[:, 1].astype(jnp.int32)
     got_col = got_meta[:, 2].astype(jnp.int32)
 
     x_in = lax.broadcasted_iota(jnp.int32, (entries, tile_side, PS), 1)
@@ -90,23 +97,36 @@
     owner_of = (
         got_patch[None, :] == jnp.arange(n_owners, dtype=jnp.int32)[:, None]
     ).astype(jnp.bfloat16)
-    bands = jnp.einsum("pk,kyX->pyX", owner_of, shifted, preferred_element_type=jnp.float32)
+    pieces = jnp.einsum("pk,kyX->pyX", owner_of, shifted, preferred_element_type=jnp.float32)
 
-    per_owner = n_bands * 2
+    per_owner = peers * 2
     onehot = (got_patch[:, None] == jnp.arange(n_owners, dtype=jnp.int32)[None, :]).astype(
         jnp.int32
     )
     before = jnp.cumsum(onehot, axis=0) - onehot
     rank = jnp.sum(before * onehot, axis=1)
     target = got_patch * per_owner + rank
+    keep = (h == 0).astype(jnp.float32)
+    meta_cover = jnp.concatenate([got_meta[:, 1:3], got_meta[:, 3:4] * keep], axis=1)
     meta_slots = (
         jnp.zeros((n_owners * per_owner, 3), jnp.float32)
         .at[target]
-        .set(got_meta[:, 1:], mode="drop")
+        .set(meta_cover, mode="drop")
     )
 
-    flux = lax.psum_scatter(bands, "exp", scatter_dimension=0, tiled=True)[0]
-    recv_meta = lax.all_to_all(meta_slots, "exp", split_axis=0, concat_axis=0, tiled=True)
+    chips = n_owners // n_halves
+    pieces = pieces.reshape(chips, n_halves, piece_rows, PS)
+    mine = lax.psum_scatter(pieces, CHIP, scatter_dimension=0, tiled=True)[0]
+    other = lax.ppermute(
+        jnp.where(h == 0, mine[1], mine[0]), "ec", perm=[(0, 1), (1, 0)]
+    )
+    own_half = jnp.where(h == 0, mine[0], mine[1])
+    flux = jnp.where(
+        h == 0,
+        jnp.concatenate([own_half, other], axis=0),
+        jnp.concatenate([other, own_half], axis=0),
+    )
+    recv_meta = lax.all_to_all(meta_slots, EXP, split_axis=0, concat_axis=0, tiled=True)
 
     rows = recv_meta[:, 0].astype(jnp.int32)
     cols = recv_meta[:, 1].astype(jnp.int32)
@@ -125,17 +145,22 @@
 
 
 def solution(mesh):
+    n_exp, n_grp = mesh.devices.shape
+    n_core = 2
+    n_y = 4
+    split = Mesh(mesh.devices.reshape(n_y, n_exp // (n_y * n_core), n_core, n_grp), EXP + ("grp",))
+    every = EXP + ("grp",)
     in_specs = (
-        P(("exp", "grp"), None, None),
-        P(("exp", "grp")),
-        P(("exp", "grp"), None),
-        P(("exp", "grp"), None, None),
-        P(("exp", "grp"), None),
-        P(("exp", "grp")),
+        P(every, None, None),
+        P(every),
+        P(every, None),
+        P(every, None, None),
+        P(every, None),
+        P(every),
         P(),
         P(),
     )
-    out_specs = P("exp", "grp", None)
+    out_specs = P(EXP, "grp", None)
     return jax.shard_map(
-        per_device, mesh=mesh, in_specs=in_specs, out_specs=out_specs, check_vma=False
+        per_device, mesh=split, in_specs=in_specs, out_specs=out_specs, check_vma=False
     )

time: 360 us -> 386 us (1.072)
  waiting for transfers between devices: 233 us -> 276 us
  local copies, waits for them, and re-layouts: 32.3 us -> 16.4 us
    reduce_scatter x1, waiting for transfers between devices: 166 us -> 207 us  [per_device(): mine = lax.psum_scatter(pieces, CHIP, scatter_dimension=0, tiled=True)[0]]
    dot_general x1 -> x0, local copies, waits for them, and re-layouts: 19.5 us -> none  [per_device(): jnp.einsum('pk,kyX->pyX', owner_of, shifted, preferred_element_type=jnp.f...]
    reshape x0 -> x1, local copies, waits for them, and re-layouts: none -> 8.3 us  [per_device(): pieces = pieces.reshape(chips, n_halves, piece_rows, PS)]
    convert_element_type x1, local copies, waits for them, and re-layouts: 7.25 us -> 2.28 us  [per_device(): slabs.astype(jnp.bfloat16)]
    dot_general x1, matrix products: 14.2 us -> 9.86 us  [per_device(): jnp.einsum('pk,kyX->pyX', owner_of, shifted, preferred_element_type=jnp.f...]
  transfers between devices with their start and end apart: 6 -> 7, of which waited for: 4 -> 5; matrix products, arithmetic and copies ran while one was open for 8% -> 5% of each run, Pallas kernels for 0% -> 0%
where the time goes in v3:
time: 386 us; the launch traced here: 383 us
  waiting for transfers between devices  276 us (72%)
  matrix products  42.8 us (11%)
  starting transfers between devices  32.2 us (8%)
  local copies, waits for them, and re-layouts  16.4 us (4%)
  between operations  13.6 us (4%)
    reduce_scatter x1, waiting for transfers between devices, per_device(): mine = lax.psum_scatter(pieces, CHIP, scatter_dimension=0, tiled=True)[0]  207 us
    all_to_all x1, waiting for transfers between devices, per_device(): lax.all_to_all(slabs, PAIR, split_axis=0, concat_axis=0, tiled=True)  48.8 us
    dot_general x1, matrix products, per_device(): jnp.einsum('kyx,kxX->kyX', got_slabs, shifter, preferred_element_type=jnp...  15.8 us
    all_to_all x1, starting transfers between devices, per_device(): lax.all_to_all(packed, EXP, split_axis=0, concat_axis=0, tiled=True)  12.1 us
    dot_general x1, matrix products, per_device(): jnp.einsum('pk,kyX->pyX', owner_of, shifted, preferred_element_type=jnp.f...  9.86 us
    all_to_all x1, waiting for transfers between devices, per_device(): lax.all_to_all(meta_slots, EXP, split_axis=0, concat_axis=0, tiled=True)  9.83 us
    all_to_all x1, waiting for transfers between devices, per_device(): lax.all_to_all(packed, EXP, split_axis=0, concat_axis=0, tiled=True)  9.13 us
    reshape x1, local copies, waits for them, and re-layouts, per_device(): pieces = pieces.reshape(chips, n_halves, piece_rows, PS)  8.3 us
  transfers between devices with their start and end apart: 7, of which 5 were waited for; matrix products, arithmetic and copies ran while one was open for 5% of the time, Pallas kernels for 0%

profile of v3, /device:TPU:8, one launch (start us, length us, event | category | flops | bytes accessed | tf_op | source)
XLA Modules:
  0.0 383.0 jit_solution(14040440785005276860)
XLA Ops:
  6.5 0.8 copy.28
  7.4 0.7 pad_maximum_fusion.1
  8.1 0.6 broadcast_in_dim.17
  8.7 4.3 %all-to-all-start = ((bf16[4,2,11]{2,1,0:T(2,128)(2,1)}), bf16[4,2,11]{2,1,0:T(2,128)(2,1)S(1)}, u32[]{:S(2)}, u32[]{:S(2)}) async-start(bf16[4,2,11]{2,1,0:T(2,128)(2,1)} %broadcast_in_dim.17), calls=%async_computation | async-start | bytes 4096 | tf_op jit(solution)/shard_map/all_to_all | solution.py:39
  13.0 0.0 copy-start.4
  13.0 2.6 convert_bitcast_fusion.1
  15.6 0.0 copy-done.3
  15.6 3.2 convert_bitcast_fusion.2
  18.9 0.0 all-to-all-done
  18.9 0.7 broadcast_in_dim.19
  19.6 12.1 %all-to-all-start.1 = ((bf16[64,8,11]{2,1,0:T(8,128)(2,1)}), bf16[64,8,11]{2,1,0:T(8,128)(2,1)S(1)}, u32[]{:S(2)}, u32[]{:S(2)}) async-start(bf16[64,8,11]{2,1,0:T(8,128)(2,1)} %broadcast_in_dim.19), calls=%async_computation.1 | async-start | bytes 262144 | tf_op jit(solution)/shard_map/all_to_all | solution.py:42
  31.7 0.1 stack.14
  31.8 0.1 stack.13
  31.9 0.1 stack.12
  32.0 9.1 %all-to-all-done.1 = bf16[64,8,11]{2,1,0:T(8,128)(2,1)S(1)} async-done(((bf16[64,8,11]{2,1,0:T(8,128)(2,1)}), bf16[64,8,11]{2,1,0:T(8,128)(2,1)S(1)}, u32[]{:S(2)}, u32[]{:S(2)}) %all-to-all-start.1) | async-done | bytes 11296 | tf_op jit(solution)/shard_map/all_to_all | solution.py:42
  41.1 0.2 fusion.75
  41.3 0.2 slice_reduce_fusion
  41.5 0.1 copy.31
  41.6 0.1 stack_broadcast_in_dim.7
  41.7 0.1 stack_broadcast_in_dim.8
  41.8 0.6 broadcast_in_dim.21
  42.4 4.8 %all-to-all-start.2 = ((f32[8,16,4]{1,2,0:T(4,128)}), f32[8,16,4]{1,2,0:T(4,128)S(1)}, u32[]{:S(2)}, u32[]{:S(2)}) async-start(f32[8,16,4]{1,2,0:T(4,128)} %broadcast_in_dim.21), calls=%async_computation.2 | async-start | bytes 32768 | tf_op jit(solution)/shard_map/all_to_all | solution.py:87
  47.2 6.9 %fusion.44 = bf16[4,256,256,1,1]{2,1,4,3,0:T(8,128)(2,1)S(1)} fusion(bf16[10,256,256,1]{2,0,1,3:T(8,128)(2,1)S(1)} %convert_bitcast_fusion.1, f32[4,10]{0,1:T(8,128)S(1)} %copy.31, bf16[10,256,256,1]{2,0,1,3:T(8,128)(2,1)} %convert_bitcast_fusion.2, bf16[4,256,256]{2,1,0:T(8,128)(2,1)S(1)} %copy-done, f32[4]{0:T(128)S(1)} %slice_reduce_fusion), kind=kOutput, calls=%fused_computation.40 | convolution fusion | flops 2690121728 | bytes 3670192 | tf_op jit(solution)/shard_map/byk,tkbx->tyx/dot_general | solution.py:59
  54.1 1.9 convert_bitcast_fusion
  56.0 2.3 copy.33
  58.3 0.0 all-to-all-done.2
  58.3 4.8 %all-to-all-start.3 = ((bf16[128,64,256]{2,1,0:T(8,128)(2,1)}), bf16[128,64,256]{2,1,0:T(8,128)(2,1)}, u32[]{:S(2)}, u32[]{:S(2)}) async-start(bf16[128,64,256]{2,1,0:T(8,128)(2,1)} %bitcast.88), calls=%async_computation.3 | async-start | bytes 8388608 | tf_op jit(solution)/shard_map/all_to_all | solution.py:86
  63.1 0.2 reduce-scatter.2.cloned.1.call-start
  63.4 0.1 all_to_all.26
  63.5 48.8 %all-to-all-done.3 = bf16[128,64,256]{2,1,0:T(8,128)(2,1)} async-done(((bf16[128,64,256]{2,1,0:T(8,128)(2,1)}), bf16[128,64,256]{2,1,0:T(8,128)(2,1)}, u32[]{:S(2)}, u32[]{:S(2)}) %all-to-all-start.3) | async-done | bytes 4194336 | tf_op jit(solution)/shard_map/all_to_all | solution.py:86
  112.3 15.8 %fusion.8 = bf16[128,64,512]{2,1,0:T(8,128)(2,1)S(1)} fusion(bf16[128,64,256]{2,1,0:T(8,128)(2,1)} %all-to-all-done.3, s32[128]{0:T(128)S(1)} %get-tuple-element.15), kind=kOutput, calls=%fused_computation.13 | convolution fusion | flops 2185232384 | bytes 12583424 | tf_op jit(solution)/shard_map/kyx,kxX->kyX/dot_general | solution.py:95
  128.1 9.9 %fusion.5 = f32[64,64,512]{2,0,1:T(8,128)S(1)} fusion(bf16[128,64,512]{2,1,0:T(8,128)(2,1)S(1)} %fusion.8, s32[128]{0:T(128)S(1)} %get-tuple-element.16), kind=kOutput, calls=%fused_computation.9 | convolution fusion | flops 536879104 | bytes 16777728 | tf_op jit(solution)/shard_map/pk,kyX->pyX/dot_general | solution.py:100
  138.0 8.3 %copy.46 = f32[64,64,512]{2,1,0:T(8,128)} copy(f32[64,64,512]{2,0,1:T(8,128)S(1)} %fusion.5) | data formatting | bytes 16777216 | tf_op jit(solution)/shard_map/reshape | solution.py:118
  146.3 0.0 reduce-scatter.2.cloned.1.call-update
  146.3 0.1 fusion.77
  146.4 0.2 reduce_window_sum.11
  146.6 0.1 copy.36
  146.7 0.2 select_reduce_fusion
  146.9 1.0 scatter_custom_fusion
  147.9 1.1 copy.37
  149.0 5.8 %all-to-all-start.4 = ((f32[64,16,3]{1,2,0:T(4,128)}), f32[64,16,3]{1,2,0:T(4,128)S(1)}, u32[]{:S(2)}, u32[]{:S(2)}) async-start(f32[64,16,3]{1,2,0:T(4,128)} %copy.37), calls=%async_computation.5 | async-start | bytes 262144 | tf_op jit(solution)/shard_map/all_to_all | solution.py:129
  154.8 9.8 %all-to-all-done.4 = f32[64,16,3]{1,2,0:T(4,128)S(1)} async-done(((f32[64,16,3]{1,2,0:T(4,128)}), f32[64,16,3]{1,2,0:T(4,128)S(1)}, u32[]{:S(2)}, u32[]{:S(2)}) %all-to-all-start.4) | async-done | bytes 12320 | tf_op jit(solution)/shard_map/all_to_all | solution.py:129
  164.7 0.1 all_to_all.30
  164.8 206.6 %reduce-scatter.2.cloned.1.call-done = f32[1,2,64,512]{3,2,1,0:T(8,128)} async-done(((f32[32,2,64,512]{3,2,1,0:T(8,128)}), f32[1,2,64,512]{3,2,1,0:T(8,128)}) %reduce-scatter.2.cloned.1.call-update) | async-done | bytes 262160 | tf_op jit(solution)/shard_map/reduce_scatter | solution.py:119
  371.4 1.0 select_bitcast_fusion.1
  372.4 0.1 collective-permute-start
  372.6 1.3 collective-permute-done
  373.9 2.3 fusion.63
  (25 shorter events, 0.1 us)
Async XLA Ops:
  6.5 40.6 %copy-start = (bf16[4,256,256]{2,1,0:T(8,128)(2,1)S(1)}, bf16[4,256,256]{2,1,0:T(8,128)(2,1)}, u32[]{:S(2)}) copy-start(bf16[4,256,256]{2,1,0:T(8,128)(2,1)} %param.8) | copy-start | bytes 1572868
  6.5 9.1 %copy-start.3 = (bf16[10,41]{1,0:T(8,128)(2,1)S(1)}, bf16[10,41]{1,0:T(8,128)(2,1)}, u32[]{:S(2)}) copy-start(bf16[10,41]{1,0:T(8,128)(2,1)} %param.15) | copy-start | bytes 2464
  8.7 10.2 %all-to-all-start = ((bf16[4,2,11]{2,1,0:T(2,128)(2,1)}), bf16[4,2,11]{2,1,0:T(2,128)(2,1)S(1)}, u32[]{:S(2)}, u32[]{:S(2)}) async-start(bf16[4,2,11]{2,1,0:T(2,128)(2,1)} %broadcast_in_dim.17), calls=%async_computation | async-start | bytes 4096 | tf_op jit(solution)/shard_map/all_to_all | solution.py:39
  13.0 5.9 %copy-start.1 = (s32[4,4,2]{1,2,0:T(2,128)S(1)}, s32[4,4,2]{1,2,0:T(2,128)}, u32[]{:S(2)}) copy-start(s32[4,4,2]{1,2,0:T(2,128)} %param.11) | copy-start | bytes 388
  13.0 18.9 %copy-start.2 = (s32[4,4]{1,0:T(4,128)S(1)}, s32[4,4]{1,0:T(4,128)}, u32[]{:S(2)}) copy-start(s32[4,4]{1,0:T(4,128)} %param.10) | copy-start | bytes 196
  13.0 28.1 %copy-start.4 = (s32[4]{0:T(128)S(1)}, s32[4]{0:T(128)}, u32[]{:S(2)}) copy-start(s32[4]{0:T(128)} %param.9) | copy-start | bytes 52
  18.9 35.2 %slice-start = ((s32[4,4,2]{1,2,0:T(2,128)}), s32[4,4,1]{1,2,0:T(1,128)S(1)}, s32[]{:S(2)}) async-start(s32[4,4,2]{1,2,0:T(2,128)} %param.11), calls=%async_computation.7 | async-start | bytes 4096 | tf_op jit(solution)/shard_map/slice | solution.py:66
  19.6 21.5 %all-to-all-start.1 = ((bf16[64,8,11]{2,1,0:T(8,128)(2,1)}), bf16[64,8,11]{2,1,0:T(8,128)(2,1)S(1)}, u32[]{:S(2)}, u32[]{:S(2)}) async-start(bf16[64,8,11]{2,1,0:T(8,128)(2,1)} %broadcast_in_dim.19), calls=%async_computation.1 | async-start | bytes 262144 | tf_op jit(solution)/shard_map/all_to_all | solution.py:42
  42.4 15.9 %all-to-all-start.2 = ((f32[8,16,4]{1,2,0:T(4,128)}), f32[8,16,4]{1,2,0:T(4,128)S(1)}, u32[]{:S(2)}, u32[]{:S(2)}) async-start(f32[8,16,4]{1,2,0:T(4,128)} %broadcast_in_dim.21), calls=%async_computation.2 | async-start | bytes 32768 | tf_op jit(solution)/shard_map/all_to_all | solution.py:87
  58.3 54.0 %all-to-all-start.3 = ((bf16[128,64,256]{2,1,0:T(8,128)(2,1)}), bf16[128,64,256]{2,1,0:T(8,128)(2,1)}, u32[]{:S(2)}, u32[]{:S(2)}) async-start(bf16[128,64,256]{2,1,0:T(8,128)(2,1)} %bitcast.88), calls=%async_computation.3 | async-start | bytes 8388608 | tf_op jit(solution)/shard_map/all_to_all | solution.py:86
  63.1 308.3 %reduce-scatter.2.cloned.1.call-start = ((), (), s32[]{:S(2)}) async-start(), calls=%async_computation.6 | async-start | bytes 8650752 | tf_op jit(solution)/shard_map/reduce_scatter | solution.py:119
  149.0 15.7 %all-to-all-start.4 = ((f32[64,16,3]{1,2,0:T(4,128)}), f32[64,16,3]{1,2,0:T(4,128)S(1)}, u32[]{:S(2)}, u32[]{:S(2)}) async-start(f32[64,16,3]{1,2,0:T(4,128)} %copy.37), calls=%async_computation.5 | async-start | bytes 262144 | tf_op jit(solution)/shard_map/all_to_all | solution.py:129
  372.4 1.4 collective-permute-start
Sparse Core Ops, SparseCore 0:
  146.4 224.9 reduce-scatter.1

commit v4 on v2

--- a/solution.py
+++ b/solution.py
@@ -55,16 +55,10 @@
     )
     weighted = (weight_tile[:, None, None] * smoothed).astype(jnp.bfloat16)
 
+    n_chunks = 2
+    chunk_rows = band_rows // n_chunks
     row_off = tile_offset[:, :, 0]
     col_off = tile_offset[:, :, 1]
-    band_i = lax.broadcasted_iota(jnp.int32, (n_bands, tile_count, listed, band_rows, tile_side), 0)
-    inner = lax.broadcasted_iota(jnp.int32, (n_bands, tile_count, listed, band_rows, tile_side), 3)
-    src = lax.broadcasted_iota(jnp.int32, (n_bands, tile_count, listed, band_rows, tile_side), 4)
-    picks = (src == band_i * band_rows + inner - row_off[None, :, :, None, None]).astype(
-        jnp.bfloat16
-    )
-    slabs = jnp.einsum("gtjiy,tyx->gtjix", picks, weighted, preferred_element_type=jnp.float32)
-    slabs = slabs.astype(jnp.bfloat16).reshape(n_bands * tile_count * listed, band_rows, tile_side)
     meta = jnp.stack(
         [
             tile_patch.astype(jnp.float32),
@@ -75,22 +69,44 @@
         axis=-1,
     ).reshape(tile_count * listed, 4)
     meta_send = jnp.broadcast_to(meta[None], (n_bands,) + meta.shape).reshape(-1, 4)
-    got_slabs = lax.all_to_all(slabs, "grp", split_axis=0, concat_axis=0, tiled=True)
     got_meta = lax.all_to_all(meta_send, "grp", split_axis=0, concat_axis=0, tiled=True)
     entries = got_meta.shape[0]
     got_patch = got_meta[:, 0].astype(jnp.int32)
-    got_row = got_meta[:, 1].astype(jnp.int32)
     got_col = got_meta[:, 2].astype(jnp.int32)
-
+    owner_of = (
+        got_patch[None, :] == jnp.arange(n_owners, dtype=jnp.int32)[:, None]
+    ).astype(jnp.bfloat16)
     x_in = lax.broadcasted_iota(jnp.int32, (entries, tile_side, PS), 1)
     x_out = lax.broadcasted_iota(jnp.int32, (entries, tile_side, PS), 2)
     shifter = (x_out == got_col[:, None, None] + x_in).astype(jnp.bfloat16)
-    shifted = jnp.einsum("kyx,kxX->kyX", got_slabs, shifter, preferred_element_type=jnp.float32)
-    shifted = shifted.astype(jnp.bfloat16)
-    owner_of = (
-        got_patch[None, :] == jnp.arange(n_owners, dtype=jnp.int32)[:, None]
-    ).astype(jnp.bfloat16)
-    bands = jnp.einsum("pk,kyX->pyX", owner_of, shifted, preferred_element_type=jnp.float32)
+
+    flat_weighted = weighted.reshape(tile_count * tile_side, tile_side)
+    shape6 = (n_bands, tile_count, listed, chunk_rows, tile_count, tile_side)
+    band_i = lax.broadcasted_iota(jnp.int32, shape6, 0)
+    tile_i = lax.broadcasted_iota(jnp.int32, shape6, 1)
+    inner = lax.broadcasted_iota(jnp.int32, shape6, 3)
+    tile_k = lax.broadcasted_iota(jnp.int32, shape6, 4)
+    src = lax.broadcasted_iota(jnp.int32, shape6, 5)
+    flux_chunks = []
+    for c in range(n_chunks):
+        first = band_i * band_rows + c * chunk_rows + inner
+        picks = (
+            (tile_i == tile_k) & (src == first - row_off[None, :, :, None, None, None])
+        ).astype(jnp.bfloat16)
+        picks = picks.reshape(n_bands * tile_count * listed * chunk_rows, tile_count * tile_side)
+        slabs = jnp.dot(picks, flat_weighted, preferred_element_type=jnp.float32)
+        slabs = slabs.astype(jnp.bfloat16).reshape(
+            n_bands * tile_count * listed, chunk_rows, tile_side
+        )
+        got_slabs = lax.all_to_all(slabs, "grp", split_axis=0, concat_axis=0, tiled=True)
+        shifted = jnp.einsum(
+            "kyx,kxX->kyX", got_slabs, shifter, preferred_element_type=jnp.float32
+        ).astype(jnp.bfloat16)
+        bands = jnp.dot(
+            owner_of, shifted.reshape(entries, chunk_rows * PS), preferred_element_type=jnp.float32
+        ).reshape(n_owners, chunk_rows, PS)
+        flux_chunks.append(lax.psum_scatter(bands, "exp", scatter_dimension=0, tiled=True)[0])
+    flux = jnp.concatenate(flux_chunks, axis=0)
 
     per_owner = n_bands * 2
     onehot = (got_patch[:, None] == jnp.arange(n_owners, dtype=jnp.int32)[None, :]).astype(
@@ -104,8 +120,6 @@
         .at[target]
         .set(got_meta[:, 1:], mode="drop")
     )
-
-    flux = lax.psum_scatter(bands, "exp", scatter_dimension=0, tiled=True)[0]
     recv_meta = lax.all_to_all(meta_slots, "exp", split_axis=0, concat_axis=0, tiled=True)
 
     rows = recv_meta[:, 0].astype(jnp.int32)

time: 360 us -> 430 us (1.19); the launches traced: 359 us -> 421 us
  blocking collectives: 0 us -> 38.5 us
  waiting for transfers between devices: 233 us -> 262 us
  local copies, waits for them, and re-layouts: 32.3 us -> 21.9 us
  matrix products: 46.2 us -> 51 us
    reduce_scatter x1 -> x2, waiting for transfers between devices: 166 us -> 217 us  [per_device(): lax.psum_scatter(bands, 'exp', scatter_dimension=0, tiled=True)[0]]
    all_to_all x0 -> x1, blocking collectives: none -> 38.5 us  [per_device(): lax.all_to_all(slabs, 'grp', split_axis=0, concat_axis=0, tiled=True)]
    all_to_all x1, waiting for transfers between devices: 49 us -> 25.7 us  [per_device(): lax.all_to_all(slabs, 'grp', split_axis=0, concat_axis=0, tiled=True)]
    convert_element_type x1 -> x0, local copies, waits for them, and re-layouts: 7.25 us -> none  [per_device(): slabs.astype(jnp.bfloat16)]
    dot_general x1 -> x2, local copies, waits for them, and re-layouts: 19.5 us -> 16.2 us  [per_device(): jnp.dot(owner_of, shifted.reshape(entries, chunk_rows * PS), preferred_el...]
    dot_general x2 -> x4, matrix products: 18.6 us -> 21.4 us  [the longest x2 11 us: per_device(): jnp.dot(owner_of, shifted.reshape(entries, chunk_rows * PS), preferred_el...]
    dot_general x1 -> x2, matrix products: 12.3 us -> 14 us  [per_device(): jnp.einsum('kyx,kxX->kyX', got_slabs, shifter, preferred_element_type=jnp...]
  transfers between devices with their start and end apart: 6 -> 7, of which waited for: 4 -> 5; matrix products, arithmetic and copies ran while one was open for 8% -> 11% of each run, Pallas kernels for 0% -> 0%
where the time goes in v4:
time: 430 us; the launch traced here: 421 us
  waiting for transfers between devices  262 us (61%)
  matrix products  51 us (12%)
  blocking collectives  38.5 us (9%)
  starting transfers between devices  32 us (7%)
  local copies, waits for them, and re-layouts  21.9 us (5%)
  between operations  13.8 us (3%)
    reduce_scatter x2, waiting for transfers between devices, per_device(): lax.psum_scatter(bands, 'exp', scatter_dimension=0, tiled=True)[0]  217 us
    all_to_all x1, blocking collectives, per_device(): lax.all_to_all(slabs, 'grp', split_axis=0, concat_axis=0, tiled=True)  38.5 us
    all_to_all x1, waiting for transfers between devices, per_device(): lax.all_to_all(slabs, 'grp', split_axis=0, concat_axis=0, tiled=True)  25.7 us
    dot_general x2, local copies, waits for them, and re-layouts, per_device(): jnp.dot(owner_of, shifted.reshape(entries, chunk_rows * PS), preferred_el...  16.2 us
    dot_general x2, matrix products, per_device(): jnp.einsum('kyx,kxX->kyX', got_slabs, shifter, preferred_element_type=jnp...  14 us
    all_to_all x1, starting transfers between devices, per_device(): lax.all_to_all(packed, 'exp', split_axis=0, concat_axis=0, tiled=True)  12.1 us
    dot_general x2, matrix products, per_device(): jnp.dot(owner_of, shifted.reshape(entries, chunk_rows * PS), preferred_el...  11 us
    dot_general x2, matrix products, per_device(): slabs = jnp.dot(picks, flat_weighted, preferred_element_type=jnp.float32)  10.4 us
  transfers between devices with their start and end apart: 7, of which 5 were waited for; matrix products, arithmetic and copies ran while one was open for 11% of the time, Pallas kernels for 0%

profile of v4, /device:TPU:8, one launch (start us, length us, event | category | flops | bytes accessed | tf_op | source)
XLA Modules:
  0.0 421.3 jit_solution(7297426445652278993)
XLA Ops:
  6.5 0.8 copy.37
  7.4 0.7 pad_maximum_fusion
  8.1 0.6 broadcast_in_dim.17
  8.7 4.3 %all-to-all-start = ((bf16[4,2,11]{2,1,0:T(2,128)(2,1)}), bf16[4,2,11]{2,1,0:T(2,128)(2,1)S(1)}, u32[]{:S(2)}, u32[]{:S(2)}) async-start(bf16[4,2,11]{2,1,0:T(2,128)(2,1)} %broadcast_in_dim.17), calls=%async_computation | async-start | bytes 4096 | tf_op jit(solution)/shard_map/all_to_all | solution.py:33
  13.0 0.8 convert_reduce_fusion.1
  13.8 4.0 convert_bitcast_fusion
  17.7 3.2 convert_bitcast_fusion.1
  20.9 0.1 add_subtract_fusion.1
  21.0 0.7 broadcast_in_dim.19
  21.7 12.1 %all-to-all-start.1 = ((bf16[64,8,11]{2,1,0:T(8,128)(2,1)}), bf16[64,8,11]{2,1,0:T(8,128)(2,1)S(1)}, u32[]{:S(2)}, u32[]{:S(2)}) async-start(bf16[64,8,11]{2,1,0:T(8,128)(2,1)} %broadcast_in_dim.19), calls=%async_computation.1 | async-start | bytes 262144 | tf_op jit(solution)/shard_map/all_to_all | solution.py:36
  33.8 0.1 stack.13
  33.9 0.1 stack.14
  34.0 0.1 stack.12
  34.1 0.1 sub.42
  34.2 0.1 iota.135
  34.3 8.9 %all-to-all-done.1 = bf16[64,8,11]{2,1,0:T(8,128)(2,1)S(1)} async-done(((bf16[64,8,11]{2,1,0:T(8,128)(2,1)}), bf16[64,8,11]{2,1,0:T(8,128)(2,1)S(1)}, u32[]{:S(2)}, u32[]{:S(2)}) %all-to-all-start.1) | async-done | bytes 11296 | tf_op jit(solution)/shard_map/all_to_all | solution.py:36
  43.2 0.2 fusion.65
  43.4 0.2 slice_reduce_fusion
  43.6 0.1 stack_broadcast_in_dim.7
  43.7 0.1 stack_broadcast_in_dim.8
  43.8 0.6 broadcast_in_dim.21
  44.4 4.8 %all-to-all-start.2 = ((f32[4,16,4]{1,2,0:T(4,128)}), f32[4,16,4]{1,2,0:T(4,128)S(1)}, u32[]{:S(2)}, u32[]{:S(2)}) async-start(f32[4,16,4]{1,2,0:T(4,128)} %broadcast_in_dim.21), calls=%async_computation.2 | async-start | bytes 16384 | tf_op jit(solution)/shard_map/all_to_all | solution.py:72
  49.2 5.7 %fusion.46 = bf16[4,256,256]{1,2,0:T(8,128)(2,1)S(1)} fusion(bf16[10,256,256]{2,0,1:T(8,128)(2,1)} %convert_bitcast_fusion, f32[4,10]{1,0:T(4,128)S(1)} %bitcast.129, bf16[10,256,256]{2,0,1:T(8,128)(2,1)} %convert_bitcast_fusion.1, bf16[4,256,256]{2,1,0:T(8,128)(2,1)S(1)} %copy-done, f32[4]{0:T(128)S(1)} %slice_reduce_fusion), kind=kOutput, calls=%fused_computation.46 | convolution fusion | flops 2690121728 | bytes 3670192 | tf_op jit(solution)/shard_map/byk,tkbx->tyx/dot_general | solution.py:53
  54.9 5.4 %fusion.23 = bf16[4096,256]{1,0:T(8,128)(2,1)} fusion(bf16[1024,256]{1,0:T(8,128)(2,1)S(1)} %bitcast.138, s32[1024]{0:T(1024)S(1)} %bitcast.127, s32[1024]{0:T(1024)S(1)} %bitcast.125, s32[4096]{0:T(1024)S(1)} %sub.42, s32[4096]{0:T(1024)S(1)} %iota.135), kind=kOutput, calls=%fused_computation.28 | convolution fusion | flops 2161115136 | bytes 2662400 | tf_op jit(solution)/shard_map/dot_general | solution.py:97
  60.3 4.8 %all-to-all-start.3 = ((bf16[64,64,256]{2,1,0:T(8,128)(2,1)}), bf16[64,64,256]{2,1,0:T(8,128)(2,1)S(1)}, u32[]{:S(2)}, u32[]{:S(2)}) async-start(bf16[64,64,256]{2,1,0:T(8,128)(2,1)} %bitcast.20), calls=%async_computation.3 | async-start | bytes 4194304 | tf_op jit(solution)/shard_map/all_to_all | solution.py:101
  65.1 0.3 reduce-scatter.3.cloned.1.call-start
  65.4 0.1 all_to_all.29
  65.5 25.7 %all-to-all-done.3 = bf16[64,64,256]{2,1,0:T(8,128)(2,1)S(1)} async-done(((bf16[64,64,256]{2,1,0:T(8,128)(2,1)}), bf16[64,64,256]{2,1,0:T(8,128)(2,1)S(1)}, u32[]{:S(2)}, u32[]{:S(2)}) %all-to-all-start.3) | async-done | bytes 2097184 | tf_op jit(solution)/shard_map/all_to_all | solution.py:101
  91.2 7.0 %fusion.32 = bf16[64,64,512]{2,1,0:T(8,128)(2,1)S(1)} fusion(bf16[64,64,256]{2,1,0:T(8,128)(2,1)S(1)} %all-to-all-done.3, s32[64]{0:T(128)S(1)} %get-tuple-element.14), kind=kOutput, calls=%fused_computation.36 | convolution fusion | flops 1092616192 | bytes 6291712 | tf_op jit(solution)/shard_map/kyx,kxX->kyX/dot_general | solution.py:102
  98.2 5.5 %fusion.27 = f32[64,64,512]{2,0,1:T(8,128)S(1)} fusion(s32[64]{0:T(128)S(1)} %get-tuple-element.15, bf16[8,8,64,512]{3,2,1,0:T(8,128)(2,1)S(1)} %bitcast.119), kind=kOutput, calls=%fused_computation.32 | convolution fusion | flops 268439552 | bytes 12583168 | tf_op jit(solution)/shard_map/dot_general | solution.py:105
  103.7 8.1 %copy.43 = f32[64,64,512]{2,1,0:T(8,128)} copy(f32[64,64,512]{2,0,1:T(8,128)S(1)} %fusion.27) | data formatting | bytes 16777216 | tf_op jit(solution)/shard_map/dot_general | solution.py:105
  111.8 0.1 sub.46
  111.9 5.0 %fusion.22 = bf16[4096,256]{1,0:T(8,128)(2,1)S(1)} fusion(bf16[1024,256]{1,0:T(8,128)(2,1)S(1)} %bitcast.139, s32[1024]{0:T(1024)S(1)} %bitcast.128, s32[1024]{0:T(1024)S(1)} %bitcast.126, s32[4096]{0:T(1024)S(1)} %sub.46, s32[4096]{0:T(1024)S(1)} %iota.135), kind=kOutput, calls=%fused_computation.27 | convolution fusion | flops 2161115136 | bytes 2662400 | tf_op jit(solution)/shard_map/dot_general | solution.py:97
  116.9 38.5 %all_to_all.41 = bf16[64,64,256]{2,1,0:T(8,128)(2,1)S(1)} all-to-all(bf16[64,64,256]{2,1,0:T(8,128)(2,1)S(1)} %bitcast.121), channel_id=1, replica_groups=mesh['exp'=64,'grp'=4] {'grp'}, dimensions={0} | all-to-all | bytes 4194304 | tf_op jit(solution)/shard_map/all_to_all | solution.py:101
  155.4 7.0 %fusion.33 = bf16[64,64,512]{2,1,0:T(8,128)(2,1)S(1)} fusion(bf16[64,64,256]{2,1,0:T(8,128)(2,1)S(1)} %all_to_all.41, s32[64]{0:T(128)S(1)} %get-tuple-element.14), kind=kOutput, calls=%fused_computation.37 | convolution fusion | flops 1092616192 | bytes 6291712 | tf_op jit(solution)/shard_map/kyx,kxX->kyX/dot_general | solution.py:102
  162.4 5.5 %fusion.24 = f32[64,64,512]{2,0,1:T(8,128)S(1)} fusion(s32[64]{0:T(128)S(1)} %get-tuple-element.15, bf16[8,8,64,512]{3,2,1,0:T(8,128)(2,1)S(1)} %bitcast.120), kind=kOutput, calls=%fused_computation.29 | convolution fusion | flops 268439552 | bytes 12583168 | tf_op jit(solution)/shard_map/dot_general | solution.py:105
  167.9 8.1 %copy.45 = f32[64,64,512]{2,1,0:T(8,128)} copy(f32[64,64,512]{2,0,1:T(8,128)S(1)} %fusion.24) | data formatting | bytes 16777216 | tf_op jit(solution)/shard_map/dot_general | solution.py:105
  176.0 0.1 copy.46
  176.2 0.1 reduce_window_sum.11
  176.3 0.2 select_reduce_fusion
  176.5 0.8 scatter_custom_fusion
  177.3 1.1 copy.47
  178.4 5.7 %all-to-all-start.5 = ((f32[64,8,3]{1,2,0:T(4,128)}), f32[64,8,3]{1,2,0:T(4,128)S(1)}, u32[]{:S(2)}, u32[]{:S(2)}) async-start(f32[64,8,3]{1,2,0:T(4,128)} %copy.47), calls=%async_computation.7 | async-start | bytes 262144 | tf_op jit(solution)/shard_map/all_to_all | solution.py:123
  184.2 10.0 %all-to-all-done.5 = f32[64,8,3]{1,2,0:T(4,128)S(1)} async-done(((f32[64,8,3]{1,2,0:T(4,128)}), f32[64,8,3]{1,2,0:T(4,128)S(1)}, u32[]{:S(2)}, u32[]{:S(2)}) %all-to-all-start.5) | async-done | bytes 6176 | tf_op jit(solution)/shard_map/all_to_all | solution.py:123
  194.2 0.1 all_to_all.34
  194.3 62.9 %reduce-scatter.3.cloned.1.call-done = f32[1,64,512]{2,1,0:T(8,128)} async-done(((f32[64,64,512]{2,1,0:T(8,128)}), f32[1,64,512]{2,1,0:T(8,128)}) %reduce-scatter.3.cloned.1.call-update) | async-done | bytes 131088 | tf_op jit(solution)/shard_map/reduce_scatter | solution.py:108
  257.3 154.4 %reduce-scatter.5.cloned.1.call-done = f32[1,64,512]{2,1,0:T(8,128)} async-done(((f32[64,64,512]{2,1,0:T(8,128)}), f32[1,64,512]{2,1,0:T(8,128)}) %reduce-scatter.5.cloned.1.call-update) | async-done | bytes 131088 | tf_op jit(solution)/shard_map/reduce_scatter | solution.py:108
  411.7 2.5 fusion.54
  (32 shorter events, 0.3 us)
Async XLA Ops:
  6.5 42.7 %copy-start = (bf16[4,256,256]{2,1,0:T(8,128)(2,1)S(1)}, bf16[4,256,256]{2,1,0:T(8,128)(2,1)}, u32[]{:S(2)}) copy-start(bf16[4,256,256]{2,1,0:T(8,128)(2,1)} %param.8) | copy-start | bytes 1572868
  8.7 12.4 %all-to-all-start = ((bf16[4,2,11]{2,1,0:T(2,128)(2,1)}), bf16[4,2,11]{2,1,0:T(2,128)(2,1)S(1)}, u32[]{:S(2)}, u32[]{:S(2)}) async-start(bf16[4,2,11]{2,1,0:T(2,128)(2,1)} %broadcast_in_dim.17), calls=%async_computation | async-start | bytes 4096 | tf_op jit(solution)/shard_map/all_to_all | solution.py:33
  13.7 4.0 copy-start.2
  17.7 3.2 slice-start
  17.7 16.3 %copy-start.1 = (s32[4,4]{1,0:T(4,128)S(1)}, s32[4,4]{1,0:T(4,128)}, u32[]{:S(2)}) copy-start(s32[4,4]{1,0:T(4,128)} %param.10) | copy-start | bytes 196
  17.7 25.5 %copy-start.3 = (s32[4]{0:T(128)S(1)}, s32[4]{0:T(128)}, u32[]{:S(2)}) copy-start(s32[4]{0:T(128)} %param.9) | copy-start | bytes 52
  21.7 21.5 %all-to-all-start.1 = ((bf16[64,8,11]{2,1,0:T(8,128)(2,1)}), bf16[64,8,11]{2,1,0:T(8,128)(2,1)S(1)}, u32[]{:S(2)}, u32[]{:S(2)}) async-start(bf16[64,8,11]{2,1,0:T(8,128)(2,1)} %broadcast_in_dim.19), calls=%async_computation.1 | async-start | bytes 262144 | tf_op jit(solution)/shard_map/all_to_all | solution.py:36
  44.4 16.0 %all-to-all-start.2 = ((f32[4,16,4]{1,2,0:T(4,128)}), f32[4,16,4]{1,2,0:T(4,128)S(1)}, u32[]{:S(2)}, u32[]{:S(2)}) async-start(f32[4,16,4]{1,2,0:T(4,128)} %broadcast_in_dim.21), calls=%async_computation.2 | async-start | bytes 16384 | tf_op jit(solution)/shard_map/all_to_all | solution.py:72
  60.3 30.8 %all-to-all-start.3 = ((bf16[64,64,256]{2,1,0:T(8,128)(2,1)}), bf16[64,64,256]{2,1,0:T(8,128)(2,1)S(1)}, u32[]{:S(2)}, u32[]{:S(2)}) async-start(bf16[64,64,256]{2,1,0:T(8,128)(2,1)} %bitcast.20), calls=%async_computation.3 | async-start | bytes 4194304 | tf_op jit(solution)/shard_map/all_to_all | solution.py:101
  65.1 192.1 %reduce-scatter.3.cloned.1.call-start = ((), (), s32[]{:S(2)}) async-start(), calls=%async_computation.8 | async-start | bytes 8519680 | tf_op jit(solution)/shard_map/reduce_scatter | solution.py:108
  111.8 299.9 %reduce-scatter.5.cloned.1.call-start = ((), (), s32[]{:S(2)}) async-start(), calls=%async_computation.9 | async-start | bytes 8519680 | tf_op jit(solution)/shard_map/reduce_scatter | solution.py:108
  178.4 15.8 %all-to-all-start.5 = ((f32[64,8,3]{1,2,0:T(4,128)}), f32[64,8,3]{1,2,0:T(4,128)S(1)}, u32[]{:S(2)}, u32[]{:S(2)}) async-start(f32[64,8,3]{1,2,0:T(4,128)} %copy.47), calls=%async_computation.7 | async-start | bytes 262144 | tf_op jit(solution)/shard_map/all_to_all | solution.py:123
Sparse Core Ops, SparseCore 0:
  111.9 145.3 reduce-scatter.2
  262.1 149.5 reduce-scatter.4

commit v5 on v2

--- a/solution.py
+++ b/solution.py
@@ -1,9 +1,12 @@
 import jax
 import jax.numpy as jnp
 from jax import lax
+from jax.sharding import Mesh
 from jax.sharding import PartitionSpec as P
 
 PS = 512
+EXP = ("ey", "ez", "ec")
+CHIP = ("ey", "ez")
 
 
 def band_matrix(filters, tile_side):
@@ -20,20 +23,22 @@
 def per_device(
     tiles, tile_exposure, tile_patch, tile_offset, coeffs, inv_var, vert_taps, horiz_taps
 ):
-    n_owners = lax.axis_size("exp")
+    n_owners = lax.axis_size(EXP)
     n_bands = lax.axis_size("grp")
     tile_count, tile_side, _ = tiles.shape
     listed = tile_patch.shape[1]
     terms = coeffs.shape[1]
     band_rows = PS // n_bands
     g = lax.axis_index("grp")
+    h = lax.axis_index("ec")
+    n_halves = lax.axis_size("ec")
 
     packed = jnp.concatenate([coeffs, inv_var[:, None]], axis=1)
     packed = jnp.broadcast_to(packed[None], (n_bands,) + packed.shape)
     packed = lax.all_to_all(packed, "grp", split_axis=0, concat_axis=0, tiled=True)
     packed = packed.reshape(1, -1, terms + 1)
     packed = jnp.broadcast_to(packed, (n_owners,) + packed.shape[1:])
-    packed = lax.all_to_all(packed, "exp", split_axis=0, concat_axis=0, tiled=True)
+    packed = lax.all_to_all(packed, EXP, split_axis=0, concat_axis=0, tiled=True)
     packed = packed.reshape(-1, terms + 1)
 
     vband = band_matrix(vert_taps, tile_side)
@@ -90,7 +95,9 @@
     owner_of = (
         got_patch[None, :] == jnp.arange(n_owners, dtype=jnp.int32)[:, None]
     ).astype(jnp.bfloat16)
-    bands = jnp.einsum("pk,kyX->pyX", owner_of, shifted, preferred_element_type=jnp.float32)
+    bands = jnp.dot(
+        owner_of, shifted.reshape(entries, band_rows * PS), preferred_element_type=jnp.float32
+    ).reshape(n_owners // n_halves, n_halves, band_rows, PS)
 
     per_owner = n_bands * 2
     onehot = (got_patch[:, None] == jnp.arange(n_owners, dtype=jnp.int32)[None, :]).astype(
@@ -105,8 +112,12 @@
         .set(got_meta[:, 1:], mode="drop")
     )
 
-    flux = lax.psum_scatter(bands, "exp", scatter_dimension=0, tiled=True)[0]
-    recv_meta = lax.all_to_all(meta_slots, "exp", split_axis=0, concat_axis=0, tiled=True)
+    keep = lax.dynamic_index_in_dim(bands, h, axis=1, keepdims=False)
+    give = lax.dynamic_index_in_dim(bands, 1 - h, axis=1, keepdims=False)
+    pair = keep + lax.ppermute(give, "ec", perm=[(0, 1), (1, 0)])
+    recv_bands = lax.all_to_all(pair.astype(jnp.bfloat16), CHIP, split_axis=0, concat_axis=0, tiled=True)
+    flux = jnp.sum(recv_bands.astype(jnp.float32), axis=0)
+    recv_meta = lax.all_to_all(meta_slots, EXP, split_axis=0, concat_axis=0, tiled=True)
 
     rows = recv_meta[:, 0].astype(jnp.int32)
     cols = recv_meta[:, 1].astype(jnp.int32)
@@ -125,17 +136,22 @@
 
 
 def solution(mesh):
+    n_exp, n_grp = mesh.devices.shape
+    n_core = 2
+    n_y = 4
+    split = Mesh(mesh.devices.reshape(n_y, n_exp // (n_y * n_core), n_core, n_grp), EXP + ("grp",))
+    every = EXP + ("grp",)
     in_specs = (
-        P(("exp", "grp"), None, None),
-        P(("exp", "grp")),
-        P(("exp", "grp"), None),
-        P(("exp", "grp"), None, None),
-        P(("exp", "grp"), None),
-        P(("exp", "grp")),
+        P(every, None, None),
+        P(every),
+        P(every, None),
+        P(every, None, None),
+        P(every, None),
+        P(every),
         P(),
         P(),
     )
-    out_specs = P("exp", "grp", None)
+    out_specs = P(EXP, "grp", None)
     return jax.shard_map(
-        per_device, mesh=mesh, in_specs=in_specs, out_specs=out_specs, check_vma=False
+        per_device, mesh=split, in_specs=in_specs, out_specs=out_specs, check_vma=False
     )

time: 360 us -> 287 us (0.80)
  waiting for transfers between devices: 233 us -> 157 us
  other arithmetic: 1.16 us -> 16.6 us
  between operations: 13.6 us -> 0.19 us
  starting transfers between devices: 32.1 us -> 38 us
  matrix products: 46.2 us -> 41.5 us
    reduce_scatter x1 -> x0, waiting for transfers between devices: 166 us -> none  [per_device(): flux = lax.psum_scatter(bands, 'exp', scatter_dimension=0, tiled=True)[0]]
    all_to_all x2 -> x3, waiting for transfers between devices: 18.5 us -> 103 us  [the longest x1 93.8 us: per_device(): lax.all_to_all(pair.astype(jnp.bfloat16), CHIP, split_axis=0, concat_axis...]
    dot_general x1 -> x0, local copies, waits for them, and re-layouts: 19.5 us -> none  [per_device(): jnp.einsum('pk,kyX->pyX', owner_of, shifted, preferred_element_type=jnp.f...]
    dynamic_slice x0 -> x2, local copies, waits for them, and re-layouts: none -> 18.3 us  [the longest x1 11.5 us: per_device(): give = lax.dynamic_index_in_dim(bands, 1 - h, axis=1, keepdims=False)]
    convert_element_type x1 -> x2, other arithmetic: 0.01 us -> 12.6 us  [the longest x1 12.6 us: per_device(): pair.astype(jnp.bfloat16)]
    all_to_all x2 -> x3, starting transfers between devices: 17.8 us -> 23.8 us  [the longest x1 12.1 us: per_device(): lax.all_to_all(packed, EXP, split_axis=0, concat_axis=0, tiled=True)]
    ppermute x0 -> x1, waiting for transfers between devices: none -> 5.26 us  [per_device(): pair = keep + lax.ppermute(give, 'ec', perm=[(0, 1), (1, 0)])]
    dot_general x1, matrix products: 14.2 us -> 10.5 us  [per_device(): jnp.dot(owner_of, shifted.reshape(entries, band_rows * PS), preferred_ele...]
  transfers between devices with their start and end apart: 6 -> 7, of which waited for: 4 -> 4; matrix products, arithmetic and copies ran while one was open for 8% -> 14% of each run, Pallas kernels for 0% -> 0%
where the time goes in v5:
time: 287 us; the launch traced here: 285 us
  waiting for transfers between devices  157 us (55%)
  matrix products  41.5 us (14%)
  starting transfers between devices  38 us (13%)
  local copies, waits for them, and re-layouts  31.1 us (11%)
  other arithmetic  16.6 us (6%)
    all_to_all x1, waiting for transfers between devices, per_device(): lax.all_to_all(pair.astype(jnp.bfloat16), CHIP, split_axis=0, concat_axis...  93.8 us
    all_to_all x1, waiting for transfers between devices, per_device(): lax.all_to_all(slabs, 'grp', split_axis=0, concat_axis=0, tiled=True)  49 us
    convert_element_type x1, other arithmetic, per_device(): pair.astype(jnp.bfloat16)  12.6 us
    dot_general x1, matrix products, per_device(): jnp.einsum('kyx,kxX->kyX', got_slabs, shifter, preferred_element_type=jnp...  12.3 us
    all_to_all x1, starting transfers between devices, per_device(): lax.all_to_all(packed, EXP, split_axis=0, concat_axis=0, tiled=True)  12.1 us
    dynamic_slice x1, local copies, waits for them, and re-layouts, per_device(): give = lax.dynamic_index_in_dim(bands, 1 - h, axis=1, keepdims=False)  11.5 us
    dot_general x1, matrix products, per_device(): jnp.dot(owner_of, shifted.reshape(entries, band_rows * PS), preferred_ele...  10.5 us
    all_to_all x1, waiting for transfers between devices, per_device(): lax.all_to_all(packed, EXP, split_axis=0, concat_axis=0, tiled=True)  9.13 us
  transfers between devices with their start and end apart: 7, of which 4 were waited for; matrix products, arithmetic and copies ran while one was open for 14% of the time, Pallas kernels for 0%

profile of v5, /device:TPU:8, one launch (start us, length us, event | category | flops | bytes accessed | tf_op | source)
XLA Modules:
  0.0 284.6 jit_solution(3004443443569623823)
XLA Ops:
  0.0 0.8 copy.36
  0.8 0.7 pad_maximum_fusion
  1.6 0.6 broadcast_in_dim.17
  2.1 4.3 %all-to-all-start = ((bf16[4,2,11]{2,1,0:T(2,128)(2,1)}), bf16[4,2,11]{2,1,0:T(2,128)(2,1)S(1)}, u32[]{:S(2)}, u32[]{:S(2)}) async-start(bf16[4,2,11]{2,1,0:T(2,128)(2,1)} %broadcast_in_dim.17), calls=%async_computation | async-start | bytes 4096 | tf_op jit(solution)/shard_map/all_to_all | solution.py:38
  6.4 2.6 convert_bitcast_fusion.1
  9.1 3.3 %convert_bitcast_fusion.2 = bf16[10,256,256,1]{2,0,1,3:T(8,128)(2,1)} fusion(bf16[10,41]{1,0:T(8,128)(2,1)S(1)} %copy-done.4), kind=kOutput, calls=%fused_computation.28 | convolution fusion | flops 62455808 | bytes 1311540 | tf_op jit(solution)/shard_map/bd,dij->bij/dot_general | solution.py:19
  12.4 0.0 all-to-all-done
  12.4 0.7 broadcast_in_dim.19
  13.1 12.1 %all-to-all-start.1 = ((bf16[64,8,11]{2,1,0:T(8,128)(2,1)}), bf16[64,8,11]{2,1,0:T(8,128)(2,1)S(1)}, u32[]{:S(2)}, u32[]{:S(2)}) async-start(bf16[64,8,11]{2,1,0:T(8,128)(2,1)} %broadcast_in_dim.19), calls=%async_computation.1 | async-start | bytes 262144 | tf_op jit(solution)/shard_map/all_to_all | solution.py:41
  25.2 0.1 stack.13
  25.3 0.1 stack.14
  25.4 0.1 stack.12
  25.4 9.1 %all-to-all-done.1 = bf16[64,8,11]{2,1,0:T(8,128)(2,1)S(1)} async-done(((bf16[64,8,11]{2,1,0:T(8,128)(2,1)}), bf16[64,8,11]{2,1,0:T(8,128)(2,1)S(1)}, u32[]{:S(2)}, u32[]{:S(2)}) %all-to-all-start.1) | async-done | bytes 11296 | tf_op jit(solution)/shard_map/all_to_all | solution.py:41
  34.6 0.2 fusion.54
  34.8 0.2 slice_reduce_fusion
  35.0 0.1 stack_broadcast_in_dim.7
  35.0 0.1 stack_broadcast_in_dim.8
  35.1 0.6 broadcast_in_dim.21
  35.7 4.8 %all-to-all-start.2 = ((f32[4,16,4]{1,2,0:T(4,128)}), f32[4,16,4]{1,2,0:T(4,128)S(1)}, u32[]{:S(2)}, u32[]{:S(2)}) async-start(f32[4,16,4]{1,2,0:T(4,128)} %broadcast_in_dim.21), calls=%async_computation.2 | async-start | bytes 16384 | tf_op jit(solution)/shard_map/all_to_all | solution.py:84
  40.5 0.1 copy.39
  40.6 0.0 copy-done
  40.6 6.7 %fusion.35 = bf16[4,256,256,1,1]{2,1,4,3,0:T(8,128)(2,1)S(1)} fusion(bf16[10,256,256,1]{2,0,1,3:T(8,128)(2,1)S(1)} %convert_bitcast_fusion.1, f32[4,10]{0,1:T(8,128)S(1)} %copy.39, bf16[10,256,256,1]{2,0,1,3:T(8,128)(2,1)} %convert_bitcast_fusion.2, bf16[4,256,256]{2,1,0:T(8,128)(2,1)S(1)} %copy-done, f32[4]{0:T(128)S(1)} %slice_reduce_fusion), kind=kOutput, calls=%fused_computation.34 | convolution fusion | flops 2690121728 | bytes 3670192 | tf_op jit(solution)/shard_map/byk,tkbx->tyx/dot_general | solution.py:58
  47.4 4.3 %convert_bitcast_fusion = bf16[4,4,4,128,256]{3,4,2,0,1:T(8,128)(2,1)} fusion(bf16[4,256,256,1,1]{2,1,4,3,0:T(8,128)(2,1)S(1)} %fusion.35, s32[4,4]{1,0:T(4,128)S(1)} %bitcast.108, s32[4]{0:T(128)S(1)} %iota_multiply_fusion), kind=kOutput, calls=%fused_computation.23 | convolution fusion | flops 1082130432 | bytes 4718672 | tf_op jit(solution)/shard_map/gtjiy,tyx->gtjix/dot_general | solution.py:71
  51.7 7.3 %copy.41 = bf16[4,4,4,128,256]{4,3,2,1,0:T(8,128)(2,1)} copy(bf16[4,4,4,128,256]{3,4,2,0,1:T(8,128)(2,1)} %convert_bitcast_fusion) | data formatting | bytes 8388608 | tf_op jit(solution)/shard_map/convert_element_type | solution.py:72
  59.0 0.0 all-to-all-done.2
  59.0 5.1 %all-to-all-start.3 = ((bf16[64,128,256]{2,1,0:T(8,128)(2,1)}), bf16[64,128,256]{2,1,0:T(8,128)(2,1)}, u32[]{:S(2)}, u32[]{:S(2)}) async-start(bf16[64,128,256]{2,1,0:T(8,128)(2,1)} %bitcast.105), calls=%async_computation.3 | async-start | bytes 8388608 | tf_op jit(solution)/shard_map/all_to_all | solution.py:83
  64.1 0.1 all_to_all.29
  64.2 49.0 %all-to-all-done.3 = bf16[64,128,256]{2,1,0:T(8,128)(2,1)} async-done(((bf16[64,128,256]{2,1,0:T(8,128)(2,1)}), bf16[64,128,256]{2,1,0:T(8,128)(2,1)}, u32[]{:S(2)}, u32[]{:S(2)}) %all-to-all-start.3) | async-done | bytes 4194336 | tf_op jit(solution)/shard_map/all_to_all | solution.py:83
  113.2 12.3 %fusion.9 = bf16[64,128,512]{2,1,0:T(8,128)(2,1)} fusion(bf16[64,128,256]{2,1,0:T(8,128)(2,1)} %all-to-all-done.3, s32[64]{0:T(128)S(1)} %get-tuple-element.15), kind=kOutput, calls=%fused_computation.18 | convolution fusion | flops 2168455168 | bytes 12583168 | tf_op jit(solution)/shard_map/kyx,kxX->kyX/dot_general | solution.py:93
  125.6 10.5 %fusion.5 = f32[32,2,128,512]{3,0,2,1:T(8,128)S(1)} fusion(s32[32,2]{0,1:T(2,128)S(1)} %multiply_add_fusion, s32[64]{0:T(128)S(1)} %get-tuple-element.14, bf16[8,8,128,512]{3,2,1,0:T(8,128)(2,1)} %bitcast.106), kind=kOutput, calls=%fused_computation.10 | convolution fusion | flops 536875008 | bytes 25166336 | tf_op jit(solution)/shard_map/dot_general | solution.py:98
  136.0 6.8 %constant_dynamic-slice_fusion.1 = (f32[32,1,128,512]{3,0,2,1:T(8,128)}, f32[32,1,128,512]{3,0,2,1:T(8,128)}) fusion(f32[32,2,128,512]{3,0,2,1:T(8,128)S(1)} %fusion.5, s32[]{:T(128)S(6)} %select_n.11, s32[]{:T(128)S(6)} %select_n.12), kind=kLoop, calls=%fused_computation.83 | loop fusion | bytes 33554440 | tf_op jit(solution)/shard_map/jit(dynamic_index_in_dim)/dynamic_slice | solution.py:115
  142.8 11.5 %copy.80 = f32[32,1,128,512]{3,2,0,1:T(8,128)} copy(f32[32,1,128,512]{3,0,2,1:T(8,128)} %get-tuple-element.8) | data formatting | bytes 16777216 | tf_op jit(solution)/shard_map/jit(dynamic_index_in_dim)/dynamic_slice | solution.py:116
  154.3 0.0 collective-permute-start
  154.3 0.1 fusion.63
  154.4 0.1 reduce_window_sum.11
  154.5 0.1 copy.45
  154.6 0.2 select_reduce_fusion
  154.8 0.8 scatter_custom_fusion
  155.6 1.1 copy.46
  156.7 5.9 %all-to-all-start.5 = ((f32[64,8,3]{1,2,0:T(4,128)}), f32[64,8,3]{1,2,0:T(4,128)S(1)}, u32[]{:S(2)}, u32[]{:S(2)}) async-start(f32[64,8,3]{1,2,0:T(4,128)} %copy.46), calls=%async_computation.5 | async-start | bytes 262144 | tf_op jit(solution)/shard_map/all_to_all | solution.py:120
  162.5 5.3 %collective-permute-done = f32[32,128,512]{2,1,0:T(8,128)} collective-permute-done((f32[32,128,512]{2,1,0:T(8,128)}, f32[32,128,512]{2,1,0:T(8,128)}, u32[]{:S(2)}, u32[]{:S(2)}) %collective-permute-start) | collective-permute-done | bytes 8388640 | tf_op jit(solution)/shard_map/ppermute | solution.py:117
  167.8 12.6 %fusion.7 = bf16[32,128,512]{2,1,0:T(8,128)(2,1)} fusion(f32[32,128,512]{2,1,0:T(8,128)} %collective-permute-done, f32[32,1,128,512]{3,0,2,1:T(8,128)} %get-tuple-element.7), kind=kLoop, calls=%fused_computation.13 | loop fusion | flops 4194304 | bytes 20971520 | tf_op jit(solution)/shard_map/convert_element_type | solution.py:118
  180.4 0.0 all-to-all-done.5
  180.4 5.8 %all-to-all-start.4 = ((bf16[32,128,512]{2,1,0:T(8,128)(2,1)}), bf16[32,128,512]{2,1,0:T(8,128)(2,1)}, u32[]{:S(2)}, u32[]{:S(2)}) async-start(bf16[32,128,512]{2,1,0:T(8,128)(2,1)} %fusion.7), calls=%async_computation.4 | async-start | bytes 8388608 | tf_op jit(solution)/shard_map/all_to_all | solution.py:118
  186.3 0.1 all_to_all.34
  186.4 93.8 %all-to-all-done.4 = bf16[32,128,512]{2,1,0:T(8,128)(2,1)} async-done(((bf16[32,128,512]{2,1,0:T(8,128)(2,1)}), bf16[32,128,512]{2,1,0:T(8,128)(2,1)}, u32[]{:S(2)}, u32[]{:S(2)}) %all-to-all-start.4) | async-done | bytes 4194336 | tf_op jit(solution)/shard_map/all_to_all | solution.py:118
  280.3 2.8 convert_reduce_fusion
  283.1 1.6 fusion.43
  (26 shorter events, 0.1 us)
Async XLA Ops:
  0.0 40.6 %copy-start = (bf16[4,256,256]{2,1,0:T(8,128)(2,1)S(1)}, bf16[4,256,256]{2,1,0:T(8,128)(2,1)}, u32[]{:S(2)}) copy-start(bf16[4,256,256]{2,1,0:T(8,128)(2,1)} %param.8) | copy-start | bytes 1572868
  0.0 9.1 %copy-start.4 = (bf16[10,41]{1,0:T(8,128)(2,1)S(1)}, bf16[10,41]{1,0:T(8,128)(2,1)}, u32[]{:S(2)}) copy-start(bf16[10,41]{1,0:T(8,128)(2,1)} %param.15) | copy-start | bytes 2464
  2.1 10.2 %all-to-all-start = ((bf16[4,2,11]{2,1,0:T(2,128)(2,1)}), bf16[4,2,11]{2,1,0:T(2,128)(2,1)S(1)}, u32[]{:S(2)}, u32[]{:S(2)}) async-start(bf16[4,2,11]{2,1,0:T(2,128)(2,1)} %broadcast_in_dim.17), calls=%async_computation | async-start | bytes 4096 | tf_op jit(solution)/shard_map/all_to_all | solution.py:38
  6.4 5.9 %copy-start.2 = (s32[4,4,2]{1,2,0:T(2,128)S(1)}, s32[4,4,2]{1,2,0:T(2,128)}, u32[]{:S(2)}) copy-start(s32[4,4,2]{1,2,0:T(2,128)} %param.11) | copy-start | bytes 388
  6.4 18.9 %copy-start.3 = (s32[4,4]{1,0:T(4,128)S(1)}, s32[4,4]{1,0:T(4,128)}, u32[]{:S(2)}) copy-start(s32[4,4]{1,0:T(4,128)} %param.10) | copy-start | bytes 196
  6.4 28.1 %copy-start.5 = (s32[4]{0:T(128)S(1)}, s32[4]{0:T(128)}, u32[]{:S(2)}) copy-start(s32[4]{0:T(128)} %param.9) | copy-start | bytes 52
  12.4 35.0 %slice-start = ((s32[4,4,2]{1,2,0:T(2,128)}), s32[4,4,1]{1,2,0:T(1,128)S(1)}, s32[]{:S(2)}) async-start(s32[4,4,2]{1,2,0:T(2,128)} %param.11), calls=%async_computation.6 | async-start | bytes 4096 | tf_op jit(solution)/shard_map/slice | solution.py:63
  13.1 21.5 %all-to-all-start.1 = ((bf16[64,8,11]{2,1,0:T(8,128)(2,1)}), bf16[64,8,11]{2,1,0:T(8,128)(2,1)S(1)}, u32[]{:S(2)}, u32[]{:S(2)}) async-start(bf16[64,8,11]{2,1,0:T(8,128)(2,1)} %broadcast_in_dim.19), calls=%async_computation.1 | async-start | bytes 262144 | tf_op jit(solution)/shard_map/all_to_all | solution.py:41
  35.7 23.2 %all-to-all-start.2 = ((f32[4,16,4]{1,2,0:T(4,128)}), f32[4,16,4]{1,2,0:T(4,128)S(1)}, u32[]{:S(2)}, u32[]{:S(2)}) async-start(f32[4,16,4]{1,2,0:T(4,128)} %broadcast_in_dim.21), calls=%async_computation.2 | async-start | bytes 16384 | tf_op jit(solution)/shard_map/all_to_all | solution.py:84
  59.0 54.2 %all-to-all-start.3 = ((bf16[64,128,256]{2,1,0:T(8,128)(2,1)}), bf16[64,128,256]{2,1,0:T(8,128)(2,1)}, u32[]{:S(2)}, u32[]{:S(2)}) async-start(bf16[64,128,256]{2,1,0:T(8,128)(2,1)} %bitcast.105), calls=%async_computation.3 | async-start | bytes 8388608 | tf_op jit(solution)/shard_map/all_to_all | solution.py:83
  154.3 13.5 %collective-permute-start = (f32[32,128,512]{2,1,0:T(8,128)}, f32[32,128,512]{2,1,0:T(8,128)}, u32[]{:S(2)}, u32[]{:S(2)}) collective-permute-start(f32[32,128,512]{2,1,0:T(8,128)} %bitcast.103), channel_id=1, source_target_pairs={{0,4},{4,0},{1,5},{5,1},{2,6},{6,2},{3,7},{7,3},{8,12},{12,8},{9,1... | collective-permute-start | bytes 25165832 | tf_op jit(solution)/shard_map/ppermute | solution.py:117
  156.7 23.7 %all-to-all-start.5 = ((f32[64,8,3]{1,2,0:T(4,128)}), f32[64,8,3]{1,2,0:T(4,128)S(1)}, u32[]{:S(2)}, u32[]{:S(2)}) async-start(f32[64,8,3]{1,2,0:T(4,128)} %copy.46), calls=%async_computation.5 | async-start | bytes 262144 | tf_op jit(solution)/shard_map/all_to_all | solution.py:120
  167.8 116.8 %copy-start.1 = (bf16[4,256,256]{2,1,0:T(8,128)(2,1)S(1)}, bf16[4,256,256]{2,1,0:T(8,128)(2,1)}, u32[]{:S(2)}) copy-start(bf16[4,256,256]{2,1,0:T(8,128)(2,1)} %param.8) | copy-start | bytes 1572868
  180.4 99.8 %all-to-all-start.4 = ((bf16[32,128,512]{2,1,0:T(8,128)(2,1)}), bf16[32,128,512]{2,1,0:T(8,128)(2,1)}, u32[]{:S(2)}, u32[]{:S(2)}) async-start(bf16[32,128,512]{2,1,0:T(8,128)(2,1)} %fusion.7), calls=%async_computation.4 | async-start | bytes 8388608 | tf_op jit(solution)/shard_map/all_to_all | solution.py:118

commit v6 on v5

--- a/solution.py
+++ b/solution.py
@@ -36,7 +36,7 @@
     packed = jnp.concatenate([coeffs, inv_var[:, None]], axis=1)
     packed = jnp.broadcast_to(packed[None], (n_bands,) + packed.shape)
     packed = lax.all_to_all(packed, "grp", split_axis=0, concat_axis=0, tiled=True)
-    packed = packed.reshape(1, -1, terms + 1)
+    packed = packed.reshape(1, 1, -1)
     packed = jnp.broadcast_to(packed, (n_owners,) + packed.shape[1:])
     packed = lax.all_to_all(packed, EXP, split_axis=0, concat_axis=0, tiled=True)
     packed = packed.reshape(-1, terms + 1)
@@ -92,12 +92,14 @@
     shifter = (x_out == got_col[:, None, None] + x_in).astype(jnp.bfloat16)
     shifted = jnp.einsum("kyx,kxX->kyX", got_slabs, shifter, preferred_element_type=jnp.float32)
     shifted = shifted.astype(jnp.bfloat16)
+    chips = n_owners // n_halves
+    owner_row = jnp.where(got_patch % n_halves == h, chips, 0) + got_patch // n_halves
     owner_of = (
-        got_patch[None, :] == jnp.arange(n_owners, dtype=jnp.int32)[:, None]
+        owner_row[None, :] == jnp.arange(n_owners, dtype=jnp.int32)[:, None]
     ).astype(jnp.bfloat16)
     bands = jnp.dot(
         owner_of, shifted.reshape(entries, band_rows * PS), preferred_element_type=jnp.float32
-    ).reshape(n_owners // n_halves, n_halves, band_rows, PS)
+    ).reshape(n_halves, chips, band_rows, PS)
 
     per_owner = n_bands * 2
     onehot = (got_patch[:, None] == jnp.arange(n_owners, dtype=jnp.int32)[None, :]).astype(
@@ -112,9 +114,7 @@
         .set(got_meta[:, 1:], mode="drop")
     )
 
-    keep = lax.dynamic_index_in_dim(bands, h, axis=1, keepdims=False)
-    give = lax.dynamic_index_in_dim(bands, 1 - h, axis=1, keepdims=False)
-    pair = keep + lax.ppermute(give, "ec", perm=[(0, 1), (1, 0)])
+    pair = bands[1] + lax.ppermute(bands[0], "ec", perm=[(0, 1), (1, 0)])
     recv_bands = lax.all_to_all(pair.astype(jnp.bfloat16), CHIP, split_axis=0, concat_axis=0, tiled=True)
     flux = jnp.sum(recv_bands.astype(jnp.float32), axis=0)
     recv_meta = lax.all_to_all(meta_slots, EXP, split_axis=0, concat_axis=0, tiled=True)

time: 287 us -> 305 us (1.063); the launches traced: 285 us -> 299 us
  local copies, waits for them, and re-layouts: 31.1 us -> 54.3 us
  waiting for transfers between devices: 157 us -> 151 us
  matrix products: 41.5 us -> 36.7 us
  starting transfers between devices: 38 us -> 42.7 us
  other arithmetic: 16.6 us -> 13.4 us
    unnamed x12 -> x15, local copies, waits for them, and re-layouts: 0.02 us -> 34.7 us
    dynamic_slice x2 -> x0, local copies, waits for them, and re-layouts: 18.3 us -> none  [the longest x1 11.5 us: per_device(): give = lax.dynamic_index_in_dim(bands, 1 - h, axis=1, keepdims=False)]
    slice x0 -> x1, local copies, waits for them, and re-layouts: none -> 6.62 us  [per_device(): pair = bands[1] + lax.ppermute(bands[0], 'ec', perm=[(0, 1), (1, 0)])]
    ppermute x1, waiting for transfers between devices: 5.26 us -> 0.01 us  [per_device(): pair = bands[1] + lax.ppermute(bands[0], 'ec', perm=[(0, 1), (1, 0)])]
    dot_general x1, matrix products: 10.5 us -> 5.69 us  [per_device(): jnp.dot(owner_of, shifted.reshape(entries, band_rows * PS), preferred_ele...]
    all_to_all x1, starting transfers between devices: 5.84 us -> 9.99 us  [per_device(): lax.all_to_all(pair.astype(jnp.bfloat16), CHIP, split_axis=0, concat_axis...]
    convert_element_type x1, other arithmetic: 12.6 us -> 9.34 us  [per_device(): pair.astype(jnp.bfloat16)]
  transfers between devices with their start and end apart: 7 -> 7, of which waited for: 4 -> 3; matrix products, arithmetic and copies ran while one was open for 14% -> 16% of each run, Pallas kernels for 0% -> 0%
where the time goes in v6:
time: 305 us; the launch traced here: 299 us
  waiting for transfers between devices  151 us (50%)
  local copies, waits for them, and re-layouts  54.3 us (18%)
  starting transfers between devices  42.7 us (14%)
  matrix products  36.7 us (12%)
  other arithmetic  13.4 us (4%)
    all_to_all x1, waiting for transfers between devices, per_device(): lax.all_to_all(pair.astype(jnp.bfloat16), CHIP, split_axis=0, concat_axis...  94.3 us
    all_to_all x1, waiting for transfers between devices, per_device(): lax.all_to_all(slabs, 'grp', split_axis=0, concat_axis=0, tiled=True)  48.7 us
    unnamed x15, local copies, waits for them, and re-layouts  34.7 us
    dot_general x1, matrix products, per_device(): jnp.einsum('kyx,kxX->kyX', got_slabs, shifter, preferred_element_type=jnp...  12.3 us
    all_to_all x1, starting transfers between devices, per_device(): lax.all_to_all(packed, EXP, split_axis=0, concat_axis=0, tiled=True)  12.1 us
    all_to_all x1, starting transfers between devices, per_device(): lax.all_to_all(pair.astype(jnp.bfloat16), CHIP, split_axis=0, concat_axis...  9.99 us
    convert_element_type x1, other arithmetic, per_device(): pair.astype(jnp.bfloat16)  9.34 us
    all_to_all x1, waiting for transfers between devices, per_device(): lax.all_to_all(packed, EXP, split_axis=0, concat_axis=0, tiled=True)  8.25 us
  transfers between devices with their start and end apart: 7, of which 3 were waited for; matrix products, arithmetic and copies ran while one was open for 16% of the time, Pallas kernels for 0%

profile of v6, /device:TPU:8, one launch (start us, length us, event | category | flops | bytes accessed | tf_op | source)
XLA Modules:
  0.0 298.9 jit_solution(13103330460212290528)
XLA Ops:
  0.0 0.8 copy.24
  0.8 0.7 pad_maximum_fusion
  1.6 0.6 broadcast_in_dim.23
  2.1 4.3 %all-to-all-start = ((bf16[4,2,11]{2,1,0:T(2,128)(2,1)}), bf16[4,2,11]{2,1,0:T(2,128)(2,1)S(1)}, u32[]{:S(2)}, u32[]{:S(2)}) async-start(bf16[4,2,11]{2,1,0:T(2,128)(2,1)} %broadcast_in_dim.23), calls=%async_computation | async-start | bytes 4096 | tf_op jit(solution)/shard_map/all_to_all | solution.py:38
  6.4 2.6 convert_bitcast_fusion.1
  9.1 3.2 %convert_bitcast_fusion.2 = bf16[10,256,256,1]{2,0,1,3:T(8,128)(2,1)} fusion(bf16[10,41]{1,0:T(8,128)(2,1)S(1)} %copy-done.4), kind=kOutput, calls=%fused_computation.24 | convolution fusion | flops 62455808 | bytes 1311540 | tf_op jit(solution)/shard_map/bd,dij->bij/dot_general | solution.py:19
  12.4 0.0 all-to-all-done
  12.4 0.1 broadcast_in_dim.24
  12.5 0.6 broadcast_in_dim.25
  13.1 12.1 %all-to-all-start.1 = ((bf16[64,1,88]{2,1,0:T(2,128)(2,1)}), bf16[64,1,88]{2,1,0:T(2,128)(2,1)S(1)}, u32[]{:S(2)}, u32[]{:S(2)}) async-start(bf16[64,1,88]{2,1,0:T(2,128)(2,1)} %broadcast_in_dim.25), calls=%async_computation.1 | async-start | bytes 65536 | tf_op jit(solution)/shard_map/all_to_all | solution.py:41
  25.2 0.1 stack.13
  25.3 0.1 stack.14
  25.4 0.1 stack.12
  25.5 8.3 %all-to-all-done.1 = bf16[64,1,88]{2,1,0:T(2,128)(2,1)S(1)} async-done(((bf16[64,1,88]{2,1,0:T(2,128)(2,1)}), bf16[64,1,88]{2,1,0:T(2,128)(2,1)S(1)}, u32[]{:S(2)}, u32[]{:S(2)}) %all-to-all-start.1) | async-done | bytes 11296 | tf_op jit(solution)/shard_map/all_to_all | solution.py:41
  33.7 0.1 reduce.2
  33.8 0.1 reshape.88
  34.0 0.2 fusion.62
  34.2 0.2 slice_reduce_fusion
  34.3 0.1 stack_broadcast_in_dim.7
  34.4 0.1 stack_broadcast_in_dim.8
  34.5 0.6 broadcast_in_dim.27
  35.1 5.3 %all-to-all-start.2 = ((f32[4,16,4]{1,2,0:T(4,128)}), f32[4,16,4]{1,2,0:T(4,128)S(1)}, u32[]{:S(2)}, u32[]{:S(2)}) async-start(f32[4,16,4]{1,2,0:T(4,128)} %broadcast_in_dim.27), calls=%async_computation.2 | async-start | bytes 16384 | tf_op jit(solution)/shard_map/all_to_all | solution.py:84
  40.5 0.1 copy.27
  40.6 6.7 %fusion.33 = bf16[4,256,256,1,1]{2,1,4,3,0:T(8,128)(2,1)S(1)} fusion(bf16[10,256,256,1]{2,0,1,3:T(8,128)(2,1)S(1)} %convert_bitcast_fusion.1, f32[4,10]{0,1:T(8,128)S(1)} %copy.27, bf16[10,256,256,1]{2,0,1,3:T(8,128)(2,1)} %convert_bitcast_fusion.2, bf16[4,256,256]{2,1,0:T(8,128)(2,1)S(1)} %copy-done, f32[4]{0:T(128)S(1)} %slice_reduce_fusion), kind=kOutput, calls=%fused_computation.30 | convolution fusion | flops 2690121728 | bytes 3670192 | tf_op jit(solution)/shard_map/byk,tkbx->tyx/dot_general | solution.py:58
  47.3 4.3 %convert_bitcast_fusion = bf16[4,4,4,128,256]{3,4,2,0,1:T(8,128)(2,1)} fusion(bf16[4,256,256,1,1]{2,1,4,3,0:T(8,128)(2,1)S(1)} %fusion.33, s32[4,4]{1,0:T(4,128)S(1)} %bitcast.94, s32[4]{0:T(128)S(1)} %iota_multiply_fusion), kind=kOutput, calls=%fused_computation.19 | convolution fusion | flops 1082130432 | bytes 4718672 | tf_op jit(solution)/shard_map/gtjiy,tyx->gtjix/dot_general | solution.py:71
  51.6 7.3 %copy.29 = bf16[4,4,4,128,256]{4,3,2,1,0:T(8,128)(2,1)} copy(bf16[4,4,4,128,256]{3,4,2,0,1:T(8,128)(2,1)} %convert_bitcast_fusion) | data formatting | bytes 8388608 | tf_op jit(solution)/shard_map/convert_element_type | solution.py:72
  58.9 5.1 %all-to-all-start.3 = ((bf16[64,128,256]{2,1,0:T(8,128)(2,1)}), bf16[64,128,256]{2,1,0:T(8,128)(2,1)}, u32[]{:S(2)}, u32[]{:S(2)}) async-start(bf16[64,128,256]{2,1,0:T(8,128)(2,1)} %bitcast.91), calls=%async_computation.3 | async-start | bytes 8388608 | tf_op jit(solution)/shard_map/all_to_all | solution.py:83
  64.0 0.1 all_to_all.29
  64.1 48.7 %all-to-all-done.3 = bf16[64,128,256]{2,1,0:T(8,128)(2,1)} async-done(((bf16[64,128,256]{2,1,0:T(8,128)(2,1)}), bf16[64,128,256]{2,1,0:T(8,128)(2,1)}, u32[]{:S(2)}, u32[]{:S(2)}) %all-to-all-start.3) | async-done | bytes 4194336 | tf_op jit(solution)/shard_map/all_to_all | solution.py:83
  112.9 12.3 %fusion.7 = bf16[64,128,512]{2,1,0:T(8,128)(2,1)} fusion(bf16[64,128,256]{2,1,0:T(8,128)(2,1)} %all-to-all-done.3, s32[64]{0:T(128)S(1)} %get-tuple-element.15), kind=kOutput, calls=%fused_computation.14 | convolution fusion | flops 2168455168 | bytes 12583168 | tf_op jit(solution)/shard_map/kyx,kxX->kyX/dot_general | solution.py:93
  125.2 11.8 %copy.40 = bf16[8,8,128,512]{3,1,2,0:T(8,128)(2,1)} copy(bf16[8,8,128,512]{3,2,1,0:T(8,128)(2,1)} %bitcast.92) | data formatting | bytes 16777216
  136.9 5.7 %fusion.60 = f32[64,65536]{1,0:T(8,128)S(1)} fusion(bf16[64,65536]{1,0:T(8,128)(2,1)} %bitcast.88, s32[64]{0:T(128)S(1)} %fusion.66), kind=kOutput, calls=%fused_computation.55 | convolution fusion | flops 536875008 | bytes 25166080 | tf_op jit(solution)/shard_map/dot_general | solution.py:100
  142.6 6.6 %fusion.71 = (f32[32,65536]{1,0:T(8,128)}, f32[32,65536]{1,0:T(8,128)}) fusion(f32[64,65536]{1,0:T(8,128)S(1)} %fusion.60), kind=kLoop, calls=%fused_computation.88 | loop fusion | bytes 33554432 | tf_op jit(solution)/shard_map/slice | solution.py:117
  149.3 11.5 %copy.42 = f32[4,8,128,512]{3,2,1,0:T(8,128)} copy(f32[4,8,128,512]{3,1,2,0:T(8,128)} %bitcast.90) | data formatting | bytes 16777216
  160.7 0.1 copy.30
  160.8 0.1 fusion.59
  160.9 0.1 reduce_window_sum.11
  161.0 0.2 select_reduce_fusion
  161.2 0.8 scatter_custom_fusion
  162.0 1.1 copy.31
  163.1 5.9 %all-to-all-start.5 = ((f32[64,8,3]{1,2,0:T(4,128)}), f32[64,8,3]{1,2,0:T(4,128)S(1)}, u32[]{:S(2)}, u32[]{:S(2)}) async-start(f32[64,8,3]{1,2,0:T(4,128)} %copy.31), calls=%async_computation.5 | async-start | bytes 262144 | tf_op jit(solution)/shard_map/all_to_all | solution.py:120
  169.0 11.4 %copy.41 = f32[4,8,128,512]{3,2,1,0:T(8,128)} copy(f32[4,8,128,512]{3,1,2,0:T(8,128)} %bitcast.89) | data formatting | bytes 16777216
  180.4 9.3 %fusion.5 = bf16[32,128,512]{2,1,0:T(8,128)(2,1)} fusion(f32[32,128,512]{2,1,0:T(8,128)} %collective-permute-done, f32[4,8,128,512]{3,2,1,0:T(8,128)} %copy.41), kind=kLoop, calls=%fused_computation.10 | loop fusion | flops 4194304 | bytes 20971520 | tf_op jit(solution)/shard_map/convert_element_type | solution.py:118
  189.8 10.0 %all-to-all-start.4 = ((bf16[32,128,512]{2,1,0:T(8,128)(2,1)}), bf16[32,128,512]{2,1,0:T(8,128)(2,1)}, u32[]{:S(2)}, u32[]{:S(2)}) async-start(bf16[32,128,512]{2,1,0:T(8,128)(2,1)} %fusion.5), calls=%async_computation.4 | async-start | bytes 8388608 | tf_op jit(solution)/shard_map/all_to_all | solution.py:118
  199.8 0.1 all_to_all.34
  199.9 94.3 %all-to-all-done.4 = bf16[32,128,512]{2,1,0:T(8,128)(2,1)} async-done(((bf16[32,128,512]{2,1,0:T(8,128)(2,1)}), bf16[32,128,512]{2,1,0:T(8,128)(2,1)}, u32[]{:S(2)}, u32[]{:S(2)}) %all-to-all-start.4) | async-done | bytes 4194336 | tf_op jit(solution)/shard_map/all_to_all | solution.py:118
  294.2 2.8 convert_reduce_fusion
  297.0 1.6 fusion.41
  (31 shorter events, 0.2 us)
Async XLA Ops:
  0.0 40.6 %copy-start = (bf16[4,256,256]{2,1,0:T(8,128)(2,1)S(1)}, bf16[4,256,256]{2,1,0:T(8,128)(2,1)}, u32[]{:S(2)}) copy-start(bf16[4,256,256]{2,1,0:T(8,128)(2,1)} %param.8) | copy-start | bytes 1572868
  0.0 9.1 %copy-start.4 = (bf16[10,41]{1,0:T(8,128)(2,1)S(1)}, bf16[10,41]{1,0:T(8,128)(2,1)}, u32[]{:S(2)}) copy-start(bf16[10,41]{1,0:T(8,128)(2,1)} %param.15) | copy-start | bytes 2464
  2.1 10.2 %all-to-all-start = ((bf16[4,2,11]{2,1,0:T(2,128)(2,1)}), bf16[4,2,11]{2,1,0:T(2,128)(2,1)S(1)}, u32[]{:S(2)}, u32[]{:S(2)}) async-start(bf16[4,2,11]{2,1,0:T(2,128)(2,1)} %broadcast_in_dim.23), calls=%async_computation | async-start | bytes 4096 | tf_op jit(solution)/shard_map/all_to_all | solution.py:38
  6.4 5.9 %copy-start.2 = (s32[4,4,2]{1,2,0:T(2,128)S(1)}, s32[4,4,2]{1,2,0:T(2,128)}, u32[]{:S(2)}) copy-start(s32[4,4,2]{1,2,0:T(2,128)} %param.11) | copy-start | bytes 388
  6.4 18.9 %copy-start.3 = (s32[4,4]{1,0:T(4,128)S(1)}, s32[4,4]{1,0:T(4,128)}, u32[]{:S(2)}) copy-start(s32[4,4]{1,0:T(4,128)} %param.10) | copy-start | bytes 196
  6.4 27.5 %copy-start.5 = (s32[4]{0:T(128)S(1)}, s32[4]{0:T(128)}, u32[]{:S(2)}) copy-start(s32[4]{0:T(128)} %param.9) | copy-start | bytes 52
  12.3 35.0 %slice-start = ((s32[4,4,2]{1,2,0:T(2,128)}), s32[4,4,1]{1,2,0:T(1,128)S(1)}, s32[]{:S(2)}) async-start(s32[4,4,2]{1,2,0:T(2,128)} %param.11), calls=%async_computation.6 | async-start | bytes 4096 | tf_op jit(solution)/shard_map/slice | solution.py:63
  13.1 20.6 %all-to-all-start.1 = ((bf16[64,1,88]{2,1,0:T(2,128)(2,1)}), bf16[64,1,88]{2,1,0:T(2,128)(2,1)S(1)}, u32[]{:S(2)}, u32[]{:S(2)}) async-start(bf16[64,1,88]{2,1,0:T(2,128)(2,1)} %broadcast_in_dim.25), calls=%async_computation.1 | async-start | bytes 65536 | tf_op jit(solution)/shard_map/all_to_all | solution.py:41
  35.1 23.8 %all-to-all-start.2 = ((f32[4,16,4]{1,2,0:T(4,128)}), f32[4,16,4]{1,2,0:T(4,128)S(1)}, u32[]{:S(2)}, u32[]{:S(2)}) async-start(f32[4,16,4]{1,2,0:T(4,128)} %broadcast_in_dim.27), calls=%async_computation.2 | async-start | bytes 16384 | tf_op jit(solution)/shard_map/all_to_all | solution.py:84
  58.9 54.0 %all-to-all-start.3 = ((bf16[64,128,256]{2,1,0:T(8,128)(2,1)}), bf16[64,128,256]{2,1,0:T(8,128)(2,1)}, u32[]{:S(2)}, u32[]{:S(2)}) async-start(bf16[64,128,256]{2,1,0:T(8,128)(2,1)} %bitcast.91), calls=%async_computation.3 | async-start | bytes 8388608 | tf_op jit(solution)/shard_map/all_to_all | solution.py:83
  160.7 19.7 %collective-permute-start = (f32[32,128,512]{2,1,0:T(8,128)}, f32[32,128,512]{2,1,0:T(8,128)}, u32[]{:S(2)}, u32[]{:S(2)}) collective-permute-start(f32[32,128,512]{2,1,0:T(8,128)} %bitcast.36), channel_id=1, source_target_pairs={{0,4},{4,0},{1,5},{5,1},{2,6},{6,2},{3,7},{7,3},{8,12},{12,8},{9,1... | collective-permute-start | bytes 25165832 | tf_op jit(solution)/shard_map/ppermute | solution.py:117
  163.1 26.7 %all-to-all-start.5 = ((f32[64,8,3]{1,2,0:T(4,128)}), f32[64,8,3]{1,2,0:T(4,128)S(1)}, u32[]{:S(2)}, u32[]{:S(2)}) async-start(f32[64,8,3]{1,2,0:T(4,128)} %copy.31), calls=%async_computation.5 | async-start | bytes 262144 | tf_op jit(solution)/shard_map/all_to_all | solution.py:120
  180.4 118.2 %copy-start.1 = (bf16[4,256,256]{2,1,0:T(8,128)(2,1)S(1)}, bf16[4,256,256]{2,1,0:T(8,128)(2,1)}, u32[]{:S(2)}) copy-start(bf16[4,256,256]{2,1,0:T(8,128)(2,1)} %param.8) | copy-start | bytes 1572868
  189.8 104.5 %all-to-all-start.4 = ((bf16[32,128,512]{2,1,0:T(8,128)(2,1)}), bf16[32,128,512]{2,1,0:T(8,128)(2,1)}, u32[]{:S(2)}, u32[]{:S(2)}) async-start(bf16[32,128,512]{2,1,0:T(8,128)(2,1)} %fusion.5), calls=%async_computation.4 | async-start | bytes 8388608 | tf_op jit(solution)/shard_map/all_to_all | solution.py:118

commit v7 on v6

--- a/solution.py
+++ b/solution.py
@@ -36,7 +36,7 @@
     packed = jnp.concatenate([coeffs, inv_var[:, None]], axis=1)
     packed = jnp.broadcast_to(packed[None], (n_bands,) + packed.shape)
     packed = lax.all_to_all(packed, "grp", split_axis=0, concat_axis=0, tiled=True)
-    packed = packed.reshape(1, 1, -1)
+    packed = packed.reshape(1, -1, terms + 1)
     packed = jnp.broadcast_to(packed, (n_owners,) + packed.shape[1:])
     packed = lax.all_to_all(packed, EXP, split_axis=0, concat_axis=0, tiled=True)
     packed = packed.reshape(-1, terms + 1)
@@ -93,13 +93,13 @@
     shifted = jnp.einsum("kyx,kxX->kyX", got_slabs, shifter, preferred_element_type=jnp.float32)
     shifted = shifted.astype(jnp.bfloat16)
     chips = n_owners // n_halves
-    owner_row = jnp.where(got_patch % n_halves == h, chips, 0) + got_patch // n_halves
-    owner_of = (
-        owner_row[None, :] == jnp.arange(n_owners, dtype=jnp.int32)[:, None]
-    ).astype(jnp.bfloat16)
-    bands = jnp.dot(
-        owner_of, shifted.reshape(entries, band_rows * PS), preferred_element_type=jnp.float32
-    ).reshape(n_halves, chips, band_rows, PS)
+    chip_patch = n_halves * jnp.arange(chips, dtype=jnp.int32)[:, None]
+    flat_shifted = shifted.reshape(entries, band_rows * PS)
+    give_of = (got_patch[None, :] == chip_patch + (1 - h)).astype(jnp.bfloat16)
+    give = jnp.dot(give_of, flat_shifted, preferred_element_type=jnp.float32)
+    got_give = lax.ppermute(give, "ec", perm=[(0, 1), (1, 0)])
+    keep_of = (got_patch[None, :] == chip_patch + h).astype(jnp.bfloat16)
+    keep = jnp.dot(keep_of, flat_shifted, preferred_element_type=jnp.float32)
 
     per_owner = n_bands * 2
     onehot = (got_patch[:, None] == jnp.arange(n_owners, dtype=jnp.int32)[None, :]).astype(
@@ -114,7 +114,7 @@
         .set(got_meta[:, 1:], mode="drop")
     )
 
-    pair = bands[1] + lax.ppermute(bands[0], "ec", perm=[(0, 1), (1, 0)])
+    pair = (keep + got_give).reshape(chips, band_rows, PS)
     recv_bands = lax.all_to_all(pair.astype(jnp.bfloat16), CHIP, split_axis=0, concat_axis=0, tiled=True)
     flux = jnp.sum(recv_bands.astype(jnp.float32), axis=0)
     recv_meta = lax.all_to_all(meta_slots, EXP, split_axis=0, concat_axis=0, tiled=True)

time: 305 us -> 276 us (0.905); the launches traced: 299 us -> 273 us
  local copies, waits for them, and re-layouts: 54.3 us -> 28.1 us
  other arithmetic: 13.4 us -> 3.97 us
  matrix products: 36.7 us -> 46 us
  waiting for transfers between devices: 151 us -> 157 us
  starting transfers between devices: 42.7 us -> 37.9 us
    unnamed x15 -> x12, local copies, waits for them, and re-layouts: 34.7 us -> 15.2 us
    convert_element_type x1 -> x0, other arithmetic: 9.34 us -> none  [per_device(): pair.astype(jnp.bfloat16)]
    dot_general x1 -> x2, matrix products: 5.69 us -> 15 us  [the longest x1 7.89 us: per_device(): give = jnp.dot(give_of, flat_shifted, preferred_element_type=jnp.float32)]
    slice x1 -> x0, local copies, waits for them, and re-layouts: 6.62 us -> none  [per_device(): pair = bands[1] + lax.ppermute(bands[0], 'ec', perm=[(0, 1), (1, 0)])]
    ppermute x1, waiting for transfers between devices: 0.01 us -> 5.26 us  [per_device(): got_give = lax.ppermute(give, 'ec', perm=[(0, 1), (1, 0)])]
    all_to_all x1, starting transfers between devices: 9.99 us -> 5.84 us  [per_device(): lax.all_to_all(pair.astype(jnp.bfloat16), CHIP, split_axis=0, concat_axis...]
  transfers between devices with their start and end apart: 7 -> 7, of which waited for: 3 -> 4; matrix products, arithmetic and copies ran while one was open for 16% -> 14% of each run, Pallas kernels for 0% -> 0%
where the time goes in v7:
time: 276 us; the launch traced here: 273 us
  waiting for transfers between devices  157 us (57%)
  matrix products  46 us (17%)
  starting transfers between devices  37.9 us (14%)
  local copies, waits for them, and re-layouts  28.1 us (10%)
  other arithmetic  3.97 us (1%)
    all_to_all x1, waiting for transfers between devices, per_device(): lax.all_to_all(pair.astype(jnp.bfloat16), CHIP, split_axis=0, concat_axis...  93.8 us
    all_to_all x1, waiting for transfers between devices, per_device(): lax.all_to_all(slabs, 'grp', split_axis=0, concat_axis=0, tiled=True)  49 us
    unnamed x12, local copies, waits for them, and re-layouts  15.2 us
    dot_general x1, matrix products, per_device(): jnp.einsum('kyx,kxX->kyX', got_slabs, shifter, preferred_element_type=jnp...  12.3 us
    all_to_all x1, starting transfers between devices, per_device(): lax.all_to_all(packed, EXP, split_axis=0, concat_axis=0, tiled=True)  12.1 us
    all_to_all x1, waiting for transfers between devices, per_device(): lax.all_to_all(packed, EXP, split_axis=0, concat_axis=0, tiled=True)  9.13 us
    dot_general x1, matrix products, per_device(): give = jnp.dot(give_of, flat_shifted, preferred_element_type=jnp.float32)  7.89 us
    convert_element_type x1, local copies, waits for them, and re-layouts, per_device(): slabs.astype(jnp.bfloat16)  7.31 us
  transfers between devices with their start and end apart: 7, of which 4 were waited for; matrix products, arithmetic and copies ran while one was open for 14% of the time, Pallas kernels for 0%

profile of v7, /device:TPU:8, one launch (start us, length us, event | category | flops | bytes accessed | tf_op | source)
XLA Modules:
  0.0 273.4 jit_solution(844668808022867914)
XLA Ops:
  0.0 0.0 copy-start
  0.0 0.8 copy.24
  0.8 0.7 pad_maximum_fusion
  1.6 0.6 broadcast_in_dim.17
  2.1 4.3 %all-to-all-start = ((bf16[4,2,11]{2,1,0:T(2,128)(2,1)}), bf16[4,2,11]{2,1,0:T(2,128)(2,1)S(1)}, u32[]{:S(2)}, u32[]{:S(2)}) async-start(bf16[4,2,11]{2,1,0:T(2,128)(2,1)} %broadcast_in_dim.17), calls=%async_computation | async-start | bytes 4096 | tf_op jit(solution)/shard_map/all_to_all | solution.py:38
  6.4 2.6 convert_bitcast_fusion.1
  9.1 3.2 %convert_bitcast_fusion.2 = bf16[10,256,256,1]{2,0,1,3:T(8,128)(2,1)} fusion(bf16[10,41]{1,0:T(8,128)(2,1)S(1)} %copy-done.3), kind=kOutput, calls=%fused_computation.24 | convolution fusion | flops 62455808 | bytes 1311540 | tf_op jit(solution)/shard_map/bd,dij->bij/dot_general | solution.py:19
  12.4 0.0 all-to-all-done
  12.4 0.7 broadcast_in_dim.19
  13.0 12.1 %all-to-all-start.1 = ((bf16[64,8,11]{2,1,0:T(8,128)(2,1)}), bf16[64,8,11]{2,1,0:T(8,128)(2,1)S(1)}, u32[]{:S(2)}, u32[]{:S(2)}) async-start(bf16[64,8,11]{2,1,0:T(8,128)(2,1)} %broadcast_in_dim.19), calls=%async_computation.1 | async-start | bytes 262144 | tf_op jit(solution)/shard_map/all_to_all | solution.py:41
  25.2 0.1 stack.13
  25.2 0.1 stack.14
  25.3 0.1 stack.12
  25.4 9.1 %all-to-all-done.1 = bf16[64,8,11]{2,1,0:T(8,128)(2,1)S(1)} async-done(((bf16[64,8,11]{2,1,0:T(8,128)(2,1)}), bf16[64,8,11]{2,1,0:T(8,128)(2,1)S(1)}, u32[]{:S(2)}, u32[]{:S(2)}) %all-to-all-start.1) | async-done | bytes 11296 | tf_op jit(solution)/shard_map/all_to_all | solution.py:41
  34.6 0.2 fusion.52
  34.7 0.2 slice_reduce_fusion
  34.9 0.1 stack_broadcast_in_dim.7
  35.0 0.1 stack_broadcast_in_dim.8
  35.1 0.6 broadcast_in_dim.21
  35.7 4.8 %all-to-all-start.2 = ((f32[4,16,4]{1,2,0:T(4,128)}), f32[4,16,4]{1,2,0:T(4,128)S(1)}, u32[]{:S(2)}, u32[]{:S(2)}) async-start(f32[4,16,4]{1,2,0:T(4,128)} %broadcast_in_dim.21), calls=%async_computation.2 | async-start | bytes 16384 | tf_op jit(solution)/shard_map/all_to_all | solution.py:84
  40.5 0.1 copy.27
  40.6 6.7 %fusion.33 = bf16[4,256,256,1,1]{2,1,4,3,0:T(8,128)(2,1)S(1)} fusion(bf16[10,256,256,1]{2,0,1,3:T(8,128)(2,1)S(1)} %convert_bitcast_fusion.1, f32[4,10]{0,1:T(8,128)S(1)} %copy.27, bf16[10,256,256,1]{2,0,1,3:T(8,128)(2,1)} %convert_bitcast_fusion.2, bf16[4,256,256]{2,1,0:T(8,128)(2,1)S(1)} %copy-done, f32[4]{0:T(128)S(1)} %slice_reduce_fusion), kind=kOutput, calls=%fused_computation.30 | convolution fusion | flops 2690121728 | bytes 3670192 | tf_op jit(solution)/shard_map/byk,tkbx->tyx/dot_general | solution.py:58
  47.3 4.3 %convert_bitcast_fusion = bf16[4,4,4,128,256]{3,4,2,0,1:T(8,128)(2,1)} fusion(bf16[4,256,256,1,1]{2,1,4,3,0:T(8,128)(2,1)S(1)} %fusion.33, s32[4,4]{1,0:T(4,128)S(1)} %bitcast.92, s32[4]{0:T(128)S(1)} %iota_multiply_fusion), kind=kOutput, calls=%fused_computation.19 | convolution fusion | flops 1082130432 | bytes 4718672 | tf_op jit(solution)/shard_map/gtjiy,tyx->gtjix/dot_general | solution.py:71
  51.6 7.3 %copy.29 = bf16[4,4,4,128,256]{4,3,2,1,0:T(8,128)(2,1)} copy(bf16[4,4,4,128,256]{3,4,2,0,1:T(8,128)(2,1)} %convert_bitcast_fusion) | data formatting | bytes 8388608 | tf_op jit(solution)/shard_map/convert_element_type | solution.py:72
  58.9 0.0 all-to-all-done.2
  58.9 5.0 %all-to-all-start.3 = ((bf16[64,128,256]{2,1,0:T(8,128)(2,1)}), bf16[64,128,256]{2,1,0:T(8,128)(2,1)}, u32[]{:S(2)}, u32[]{:S(2)}) async-start(bf16[64,128,256]{2,1,0:T(8,128)(2,1)} %bitcast.89), calls=%async_computation.3 | async-start | bytes 8388608 | tf_op jit(solution)/shard_map/all_to_all | solution.py:83
  64.0 0.1 all_to_all.29
  64.1 49.0 %all-to-all-done.3 = bf16[64,128,256]{2,1,0:T(8,128)(2,1)} async-done(((bf16[64,128,256]{2,1,0:T(8,128)(2,1)}), bf16[64,128,256]{2,1,0:T(8,128)(2,1)}, u32[]{:S(2)}, u32[]{:S(2)}) %all-to-all-start.3) | async-done | bytes 4194336 | tf_op jit(solution)/shard_map/all_to_all | solution.py:83
  113.1 12.3 %fusion.7 = bf16[64,128,512]{2,1,0:T(8,128)(2,1)} fusion(bf16[64,128,256]{2,1,0:T(8,128)(2,1)} %all-to-all-done.3, s32[64]{0:T(128)S(1)} %get-tuple-element.13), kind=kOutput, calls=%fused_computation.14 | convolution fusion | flops 2168455168 | bytes 12583168 | tf_op jit(solution)/shard_map/kyx,kxX->kyX/dot_general | solution.py:93
  125.5 11.7 %copy.40 = bf16[8,8,128,512]{3,1,2,0:T(8,128)(2,1)} copy(bf16[8,8,128,512]{3,2,1,0:T(8,128)(2,1)} %bitcast.90) | data formatting | bytes 16777216
  137.2 7.9 %fusion.62 = f32[32,65536]{1,0:T(8,128)} fusion(bf16[64,65536]{1,0:T(8,128)(2,1)} %bitcast.85, s32[64]{0:T(128)S(1)} %get-tuple-element.12, s32[32]{0:T(128)S(1)} %fusion.73), kind=kOutput, calls=%fused_computation.56 | convolution fusion | flops 268437504 | bytes 16777600 | tf_op jit(solution)/shard_map/dot_general | solution.py:99
  145.1 0.0 collective-permute-start
  145.1 0.1 copy.30
  145.2 0.1 fusion.61
  145.3 0.1 reduce_window_sum.11
  145.4 0.2 select_reduce_fusion
  145.6 0.8 scatter_custom_fusion
  146.4 1.1 copy.31
  147.5 5.8 %all-to-all-start.5 = ((f32[64,8,3]{1,2,0:T(4,128)}), f32[64,8,3]{1,2,0:T(4,128)S(1)}, u32[]{:S(2)}, u32[]{:S(2)}) async-start(f32[64,8,3]{1,2,0:T(4,128)} %copy.31), calls=%async_computation.5 | async-start | bytes 262144 | tf_op jit(solution)/shard_map/all_to_all | solution.py:120
  153.4 5.3 %collective-permute-done = f32[32,65536]{1,0:T(8,128)} collective-permute-done((f32[32,65536]{1,0:T(8,128)}, f32[32,65536]{1,0:T(8,128)}, u32[]{:S(2)}, u32[]{:S(2)}) %collective-permute-start) | collective-permute-done | bytes 8388640 | tf_op jit(solution)/shard_map/ppermute | solution.py:100
  158.6 7.1 %fusion = bf16[32,65536]{1,0:T(8,128)(2,1)S(1)} fusion(f32[32,65536]{1,0:T(8,128)} %collective-permute-done, bf16[64,65536]{1,0:T(8,128)(2,1)} %bitcast.86, s32[64]{0:T(128)S(1)} %get-tuple-element.12, s32[32]{0:T(128)S(1)} %fusion.74), kind=kOutput, calls=%fused_computation.2 | convolution fusion | flops 272631808 | bytes 20971904 | tf_op jit(solution)/shard_map/dot_general | solution.py:102
  165.7 3.5 %copy.41 = bf16[4,8,128,512]{3,2,1,0:T(8,128)(2,1)} copy(bf16[4,8,128,512]{3,1,2,0:T(8,128)(2,1)S(1)} %bitcast.87) | data formatting | bytes 8388608
  169.2 0.0 all-to-all-done.5
  169.2 5.8 %all-to-all-start.4 = ((bf16[32,128,512]{2,1,0:T(8,128)(2,1)}), bf16[32,128,512]{2,1,0:T(8,128)(2,1)}, u32[]{:S(2)}, u32[]{:S(2)}) async-start(bf16[32,128,512]{2,1,0:T(8,128)(2,1)} %bitcast.88), calls=%async_computation.4 | async-start | bytes 8388608 | tf_op jit(solution)/shard_map/all_to_all | solution.py:118
  175.1 0.1 all_to_all.34
  175.2 93.8 %all-to-all-done.4 = bf16[32,128,512]{2,1,0:T(8,128)(2,1)} async-done(((bf16[32,128,512]{2,1,0:T(8,128)(2,1)}), bf16[32,128,512]{2,1,0:T(8,128)(2,1)}, u32[]{:S(2)}, u32[]{:S(2)}) %all-to-all-start.4) | async-done | bytes 4194336 | tf_op jit(solution)/shard_map/all_to_all | solution.py:118
  269.0 2.8 %convert_reduce_fusion = f32[128,512]{1,0:T(8,128)S(1)} fusion(bf16[32,128,512]{2,1,0:T(8,128)(2,1)} %all-to-all-done.4), kind=kLoop, calls=%fused_computation.11 | loop fusion | flops 4128768 | bytes 4456448 | tf_op jit(solution)/shard_map/reduce_sum | solution.py:119
  271.8 1.6 fusion.41
  (25 shorter events, 0.1 us)
Async XLA Ops:
  0.0 40.6 %copy-start = (bf16[4,256,256]{2,1,0:T(8,128)(2,1)S(1)}, bf16[4,256,256]{2,1,0:T(8,128)(2,1)}, u32[]{:S(2)}) copy-start(bf16[4,256,256]{2,1,0:T(8,128)(2,1)} %param.8) | copy-start | bytes 1572868
  0.0 9.1 %copy-start.3 = (bf16[10,41]{1,0:T(8,128)(2,1)S(1)}, bf16[10,41]{1,0:T(8,128)(2,1)}, u32[]{:S(2)}) copy-start(bf16[10,41]{1,0:T(8,128)(2,1)} %param.15) | copy-start | bytes 2464
  2.1 10.2 %all-to-all-start = ((bf16[4,2,11]{2,1,0:T(2,128)(2,1)}), bf16[4,2,11]{2,1,0:T(2,128)(2,1)S(1)}, u32[]{:S(2)}, u32[]{:S(2)}) async-start(bf16[4,2,11]{2,1,0:T(2,128)(2,1)} %broadcast_in_dim.17), calls=%async_computation | async-start | bytes 4096 | tf_op jit(solution)/shard_map/all_to_all | solution.py:38
  6.4 5.9 %copy-start.1 = (s32[4,4,2]{1,2,0:T(2,128)S(1)}, s32[4,4,2]{1,2,0:T(2,128)}, u32[]{:S(2)}) copy-start(s32[4,4,2]{1,2,0:T(2,128)} %param.11) | copy-start | bytes 388
  6.4 18.9 %copy-start.2 = (s32[4,4]{1,0:T(4,128)S(1)}, s32[4,4]{1,0:T(4,128)}, u32[]{:S(2)}) copy-start(s32[4,4]{1,0:T(4,128)} %param.10) | copy-start | bytes 196
  6.4 28.1 %copy-start.4 = (s32[4]{0:T(128)S(1)}, s32[4]{0:T(128)}, u32[]{:S(2)}) copy-start(s32[4]{0:T(128)} %param.9) | copy-start | bytes 52
  12.3 35.0 %slice-start = ((s32[4,4,2]{1,2,0:T(2,128)}), s32[4,4,1]{1,2,0:T(1,128)S(1)}, s32[]{:S(2)}) async-start(s32[4,4,2]{1,2,0:T(2,128)} %param.11), calls=%async_computation.6 | async-start | bytes 4096 | tf_op jit(solution)/shard_map/slice | solution.py:63
  13.0 21.5 %all-to-all-start.1 = ((bf16[64,8,11]{2,1,0:T(8,128)(2,1)}), bf16[64,8,11]{2,1,0:T(8,128)(2,1)S(1)}, u32[]{:S(2)}, u32[]{:S(2)}) async-start(bf16[64,8,11]{2,1,0:T(8,128)(2,1)} %broadcast_in_dim.19), calls=%async_computation.1 | async-start | bytes 262144 | tf_op jit(solution)/shard_map/all_to_all | solution.py:41
  35.7 23.2 %all-to-all-start.2 = ((f32[4,16,4]{1,2,0:T(4,128)}), f32[4,16,4]{1,2,0:T(4,128)S(1)}, u32[]{:S(2)}, u32[]{:S(2)}) async-start(f32[4,16,4]{1,2,0:T(4,128)} %broadcast_in_dim.21), calls=%async_computation.2 | async-start | bytes 16384 | tf_op jit(solution)/shard_map/all_to_all | solution.py:84
  58.9 54.2 %all-to-all-start.3 = ((bf16[64,128,256]{2,1,0:T(8,128)(2,1)}), bf16[64,128,256]{2,1,0:T(8,128)(2,1)}, u32[]{:S(2)}, u32[]{:S(2)}) async-start(bf16[64,128,256]{2,1,0:T(8,128)(2,1)} %bitcast.89), calls=%async_computation.3 | async-start | bytes 8388608 | tf_op jit(solution)/shard_map/all_to_all | solution.py:83
  145.1 13.5 %collective-permute-start = (f32[32,65536]{1,0:T(8,128)}, f32[32,65536]{1,0:T(8,128)}, u32[]{:S(2)}, u32[]{:S(2)}) collective-permute-start(f32[32,65536]{1,0:T(8,128)} %fusion.62), channel_id=1, source_target_pairs={{0,4},{4,0},{1,5},{5,1},{2,6},{6,2},{3,7},{7,3},{8,12},{12,8},{9,1... | collective-permute-start | bytes 25165832 | tf_op jit(solution)/shard_map/ppermute | solution.py:100
  147.5 21.7 %all-to-all-start.5 = ((f32[64,8,3]{1,2,0:T(4,128)}), f32[64,8,3]{1,2,0:T(4,128)S(1)}, u32[]{:S(2)}, u32[]{:S(2)}) async-start(f32[64,8,3]{1,2,0:T(4,128)} %copy.31), calls=%async_computation.5 | async-start | bytes 262144 | tf_op jit(solution)/shard_map/all_to_all | solution.py:120
  169.2 99.9 %all-to-all-start.4 = ((bf16[32,128,512]{2,1,0:T(8,128)(2,1)}), bf16[32,128,512]{2,1,0:T(8,128)(2,1)}, u32[]{:S(2)}, u32[]{:S(2)}) async-start(bf16[32,128,512]{2,1,0:T(8,128)(2,1)} %bitcast.88), calls=%async_computation.4 | async-start | bytes 8388608 | tf_op jit(solution)/shard_map/all_to_all | solution.py:118

commit v8 on v7

--- a/solution.py
+++ b/solution.py
@@ -62,14 +62,6 @@
 
     row_off = tile_offset[:, :, 0]
     col_off = tile_offset[:, :, 1]
-    band_i = lax.broadcasted_iota(jnp.int32, (n_bands, tile_count, listed, band_rows, tile_side), 0)
-    inner = lax.broadcasted_iota(jnp.int32, (n_bands, tile_count, listed, band_rows, tile_side), 3)
-    src = lax.broadcasted_iota(jnp.int32, (n_bands, tile_count, listed, band_rows, tile_side), 4)
-    picks = (src == band_i * band_rows + inner - row_off[None, :, :, None, None]).astype(
-        jnp.bfloat16
-    )
-    slabs = jnp.einsum("gtjiy,tyx->gtjix", picks, weighted, preferred_element_type=jnp.float32)
-    slabs = slabs.astype(jnp.bfloat16).reshape(n_bands * tile_count * listed, band_rows, tile_side)
     meta = jnp.stack(
         [
             tile_patch.astype(jnp.float32),
@@ -80,11 +72,18 @@
         axis=-1,
     ).reshape(tile_count * listed, 4)
     meta_send = jnp.broadcast_to(meta[None], (n_bands,) + meta.shape).reshape(-1, 4)
-    got_slabs = lax.all_to_all(slabs, "grp", split_axis=0, concat_axis=0, tiled=True)
     got_meta = lax.all_to_all(meta_send, "grp", split_axis=0, concat_axis=0, tiled=True)
+    row_tiles = lax.all_gather(weighted, "grp", axis=0, tiled=True)
     entries = got_meta.shape[0]
+    sources = row_tiles.shape[0]
     got_patch = got_meta[:, 0].astype(jnp.int32)
-    got_row = got_meta[:, 1].astype(jnp.int32)
+    got_row = got_meta[:, 1].astype(jnp.int32).reshape(sources, listed)
+    shape4 = (sources, listed, band_rows, tile_side)
+    inner = lax.broadcasted_iota(jnp.int32, shape4, 2)
+    src = lax.broadcasted_iota(jnp.int32, shape4, 3)
+    picks = (src == g * band_rows + inner - got_row[:, :, None, None]).astype(jnp.bfloat16)
+    got_slabs = jnp.einsum("sjiy,syx->sjix", picks, row_tiles, preferred_element_type=jnp.float32)
+    got_slabs = got_slabs.astype(jnp.bfloat16).reshape(entries, band_rows, tile_side)
     got_col = got_meta[:, 2].astype(jnp.int32)
 
     x_in = lax.broadcasted_iota(jnp.int32, (entries, tile_side, PS), 1)

time: 276 us -> 251 us (0.909)
  waiting for transfers between devices: 157 us -> 127 us
  between operations: 0.18 us -> 13.5 us
  local copies, waits for them, and re-layouts: 28.1 us -> 21.9 us
  matrix products: 46 us -> 42.8 us
  starting transfers between devices: 37.9 us -> 40.8 us
    all_to_all x1 -> x0, waiting for transfers between devices: 49 us -> none  [per_device(): lax.all_to_all(slabs, 'grp', split_axis=0, concat_axis=0, tiled=True)]
    all_gather x0 -> x1, waiting for transfers between devices: none -> 18.1 us  [per_device(): row_tiles = lax.all_gather(weighted, 'grp', axis=0, tiled=True)]
    convert_element_type x1 -> x2, local copies, waits for them, and re-layouts: 7.31 us -> 1.08 us  [the longest x1 1 us: per_device(): weighted = (weight_tile[:, None, None] * smoothed).astype(jnp.bfloat16)]
    all_to_all x1, waiting for transfers between devices: 0.01 us -> 5.09 us  [per_device(): lax.all_to_all(meta_send, 'grp', split_axis=0, concat_axis=0, tiled=True)]
    all_to_all x1 -> x0, starting transfers between devices: 5.01 us -> none  [per_device(): lax.all_to_all(slabs, 'grp', split_axis=0, concat_axis=0, tiled=True)]
    all_to_all x1, starting transfers between devices: 5.84 us -> 10.7 us  [per_device(): lax.all_to_all(meta_slots, EXP, split_axis=0, concat_axis=0, tiled=True)]
    ppermute x1, waiting for transfers between devices: 5.26 us -> 0.8 us  [per_device(): got_give = lax.ppermute(give, 'ec', perm=[(0, 1), (1, 0)])]
    all_to_all x1, starting transfers between devices: 5.84 us -> 10.2 us  [per_device(): lax.all_to_all(pair.astype(jnp.bfloat16), CHIP, split_axis=0, concat_axis...]
  transfers between devices with their start and end apart: 7 -> 7, of which waited for: 4 -> 6; matrix products, arithmetic and copies ran while one was open for 14% -> 8% of each run, Pallas kernels for 0% -> 0%
where the time goes in v8:
time: 251 us; the launch traced here: 250 us
  waiting for transfers between devices  127 us (51%)
  matrix products  42.8 us (17%)
  starting transfers between devices  40.8 us (16%)
  local copies, waits for them, and re-layouts  21.9 us (9%)
  between operations  13.5 us (5%)
  other arithmetic  3.99 us (2%)
    all_to_all x1, waiting for transfers between devices, per_device(): lax.all_to_all(pair.astype(jnp.bfloat16), CHIP, split_axis=0, concat_axis...  94.4 us
    all_gather x1, waiting for transfers between devices, per_device(): row_tiles = lax.all_gather(weighted, 'grp', axis=0, tiled=True)  18.1 us
    unnamed x12, local copies, waits for them, and re-layouts  15.2 us
    all_to_all x1, starting transfers between devices, per_device(): lax.all_to_all(packed, EXP, split_axis=0, concat_axis=0, tiled=True)  12.1 us
    all_to_all x1, starting transfers between devices, per_device(): lax.all_to_all(meta_slots, EXP, split_axis=0, concat_axis=0, tiled=True)  10.7 us
    all_to_all x1, starting transfers between devices, per_device(): lax.all_to_all(pair.astype(jnp.bfloat16), CHIP, split_axis=0, concat_axis...  10.2 us
    dot_general x1, matrix products, per_device(): jnp.einsum('kyx,kxX->kyX', got_slabs, shifter, preferred_element_type=jnp...  10.1 us
    dot_general x1, matrix products, per_device(): give = jnp.dot(give_of, flat_shifted, preferred_element_type=jnp.float32)  7.89 us
  transfers between devices with their start and end apart: 7, of which 6 were waited for; matrix products, arithmetic and copies ran while one was open for 8% of the time, Pallas kernels for 0%

profile of v8, /device:TPU:8, one launch (start us, length us, event | category | flops | bytes accessed | tf_op | source)
XLA Modules:
  0.0 250.1 jit_solution(1392471918837765721)
XLA Ops:
  6.5 0.8 copy.23
  7.4 0.7 pad_maximum_fusion
  8.1 0.6 broadcast_in_dim.17
  8.7 4.3 %all-to-all-start = ((bf16[4,2,11]{2,1,0:T(2,128)(2,1)}), bf16[4,2,11]{2,1,0:T(2,128)(2,1)S(1)}, u32[]{:S(2)}, u32[]{:S(2)}) async-start(bf16[4,2,11]{2,1,0:T(2,128)(2,1)} %broadcast_in_dim.17), calls=%async_computation | async-start | bytes 4096 | tf_op jit(solution)/shard_map/all_to_all | solution.py:38
  13.0 2.6 %convert_bitcast_fusion = bf16[10,256,256,1]{2,0,1,3:T(8,128)(2,1)S(1)} fusion(bf16[10,41]{1,0:T(8,128)(2,1)} %param.14), kind=kOutput, calls=%fused_computation.24 | convolution fusion | flops 62455808 | bytes 1311540 | tf_op jit(solution)/shard_map/bd,dij->bij/dot_general | solution.py:19
  15.6 2.6 %all-to-all-done = bf16[4,2,11]{2,1,0:T(2,128)(2,1)S(1)} async-done(((bf16[4,2,11]{2,1,0:T(2,128)(2,1)}), bf16[4,2,11]{2,1,0:T(2,128)(2,1)S(1)}, u32[]{:S(2)}, u32[]{:S(2)}) %all-to-all-start) | async-done | bytes 208 | tf_op jit(solution)/shard_map/all_to_all | solution.py:38
  18.2 0.7 broadcast_in_dim.19
  18.8 12.1 %all-to-all-start.1 = ((bf16[64,8,11]{2,1,0:T(8,128)(2,1)}), bf16[64,8,11]{2,1,0:T(8,128)(2,1)S(1)}, u32[]{:S(2)}, u32[]{:S(2)}) async-start(bf16[64,8,11]{2,1,0:T(8,128)(2,1)} %broadcast_in_dim.19), calls=%async_computation.1 | async-start | bytes 262144 | tf_op jit(solution)/shard_map/all_to_all | solution.py:41
  30.9 0.0 all-gather.2.cloned.1.call-start
  31.0 3.2 %convert_bitcast_fusion.1 = bf16[10,256,256,1]{2,0,1,3:T(8,128)(2,1)} fusion(bf16[10,41]{1,0:T(8,128)(2,1)S(1)} %copy-done.3), kind=kOutput, calls=%fused_computation.25 | convolution fusion | flops 62455808 | bytes 1311540 | tf_op jit(solution)/shard_map/bd,dij->bij/dot_general | solution.py:19
  34.2 6.1 %all-to-all-done.1 = bf16[64,8,11]{2,1,0:T(8,128)(2,1)S(1)} async-done(((bf16[64,8,11]{2,1,0:T(8,128)(2,1)}), bf16[64,8,11]{2,1,0:T(8,128)(2,1)S(1)}, u32[]{:S(2)}, u32[]{:S(2)}) %all-to-all-start.1) | async-done | bytes 11296 | tf_op jit(solution)/shard_map/all_to_all | solution.py:41
  40.3 0.2 fusion.54
  40.5 0.2 slice_reduce_fusion
  40.7 0.1 copy.26
  40.8 6.9 %fusion.35 = bf16[4,256,256]{1,2,0:T(8,128)(2,1)S(1)} fusion(bf16[10,256,256,1]{2,0,1,3:T(8,128)(2,1)S(1)} %convert_bitcast_fusion, f32[4,10]{0,1:T(8,128)S(1)} %copy.26, bf16[10,256,256,1]{2,0,1,3:T(8,128)(2,1)} %convert_bitcast_fusion.1, bf16[4,256,256]{2,1,0:T(8,128)(2,1)S(1)} %copy-done, f32[4]{0:T(128)S(1)} %slice_reduce_fusion), kind=kOutput, calls=%fused_computation.31 | convolution fusion | flops 2690121728 | bytes 3670192 | tf_op jit(solution)/shard_map/byk,tkbx->tyx/dot_general | solution.py:58
  47.7 1.0 copy.28
  48.7 0.0 all-gather.2.cloned.1.call-update
  48.8 0.1 stack.13
  48.9 0.1 stack.14
  49.0 0.1 stack.12
  49.0 0.1 stack_broadcast_in_dim.7
  49.1 0.1 stack_broadcast_in_dim.8
  49.2 0.6 broadcast_in_dim.21
  49.8 3.4 %all-to-all-start.2 = ((f32[4,16,4]{1,2,0:T(4,128)}), f32[4,16,4]{1,2,0:T(4,128)S(1)}, u32[]{:S(2)}, u32[]{:S(2)}) async-start(f32[4,16,4]{1,2,0:T(4,128)} %broadcast_in_dim.21), calls=%async_computation.2 | async-start | bytes 16384 | tf_op jit(solution)/shard_map/all_to_all | solution.py:75
  53.3 5.1 %all-to-all-done.2 = f32[4,16,4]{1,2,0:T(4,128)S(1)} async-done(((f32[4,16,4]{1,2,0:T(4,128)}), f32[4,16,4]{1,2,0:T(4,128)S(1)}, u32[]{:S(2)}, u32[]{:S(2)}) %all-to-all-start.2) | async-done | bytes 1056 | tf_op jit(solution)/shard_map/all_to_all | solution.py:75
  58.4 0.1 all_to_all.26
  58.5 0.1 fusion.63
  58.5 0.1 reduce_window_sum.11
  58.6 0.2 select_reduce_fusion
  58.8 0.1 convert_element_type.107
  58.9 18.1 %all-gather.2.cloned.1.call-done = bf16[16,256,256]{2,1,0:T(8,128)(2,1)} async-done(((bf16[4,256,256]{2,1,0:T(8,128)(2,1)}), bf16[16,256,256]{2,1,0:T(8,128)(2,1)}) %all-gather.2.cloned.1.call-update) | async-done | bytes 2097168 | tf_op jit(solution)/shard_map/all_gather | solution.py:76
  77.0 3.2 %fusion.17 = bf16[16,4,128,256]{3,2,1,0:T(8,128)(2,1)S(1)} fusion(s32[16,4]{1,0:T(8,128)S(1)} %convert_element_type.107, s32[128]{0:T(128)S(1)} %iota_add_fusion, bf16[16,256,256]{2,1,0:T(8,128)(2,1)} %all-gather.2.cloned.1.call-done), kind=kOutput, calls=%fused_computation.22 | convolution fusion | flops 1080033280 | bytes 6292224 | tf_op jit(solution)/shard_map/sjiy,syx->sjix/dot_general | solution.py:85
  80.3 10.1 %fusion.7 = bf16[64,128,512]{2,1,0:T(8,128)(2,1)} fusion(bf16[64,128,256]{2,1,0:T(8,128)(2,1)S(1)} %bitcast.98, s32[64]{0:T(128)S(1)} %get-tuple-element.15), kind=kOutput, calls=%fused_computation.14 | convolution fusion | flops 2168455168 | bytes 12583168 | tf_op jit(solution)/shard_map/kyx,kxX->kyX/dot_general | solution.py:92
  90.4 11.7 %copy.39 = bf16[8,8,128,512]{3,1,2,0:T(8,128)(2,1)} copy(bf16[8,8,128,512]{3,2,1,0:T(8,128)(2,1)} %bitcast.88) | data formatting | bytes 16777216
  102.1 7.9 %fusion.64 = f32[32,65536]{1,0:T(8,128)} fusion(bf16[64,65536]{1,0:T(8,128)(2,1)} %bitcast.84, s32[64]{0:T(128)S(1)} %get-tuple-element.14, s32[32]{0:T(128)S(1)} %fusion.75), kind=kOutput, calls=%fused_computation.57 | convolution fusion | flops 268437504 | bytes 16777600 | tf_op jit(solution)/shard_map/dot_general | solution.py:98
  110.0 0.1 copy.29
  110.1 0.8 scatter_custom_fusion
  110.9 1.1 copy.30
  112.0 10.7 %all-to-all-start.4 = ((f32[64,8,3]{1,2,0:T(4,128)}), f32[64,8,3]{1,2,0:T(4,128)S(1)}, u32[]{:S(2)}, u32[]{:S(2)}) async-start(f32[64,8,3]{1,2,0:T(4,128)} %copy.30), calls=%async_computation.4 | async-start | bytes 262144 | tf_op jit(solution)/shard_map/all_to_all | solution.py:119
  122.7 0.8 collective-permute-done
  123.5 7.1 %fusion = bf16[32,65536]{1,0:T(8,128)(2,1)S(1)} fusion(f32[32,65536]{1,0:T(8,128)} %collective-permute-done, bf16[64,65536]{1,0:T(8,128)(2,1)} %bitcast.85, s32[64]{0:T(128)S(1)} %get-tuple-element.14, s32[32]{0:T(128)S(1)} %fusion.76), kind=kOutput, calls=%fused_computation.2 | convolution fusion | flops 272631808 | bytes 20971904 | tf_op jit(solution)/shard_map/dot_general | solution.py:101
  130.6 3.5 %copy.40 = bf16[4,8,128,512]{3,2,1,0:T(8,128)(2,1)} copy(bf16[4,8,128,512]{3,1,2,0:T(8,128)(2,1)S(1)} %bitcast.86) | data formatting | bytes 8388608
  134.1 0.0 all-to-all-done.4
  134.1 10.2 %all-to-all-start.3 = ((bf16[32,128,512]{2,1,0:T(8,128)(2,1)}), bf16[32,128,512]{2,1,0:T(8,128)(2,1)}, u32[]{:S(2)}, u32[]{:S(2)}) async-start(bf16[32,128,512]{2,1,0:T(8,128)(2,1)} %bitcast.87), calls=%async_computation.3 | async-start | bytes 8388608 | tf_op jit(solution)/shard_map/all_to_all | solution.py:117
  144.3 0.1 all_to_all.30
  144.5 94.4 %all-to-all-done.3 = bf16[32,128,512]{2,1,0:T(8,128)(2,1)} async-done(((bf16[32,128,512]{2,1,0:T(8,128)(2,1)}), bf16[32,128,512]{2,1,0:T(8,128)(2,1)}, u32[]{:S(2)}, u32[]{:S(2)}) %all-to-all-start.3) | async-done | bytes 4194336 | tf_op jit(solution)/shard_map/all_to_all | solution.py:117
  238.8 2.8 %convert_reduce_fusion = f32[128,512]{1,0:T(8,128)S(1)} fusion(bf16[32,128,512]{2,1,0:T(8,128)(2,1)} %all-to-all-done.3), kind=kLoop, calls=%fused_computation.11 | loop fusion | flops 4128768 | bytes 4456448 | tf_op jit(solution)/shard_map/reduce_sum | solution.py:118
  241.6 1.6 fusion.43
  (24 shorter events, 0.1 us)
Async XLA Ops:
  6.5 34.3 %copy-start = (bf16[4,256,256]{2,1,0:T(8,128)(2,1)S(1)}, bf16[4,256,256]{2,1,0:T(8,128)(2,1)}, u32[]{:S(2)}) copy-start(bf16[4,256,256]{2,1,0:T(8,128)(2,1)} %param.8) | copy-start | bytes 1572868
  6.5 24.5 %copy-start.3 = (bf16[10,41]{1,0:T(8,128)(2,1)S(1)}, bf16[10,41]{1,0:T(8,128)(2,1)}, u32[]{:S(2)}) copy-start(bf16[10,41]{1,0:T(8,128)(2,1)} %param.15) | copy-start | bytes 2464
  8.7 9.5 %all-to-all-start = ((bf16[4,2,11]{2,1,0:T(2,128)(2,1)}), bf16[4,2,11]{2,1,0:T(2,128)(2,1)S(1)}, u32[]{:S(2)}, u32[]{:S(2)}) async-start(bf16[4,2,11]{2,1,0:T(2,128)(2,1)} %broadcast_in_dim.17), calls=%async_computation | async-start | bytes 4096 | tf_op jit(solution)/shard_map/all_to_all | solution.py:38
  13.0 27.4 %copy-start.4 = (s32[4]{0:T(128)S(1)}, s32[4]{0:T(128)}, u32[]{:S(2)}) copy-start(s32[4]{0:T(128)} %param.9) | copy-start | bytes 52
  18.8 21.5 %all-to-all-start.1 = ((bf16[64,8,11]{2,1,0:T(8,128)(2,1)}), bf16[64,8,11]{2,1,0:T(8,128)(2,1)S(1)}, u32[]{:S(2)}, u32[]{:S(2)}) async-start(bf16[64,8,11]{2,1,0:T(8,128)(2,1)} %broadcast_in_dim.19), calls=%async_computation.1 | async-start | bytes 262144 | tf_op jit(solution)/shard_map/all_to_all | solution.py:41
  30.9 46.1 %all-gather.2.cloned.1.call-start = ((), (), s32[]{:S(2)}) async-start(), calls=%async_computation.5 | async-start | bytes 2621440 | tf_op jit(solution)/shard_map/all_gather | solution.py:76
  34.2 14.5 %copy-start.1 = (s32[4,4,2]{1,2,0:T(2,128)S(1)}, s32[4,4,2]{1,2,0:T(2,128)}, u32[]{:S(2)}) copy-start(s32[4,4,2]{1,2,0:T(2,128)} %param.11) | copy-start | bytes 388
  34.2 14.7 %copy-start.2 = (s32[4,4]{1,0:T(4,128)S(1)}, s32[4,4]{1,0:T(4,128)}, u32[]{:S(2)}) copy-start(s32[4,4]{1,0:T(4,128)} %param.10) | copy-start | bytes 196
  49.8 8.5 %all-to-all-start.2 = ((f32[4,16,4]{1,2,0:T(4,128)}), f32[4,16,4]{1,2,0:T(4,128)S(1)}, u32[]{:S(2)}, u32[]{:S(2)}) async-start(f32[4,16,4]{1,2,0:T(4,128)} %broadcast_in_dim.21), calls=%async_computation.2 | async-start | bytes 16384 | tf_op jit(solution)/shard_map/all_to_all | solution.py:75
  110.0 13.5 %collective-permute-start = (f32[32,65536]{1,0:T(8,128)}, f32[32,65536]{1,0:T(8,128)}, u32[]{:S(2)}, u32[]{:S(2)}) collective-permute-start(f32[32,65536]{1,0:T(8,128)} %fusion.64), channel_id=1, source_target_pairs={{0,4},{4,0},{1,5},{5,1},{2,6},{6,2},{3,7},{7,3},{8,12},{12,8},{9,1... | collective-permute-start | bytes 25165832 | tf_op jit(solution)/shard_map/ppermute | solution.py:99
  112.0 22.0 %all-to-all-start.4 = ((f32[64,8,3]{1,2,0:T(4,128)}), f32[64,8,3]{1,2,0:T(4,128)S(1)}, u32[]{:S(2)}, u32[]{:S(2)}) async-start(f32[64,8,3]{1,2,0:T(4,128)} %copy.30), calls=%async_computation.4 | async-start | bytes 262144 | tf_op jit(solution)/shard_map/all_to_all | solution.py:119
  134.1 104.8 %all-to-all-start.3 = ((bf16[32,128,512]{2,1,0:T(8,128)(2,1)}), bf16[32,128,512]{2,1,0:T(8,128)(2,1)}, u32[]{:S(2)}, u32[]{:S(2)}) async-start(bf16[32,128,512]{2,1,0:T(8,128)(2,1)} %bitcast.87), calls=%async_computation.3 | async-start | bytes 8388608 | tf_op jit(solution)/shard_map/all_to_all | solution.py:117
Sparse Core Ops, SparseCore 0:
  48.9 28.1 all-gather.1

commit v9 on v8

--- a/solution.py
+++ b/solution.py
@@ -33,13 +33,27 @@
     h = lax.axis_index("ec")
     n_halves = lax.axis_size("ec")
 
-    packed = jnp.concatenate([coeffs, inv_var[:, None]], axis=1)
-    packed = jnp.broadcast_to(packed[None], (n_bands,) + packed.shape)
-    packed = lax.all_to_all(packed, "grp", split_axis=0, concat_axis=0, tiled=True)
-    packed = packed.reshape(1, -1, terms + 1)
-    packed = jnp.broadcast_to(packed, (n_owners,) + packed.shape[1:])
-    packed = lax.all_to_all(packed, EXP, split_axis=0, concat_axis=0, tiled=True)
-    packed = packed.reshape(-1, terms + 1)
+    n_dev = n_owners * n_bands
+    packed = jnp.concatenate([coeffs, inv_var[:, None]], axis=1).astype(jnp.float32)
+    own_entries = jnp.stack(
+        [
+            tile_patch,
+            tile_offset[:, :, 0],
+            tile_offset[:, :, 1],
+            jnp.broadcast_to(tile_exposure[:, None], (tile_count, listed)),
+        ],
+        axis=-1,
+    ).astype(jnp.float32)
+    payload = jnp.concatenate([packed.reshape(-1), own_entries.reshape(-1)])
+    width = payload.shape[0]
+    payload = jnp.broadcast_to(payload[None], (n_bands, width))
+    payload = lax.all_to_all(payload, "grp", split_axis=0, concat_axis=0, tiled=True)
+    payload = jnp.broadcast_to(payload.reshape(1, 1, n_bands * width), (n_owners, 1, n_bands * width))
+    payload = lax.all_to_all(payload, EXP, split_axis=0, concat_axis=0, tiled=True)
+    payload = payload.reshape(n_dev, width)
+    per_dev_coef = packed.size
+    packed = payload[:, :per_dev_coef].reshape(-1, terms + 1).astype(jnp.bfloat16)
+    all_entries = payload[:, per_dev_coef:].reshape(n_dev * tile_count * listed, 4)
 
     vband = band_matrix(vert_taps, tile_side)
     hband = band_matrix(horiz_taps, tile_side)
@@ -60,19 +74,9 @@
     )
     weighted = (weight_tile[:, None, None] * smoothed).astype(jnp.bfloat16)
 
-    row_off = tile_offset[:, :, 0]
-    col_off = tile_offset[:, :, 1]
-    meta = jnp.stack(
-        [
-            tile_patch.astype(jnp.float32),
-            row_off.astype(jnp.float32),
-            col_off.astype(jnp.float32),
-            jnp.broadcast_to(weight_tile[:, None], (tile_count, listed)),
-        ],
-        axis=-1,
-    ).reshape(tile_count * listed, 4)
-    meta_send = jnp.broadcast_to(meta[None], (n_bands,) + meta.shape).reshape(-1, 4)
-    got_meta = lax.all_to_all(meta_send, "grp", split_axis=0, concat_axis=0, tiled=True)
+    e = lax.axis_index(EXP)
+    row_entries = n_bands * tile_count * listed
+    got_meta = lax.dynamic_slice_in_dim(all_entries, e * row_entries, row_entries, axis=0)
     row_tiles = lax.all_gather(weighted, "grp", axis=0, tiled=True)
     entries = got_meta.shape[0]
     sources = row_tiles.shape[0]
@@ -100,27 +104,17 @@
     keep_of = (got_patch[None, :] == chip_patch + h).astype(jnp.bfloat16)
     keep = jnp.dot(keep_of, flat_shifted, preferred_element_type=jnp.float32)
 
-    per_owner = n_bands * 2
-    onehot = (got_patch[:, None] == jnp.arange(n_owners, dtype=jnp.int32)[None, :]).astype(
-        jnp.int32
-    )
-    before = jnp.cumsum(onehot, axis=0) - onehot
-    rank = jnp.sum(before * onehot, axis=1)
-    target = got_patch * per_owner + rank
-    meta_slots = (
-        jnp.zeros((n_owners * per_owner, 3), jnp.float32)
-        .at[target]
-        .set(got_meta[:, 1:], mode="drop")
-    )
-
     pair = (keep + got_give).reshape(chips, band_rows, PS)
     recv_bands = lax.all_to_all(pair.astype(jnp.bfloat16), CHIP, split_axis=0, concat_axis=0, tiled=True)
     flux = jnp.sum(recv_bands.astype(jnp.float32), axis=0)
-    recv_meta = lax.all_to_all(meta_slots, EXP, split_axis=0, concat_axis=0, tiled=True)
-
-    rows = recv_meta[:, 0].astype(jnp.int32)
-    cols = recv_meta[:, 1].astype(jnp.int32)
-    wts = recv_meta[:, 2]
+    rows = all_entries[:, 1].astype(jnp.int32)
+    cols = all_entries[:, 2].astype(jnp.int32)
+    entry_exposure = all_entries[:, 3].astype(jnp.int32)
+    exposure_pick = (
+        entry_exposure[:, None] == jnp.arange(exposures, dtype=jnp.int32)[None, :]
+    ).astype(jnp.bfloat16)
+    wts = jnp.dot(exposure_pick, packed[:, terms], preferred_element_type=jnp.float32)
+    wts = jnp.where(all_entries[:, 0].astype(jnp.int32) == e, wts, 0.0)
     y_index = g * band_rows + jnp.arange(band_rows, dtype=jnp.int32)
     x_index = jnp.arange(PS, dtype=jnp.int32)
     row_mask = (
@@ -129,7 +123,12 @@
     col_mask = (
         (x_index[None, :] >= cols[:, None]) & (x_index[None, :] < cols[:, None] + tile_side)
     ).astype(jnp.float32)
-    cover = jnp.einsum("my,mx->yx", row_mask, col_mask, precision=lax.Precision.HIGHEST)
+    cover = jnp.einsum(
+        "my,mx->yx",
+        row_mask.astype(jnp.bfloat16),
+        col_mask.astype(jnp.bfloat16),
+        preferred_element_type=jnp.float32,
+    )
     coadd = flux / jnp.maximum(cover, 1.0)
     return coadd[None]
 

time: 251 us -> 252 us (level); the launches traced: 250 us -> 248 us
  starting transfers between devices: 40.8 us -> 27.2 us
  waiting for transfers between devices: 127 us -> 135 us
  other arithmetic: 3.99 us -> 10.5 us
  matrix products: 42.8 us -> 39.1 us
    all_to_all x4 -> x2, starting transfers between devices: 30.5 us -> 16.4 us  [the longest x1 12.1 us: per_device(): lax.all_to_all(payload, EXP, split_axis=0, concat_axis=0, tiled=True)]
    ppermute x1, waiting for transfers between devices: 0.8 us -> 13.1 us  [per_device(): got_give = lax.ppermute(give, 'ec', perm=[(0, 1), (1, 0)])]
    all_gather x1, waiting for transfers between devices: 18.1 us -> 26.2 us  [per_device(): row_tiles = lax.all_gather(weighted, 'grp', axis=0, tiled=True)]
    all_to_all x1, waiting for transfers between devices: 94.4 us -> 87.4 us  [per_device(): lax.all_to_all(pair.astype(jnp.bfloat16), CHIP, split_axis=0, concat_axis...]
    dot_general x1, matrix products: 7.09 us -> 1.33 us  [per_device(): keep = jnp.dot(keep_of, flat_shifted, preferred_element_type=jnp.float32)]
    convert_element_type x4 -> x3, other arithmetic: 0.11 us -> 5.85 us  [the longest x1 4.41 us: per_device(): rows = all_entries[:, 1].astype(jnp.int32)]
    all_to_all x4 -> x2, waiting for transfers between devices: 13.7 us -> 8.29 us  [the longest x1 5.72 us: per_device(): lax.all_to_all(payload, EXP, split_axis=0, concat_axis=0, tiled=True)]
    dot_general x1 -> x2, matrix products: 1.57 us -> 6.47 us  [the longest x1 4.67 us: per_device(): jnp.einsum('my,mx->yx', row_mask.astype(jnp.bfloat16), col_mask.astype(jn...]
  transfers between devices with their start and end apart: 7 -> 5, of which waited for: 6 -> 5; matrix products, arithmetic and copies ran while one was open for 8% -> 6% of each run, Pallas kernels for 0% -> 0%
where the time goes in v9:
time: 252 us; the launch traced here: 248 us
  waiting for transfers between devices  135 us (54%)
  matrix products  39.1 us (16%)
  starting transfers between devices  27.2 us (11%)
  local copies, waits for them, and re-layouts  21.9 us (9%)
  between operations  14 us (6%)
  other arithmetic  10.5 us (4%)
    all_to_all x1, waiting for transfers between devices, per_device(): lax.all_to_all(pair.astype(jnp.bfloat16), CHIP, split_axis=0, concat_axis...  87.4 us
    all_gather x1, waiting for transfers between devices, per_device(): row_tiles = lax.all_gather(weighted, 'grp', axis=0, tiled=True)  26.2 us
    unnamed x12, local copies, waits for them, and re-layouts  15.2 us
    ppermute x1, waiting for transfers between devices, per_device(): got_give = lax.ppermute(give, 'ec', perm=[(0, 1), (1, 0)])  13.1 us
    all_to_all x1, starting transfers between devices, per_device(): lax.all_to_all(payload, EXP, split_axis=0, concat_axis=0, tiled=True)  12.1 us
    dot_general x1, matrix products, per_device(): jnp.einsum('kyx,kxX->kyX', got_slabs, shifter, preferred_element_type=jnp...  10.3 us
    all_to_all x1, starting transfers between devices, per_device(): lax.all_to_all(pair.astype(jnp.bfloat16), CHIP, split_axis=0, concat_axis...  10.2 us
    dot_general x1, matrix products, per_device(): jnp.einsum('byk,tkbx->tyx', vband, partial_value, preferred_element_type=...  6.9 us
  transfers between devices with their start and end apart: 5, of which 5 were waited for; matrix products, arithmetic and copies ran while one was open for 6% of the time, Pallas kernels for 0%

profile of v9, /device:TPU:8, one launch (start us, length us, event | category | flops | bytes accessed | tf_op | source)
XLA Modules:
  0.0 247.7 jit_solution(12213420991408779540)
XLA Ops:
  6.5 0.8 copy.25
  7.4 0.7 maximum_convert_fusion
  8.1 0.1 reshape.79
  8.2 0.7 stack_broadcast_in_dim.2
  8.9 0.7 add_convert_fusion
  9.6 0.1 copy.27
  9.7 0.1 convert_element_type.123
  9.9 0.6 broadcast_in_dim.14
  10.5 4.3 %all-to-all-start = ((f32[4,1,86]{2,1,0:T(1,128)}), f32[4,1,86]{2,1,0:T(1,128)S(1)}, u32[]{:S(2)}, u32[]{:S(2)}) async-start(f32[4,1,86]{2,1,0:T(1,128)} %broadcast_in_dim.14), calls=%async_computation | async-start | bytes 4096 | tf_op jit(solution)/shard_map/all_to_all | solution.py:50
  14.8 2.6 %convert_bitcast_fusion = bf16[10,256,256,1]{2,0,1,3:T(8,128)(2,1)S(1)} fusion(bf16[10,41]{1,0:T(8,128)(2,1)} %param.14), kind=kOutput, calls=%fused_computation.40 | convolution fusion | flops 62455808 | bytes 1311540 | tf_op jit(solution)/shard_map/bd,dij->bij/dot_general | solution.py:19
  17.4 2.6 %all-to-all-done = f32[4,1,86]{2,1,0:T(1,128)S(1)} async-done(((f32[4,1,86]{2,1,0:T(1,128)}), f32[4,1,86]{2,1,0:T(1,128)S(1)}, u32[]{:S(2)}, u32[]{:S(2)}) %all-to-all-start) | async-done | bytes 1408 | tf_op jit(solution)/shard_map/all_to_all | solution.py:50
  19.9 0.5 broadcast.86
  20.5 0.7 reduce.26
  21.1 0.1 broadcast_in_dim.15
  21.2 0.7 broadcast_in_dim.16
  21.9 12.1 %all-to-all-start.1 = ((f32[64,1,344]{2,1,0:T(1,128)}), f32[64,1,344]{2,1,0:T(1,128)S(1)}, u32[]{:S(2)}, u32[]{:S(2)}) async-start(f32[64,1,344]{2,1,0:T(1,128)} %broadcast_in_dim.16), calls=%async_computation.1 | async-start | bytes 196608 | tf_op jit(solution)/shard_map/all_to_all | solution.py:52
  34.0 0.2 all-gather.2.cloned.1.call-start
  34.3 3.3 %convert_bitcast_fusion.1 = bf16[10,256,256,1]{2,0,1,3:T(8,128)(2,1)} fusion(bf16[10,41]{1,0:T(8,128)(2,1)S(1)} %copy-done.2), kind=kOutput, calls=%fused_computation.41 | convolution fusion | flops 62455808 | bytes 1311540 | tf_op jit(solution)/shard_map/bd,dij->bij/dot_general | solution.py:19
  37.5 5.7 %all-to-all-done.1 = f32[64,1,344]{2,1,0:T(1,128)S(1)} async-done(((f32[64,1,344]{2,1,0:T(1,128)}), f32[64,1,344]{2,1,0:T(1,128)S(1)}, u32[]{:S(2)}, u32[]{:S(2)}) %all-to-all-start.1) | async-done | bytes 88096 | tf_op jit(solution)/shard_map/all_to_all | solution.py:52
  43.2 0.2 reduce.1
  43.5 0.1 reshape.75
  43.6 0.1 convert_element_type.128
  43.7 0.2 fusion.71
  43.9 0.2 slice_reduce_fusion.1
  44.1 0.1 copy.29
  44.2 6.9 %fusion.44 = bf16[4,256,256]{1,2,0:T(8,128)(2,1)S(1)} fusion(bf16[10,256,256,1]{2,0,1,3:T(8,128)(2,1)S(1)} %convert_bitcast_fusion, f32[4,10]{0,1:T(8,128)S(1)} %copy.29, bf16[10,256,256,1]{2,0,1,3:T(8,128)(2,1)} %convert_bitcast_fusion.1, bf16[4,256,256]{2,1,0:T(8,128)(2,1)S(1)} %copy-done, f32[4]{0:T(128)S(1)} %slice_reduce_fusion.1), kind=kOutput, calls=%fused_computation.50 | convolution fusion | flops 2690121728 | bytes 3670192 | tf_op jit(solution)/shard_map/byk,tkbx->tyx/dot_general | solution.py:72
  51.1 1.0 copy.31
  52.1 0.1 slice.52
  52.2 1.1 reshape.76
  53.4 0.2 fusion.63
  53.6 0.1 convert_element_type.127
  53.7 26.2 %all-gather.2.cloned.1.call-done = bf16[16,256,256]{2,1,0:T(8,128)(2,1)} async-done(((bf16[4,256,256]{2,1,0:T(8,128)(2,1)}), bf16[16,256,256]{2,1,0:T(8,128)(2,1)}) %all-gather.2.cloned.1.call-update) | async-done | bytes 2097168 | tf_op jit(solution)/shard_map/all_gather | solution.py:80
  79.9 3.2 %fusion.21 = bf16[16,4,128,256]{3,2,1,0:T(8,128)(2,1)S(1)} fusion(s32[16,4]{1,0:T(8,128)S(1)} %convert_element_type.127, s32[128]{0:T(128)S(1)} %iota_add_fusion, bf16[16,256,256]{2,1,0:T(8,128)(2,1)} %all-gather.2.cloned.1.call-done), kind=kOutput, calls=%fused_computation.29 | convolution fusion | flops 1080033280 | bytes 6292224 | tf_op jit(solution)/shard_map/sjiy,syx->sjix/dot_general | solution.py:89
  83.1 10.3 %fusion.9 = bf16[64,128,512]{2,1,0:T(8,128)(2,1)} fusion(bf16[64,128,256]{2,1,0:T(8,128)(2,1)S(1)} %bitcast.75, s32[64]{0:T(128)S(1)} %get-tuple-element.12), kind=kOutput, calls=%fused_computation.19 | convolution fusion | flops 2168455168 | bytes 12583168 | tf_op jit(solution)/shard_map/kyx,kxX->kyX/dot_general | solution.py:96
  93.4 11.7 %copy.39 = bf16[8,8,128,512]{3,1,2,0:T(8,128)(2,1)} copy(bf16[8,8,128,512]{3,2,1,0:T(8,128)(2,1)} %bitcast.70) | data formatting | bytes 16777216
  105.2 4.8 %fusion.64 = f32[32,65536]{1,0:T(8,128)S(1)} fusion(bf16[64,65536]{1,0:T(8,128)(2,1)} %bitcast.64, s32[64]{0:T(128)S(1)} %get-tuple-element.10, s32[32]{0:T(128)S(1)} %fusion.75), kind=kOutput, calls=%fused_computation.68 | convolution fusion | flops 268437504 | bytes 16777600 | tf_op jit(solution)/shard_map/dot_general | solution.py:102
  110.0 0.3 collective-permute-start
  110.4 13.1 %collective-permute-done = f32[32,65536]{1,0:T(8,128)S(1)} collective-permute-done((f32[32,65536]{1,0:T(8,128)S(1)}, f32[32,65536]{1,0:T(8,128)S(1)}, u32[]{:S(2)}, u32[]{:S(2)}) %collective-permute-start) | collective-permute-done | bytes 8388640 | tf_op jit(solution)/shard_map/ppermute | solution.py:103
  123.5 1.3 fusion
  124.8 3.5 %copy.40 = bf16[4,8,128,512]{3,2,1,0:T(8,128)(2,1)} copy(bf16[4,8,128,512]{3,1,2,0:T(8,128)(2,1)S(1)} %bitcast.68) | data formatting | bytes 8388608
  128.3 10.2 %all-to-all-start.2 = ((bf16[32,128,512]{2,1,0:T(8,128)(2,1)}), bf16[32,128,512]{2,1,0:T(8,128)(2,1)}, u32[]{:S(2)}, u32[]{:S(2)}) async-start(bf16[32,128,512]{2,1,0:T(8,128)(2,1)} %bitcast.69), calls=%async_computation.2 | async-start | bytes 8388608 | tf_op jit(solution)/shard_map/all_to_all | solution.py:108
  138.6 0.2 slice_reduce_fusion
  138.8 0.6 fusion.25
  139.4 4.4 %fusion.26 = (s32[4096]{0:T(1024)S(1)}, s32[4096]{0:T(1024)S(1)}, s32[4096]{0:T(1024)S(1)}, s32[4096]{0:T(1024)S(1)}, s32[4096]{0:T(1024)S(1)}) fusion(f32[4096,4]{1,0:T(8,128)S(1)} %reshape.76), kind=kLoop, calls=%fused_computation.43 | loop fusion | flops 20480 | bytes 131072 | tf_op jit(solution)/shard_map/convert_element_type | solution.py:110
  143.8 1.8 fusion.8
  145.6 87.4 %all-to-all-done.2 = bf16[32,128,512]{2,1,0:T(8,128)(2,1)} async-done(((bf16[32,128,512]{2,1,0:T(8,128)(2,1)}), bf16[32,128,512]{2,1,0:T(8,128)(2,1)}, u32[]{:S(2)}, u32[]{:S(2)}) %all-to-all-start.2) | async-done | bytes 4194336 | tf_op jit(solution)/shard_map/all_to_all | solution.py:108
  233.0 2.8 %convert_reduce_fusion = f32[128,512]{1,0:T(8,128)S(1)} fusion(bf16[32,128,512]{2,1,0:T(8,128)(2,1)} %all-to-all-done.2), kind=kLoop, calls=%fused_computation.14 | loop fusion | flops 4128768 | bytes 4456448 | tf_op jit(solution)/shard_map/reduce_sum | solution.py:109
  235.8 4.7 %fusion.53 = f32[1,128,512]{2,1,0:T(8,128)} fusion(f32[128,512]{1,0:T(8,128)S(1)} %convert_reduce_fusion, s32[4096]{0:T(1024)S(1)} %get-tuple-element.6, s32[4096]{0:T(1024)S(1)} %get-tuple-element.8, bf16[4096]{0:T(1024)(128)(2,1)S(1)} %broadcast_select_fusion, s32[128]{0:T(128)S(1)} %iota_add_fusion, s32[4096]{0:T(1024)S(1)} %get-tuple-element.7, ...), kind=kOutput, calls=%fused_computation.53 | convolution fusion | flops 549584896 | bytes 598528 | tf_op jit(solution)/shard_map/my,mx->yx/dot_general | solution.py:126
  (19 shorter events, 0.2 us)
Async XLA Ops:
  6.5 37.6 %copy-start = (bf16[4,256,256]{2,1,0:T(8,128)(2,1)S(1)}, bf16[4,256,256]{2,1,0:T(8,128)(2,1)}, u32[]{:S(2)}) copy-start(bf16[4,256,256]{2,1,0:T(8,128)(2,1)} %param.8) | copy-start | bytes 1572868
  10.5 9.5 %all-to-all-start = ((f32[4,1,86]{2,1,0:T(1,128)}), f32[4,1,86]{2,1,0:T(1,128)S(1)}, u32[]{:S(2)}, u32[]{:S(2)}) async-start(f32[4,1,86]{2,1,0:T(1,128)} %broadcast_in_dim.14), calls=%async_computation | async-start | bytes 4096 | tf_op jit(solution)/shard_map/all_to_all | solution.py:50
  14.8 19.5 %copy-start.2 = (bf16[10,41]{1,0:T(8,128)(2,1)S(1)}, bf16[10,41]{1,0:T(8,128)(2,1)}, u32[]{:S(2)}) copy-start(bf16[10,41]{1,0:T(8,128)(2,1)} %param.15) | copy-start | bytes 2464
  21.9 21.3 %all-to-all-start.1 = ((f32[64,1,344]{2,1,0:T(1,128)}), f32[64,1,344]{2,1,0:T(1,128)S(1)}, u32[]{:S(2)}, u32[]{:S(2)}) async-start(f32[64,1,344]{2,1,0:T(1,128)} %broadcast_in_dim.16), calls=%async_computation.1 | async-start | bytes 196608 | tf_op jit(solution)/shard_map/all_to_all | solution.py:52
  34.0 9.7 %copy-start.1 = (s32[4]{0:T(128)S(1)}, s32[4]{0:T(128)}, u32[]{:S(2)}) copy-start(s32[4]{0:T(128)} %param.9) | copy-start | bytes 52
  34.0 45.8 %all-gather.2.cloned.1.call-start = ((), (), s32[]{:S(2)}) async-start(), calls=%async_computation.3 | async-start | bytes 2621440 | tf_op jit(solution)/shard_map/all_gather | solution.py:80
  105.2 18.3 %slice-start = ((s8[8388608]{0:T(1024)(128)(4,1)}), s8[4194304]{0:T(1024)(128)(4,1)S(1)}, s32[]{:S(2)}) async-start(s8[8388608]{0:T(1024)(128)(4,1)} %bitcast.65), calls=%async_computation.4 | async-start | bytes 8388608
  105.2 18.3 %slice-start.1 = ((s8[8388608]{0:T(1024)(128)(4,1)}), s8[4194304]{0:T(1024)(128)(4,1)S(1)}, s32[]{:S(2)}) async-start(s8[8388608]{0:T(1024)(128)(4,1)} %bitcast.65), calls=%async_computation.5 | async-start | bytes 8388608
  110.0 13.5 %collective-permute-start = (f32[32,65536]{1,0:T(8,128)S(1)}, f32[32,65536]{1,0:T(8,128)S(1)}, u32[]{:S(2)}, u32[]{:S(2)}) collective-permute-start(f32[32,65536]{1,0:T(8,128)S(1)} %fusion.64), channel_id=1, source_target_pairs={{0,4},{4,0},{1,5},{5,1},{2,6},{6,2},{3,7},{7,3},{8,12},{12,8},{9,1... | collective-permute-start | bytes 25165832 | tf_op jit(solution)/shard_map/ppermute | solution.py:103
  128.3 104.7 %all-to-all-start.2 = ((bf16[32,128,512]{2,1,0:T(8,128)(2,1)}), bf16[32,128,512]{2,1,0:T(8,128)(2,1)}, u32[]{:S(2)}, u32[]{:S(2)}) async-start(bf16[32,128,512]{2,1,0:T(8,128)(2,1)} %bitcast.69), calls=%async_computation.2 | async-start | bytes 8388608 | tf_op jit(solution)/shard_map/all_to_all | solution.py:108
Sparse Core Ops, SparseCore 0:
  52.2 27.5 all-gather.1

commit v10 on v9

--- a/solution.py
+++ b/solution.py
@@ -100,11 +100,11 @@
     flat_shifted = shifted.reshape(entries, band_rows * PS)
     give_of = (got_patch[None, :] == chip_patch + (1 - h)).astype(jnp.bfloat16)
     give = jnp.dot(give_of, flat_shifted, preferred_element_type=jnp.float32)
-    got_give = lax.ppermute(give, "ec", perm=[(0, 1), (1, 0)])
+    got_give = lax.ppermute(give.astype(jnp.bfloat16), "ec", perm=[(0, 1), (1, 0)])
     keep_of = (got_patch[None, :] == chip_patch + h).astype(jnp.bfloat16)
     keep = jnp.dot(keep_of, flat_shifted, preferred_element_type=jnp.float32)
 
-    pair = (keep + got_give).reshape(chips, band_rows, PS)
+    pair = (keep + got_give.astype(jnp.float32)).reshape(chips, band_rows, PS)
     recv_bands = lax.all_to_all(pair.astype(jnp.bfloat16), CHIP, split_axis=0, concat_axis=0, tiled=True)
     flux = jnp.sum(recv_bands.astype(jnp.float32), axis=0)
     rows = all_entries[:, 1].astype(jnp.int32)
@@ -129,6 +129,7 @@
         col_mask.astype(jnp.bfloat16),
         preferred_element_type=jnp.float32,
     )
+    cover = lax.optimization_barrier(cover)
     coadd = flux / jnp.maximum(cover, 1.0)
     return coadd[None]
 

time: 252 us -> 242 us (0.960)
  waiting for transfers between devices: 135 us -> 125 us
    ppermute x1, waiting for transfers between devices: 13.1 us -> 7.13 us  [per_device(): lax.ppermute(give.astype(jnp.bfloat16), 'ec', perm=[(0, 1), (1, 0)])]
    all_to_all x1, waiting for transfers between devices: 87.4 us -> 83.5 us  [per_device(): lax.all_to_all(pair.astype(jnp.bfloat16), CHIP, split_axis=0, concat_axis...]
    unnamed x12 -> x10, local copies, waits for them, and re-layouts: 15.2 us -> 15.3 us
  transfers between devices with their start and end apart: 5 -> 5, of which waited for: 5 -> 5; matrix products, arithmetic and copies ran while one was open for 6% -> 8% of each run, Pallas kernels for 0% -> 0%
where the time goes in v10:
time: 242 us; the launch traced here: 238 us
  waiting for transfers between devices  125 us (52%)
  matrix products  38.3 us (16%)
  starting transfers between devices  27.2 us (11%)
  local copies, waits for them, and re-layouts  22 us (9%)
  between operations  14 us (6%)
  other arithmetic  11.2 us (5%)
    all_to_all x1, waiting for transfers between devices, per_device(): lax.all_to_all(pair.astype(jnp.bfloat16), CHIP, split_axis=0, concat_axis...  83.5 us
    all_gather x1, waiting for transfers between devices, per_device(): row_tiles = lax.all_gather(weighted, 'grp', axis=0, tiled=True)  26.2 us
    unnamed x10, local copies, waits for them, and re-layouts  15.3 us
    all_to_all x1, starting transfers between devices, per_device(): lax.all_to_all(payload, EXP, split_axis=0, concat_axis=0, tiled=True)  12.1 us
    dot_general x1, matrix products, per_device(): jnp.einsum('kyx,kxX->kyX', got_slabs, shifter, preferred_element_type=jnp...  10.3 us
    all_to_all x1, starting transfers between devices, per_device(): lax.all_to_all(pair.astype(jnp.bfloat16), CHIP, split_axis=0, concat_axis...  10.2 us
    ppermute x1, waiting for transfers between devices, per_device(): lax.ppermute(give.astype(jnp.bfloat16), 'ec', perm=[(0, 1), (1, 0)])  7.13 us
    dot_general x1, matrix products, per_device(): jnp.einsum('byk,tkbx->tyx', vband, partial_value, preferred_element_type=...  6.9 us
  transfers between devices with their start and end apart: 5, of which 5 were waited for; matrix products, arithmetic and copies ran while one was open for 8% of the time, Pallas kernels for 0%

profile of v10, /device:TPU:8, one launch (start us, length us, event | category | flops | bytes accessed | tf_op | source)
XLA Modules:
  0.0 238.0 jit_solution(3451372265202907743)
XLA Ops:
  6.5 0.8 copy.25
  7.4 0.7 maximum_convert_fusion
  8.1 0.1 reshape.79
  8.2 0.7 stack_broadcast_in_dim.2
  8.9 0.7 add_convert_fusion.1
  9.6 0.1 copy.27
  9.7 0.1 convert_element_type.129
  9.9 0.6 broadcast_in_dim.14
  10.5 4.3 %all-to-all-start = ((f32[4,1,86]{2,1,0:T(1,128)}), f32[4,1,86]{2,1,0:T(1,128)S(1)}, u32[]{:S(2)}, u32[]{:S(2)}) async-start(f32[4,1,86]{2,1,0:T(1,128)} %broadcast_in_dim.14), calls=%async_computation | async-start | bytes 4096 | tf_op jit(solution)/shard_map/all_to_all | solution.py:50
  14.8 2.6 %convert_bitcast_fusion = bf16[10,256,256,1]{2,0,1,3:T(8,128)(2,1)S(1)} fusion(bf16[10,41]{1,0:T(8,128)(2,1)} %param.14), kind=kOutput, calls=%fused_computation.40 | convolution fusion | flops 62455808 | bytes 1311540 | tf_op jit(solution)/shard_map/bd,dij->bij/dot_general | solution.py:19
  17.4 2.6 %all-to-all-done = f32[4,1,86]{2,1,0:T(1,128)S(1)} async-done(((f32[4,1,86]{2,1,0:T(1,128)}), f32[4,1,86]{2,1,0:T(1,128)S(1)}, u32[]{:S(2)}, u32[]{:S(2)}) %all-to-all-start) | async-done | bytes 1408 | tf_op jit(solution)/shard_map/all_to_all | solution.py:50
  19.9 0.5 broadcast.86
  20.5 0.7 reduce.26
  21.1 0.1 broadcast_in_dim.15
  21.2 0.7 broadcast_in_dim.16
  21.9 12.1 %all-to-all-start.1 = ((f32[64,1,344]{2,1,0:T(1,128)}), f32[64,1,344]{2,1,0:T(1,128)S(1)}, u32[]{:S(2)}, u32[]{:S(2)}) async-start(f32[64,1,344]{2,1,0:T(1,128)} %broadcast_in_dim.16), calls=%async_computation.1 | async-start | bytes 196608 | tf_op jit(solution)/shard_map/all_to_all | solution.py:52
  34.0 0.2 all-gather.2.cloned.1.call-start
  34.3 3.3 %convert_bitcast_fusion.1 = bf16[10,256,256,1]{2,0,1,3:T(8,128)(2,1)} fusion(bf16[10,41]{1,0:T(8,128)(2,1)S(1)} %copy-done.3), kind=kOutput, calls=%fused_computation.41 | convolution fusion | flops 62455808 | bytes 1311540 | tf_op jit(solution)/shard_map/bd,dij->bij/dot_general | solution.py:19
  37.5 5.7 %all-to-all-done.1 = f32[64,1,344]{2,1,0:T(1,128)S(1)} async-done(((f32[64,1,344]{2,1,0:T(1,128)}), f32[64,1,344]{2,1,0:T(1,128)S(1)}, u32[]{:S(2)}, u32[]{:S(2)}) %all-to-all-start.1) | async-done | bytes 88096 | tf_op jit(solution)/shard_map/all_to_all | solution.py:52
  43.2 0.2 reduce.1
  43.5 0.1 reshape.75
  43.6 0.1 convert_element_type.134
  43.7 0.2 fusion.69
  43.9 0.2 slice_reduce_fusion.1
  44.1 0.1 copy.29
  44.2 6.9 %fusion.43 = bf16[4,256,256]{1,2,0:T(8,128)(2,1)S(1)} fusion(bf16[10,256,256,1]{2,0,1,3:T(8,128)(2,1)S(1)} %convert_bitcast_fusion, f32[4,10]{0,1:T(8,128)S(1)} %copy.29, bf16[10,256,256,1]{2,0,1,3:T(8,128)(2,1)} %convert_bitcast_fusion.1, bf16[4,256,256]{2,1,0:T(8,128)(2,1)S(1)} %copy-done, f32[4]{0:T(128)S(1)} %slice_reduce_fusion.1), kind=kOutput, calls=%fused_computation.50 | convolution fusion | flops 2690121728 | bytes 3670192 | tf_op jit(solution)/shard_map/byk,tkbx->tyx/dot_general | solution.py:72
  51.1 1.0 copy.31
  52.1 0.1 slice.52
  52.2 1.1 reshape.76
  53.4 0.2 fusion.59
  53.7 26.2 %all-gather.2.cloned.1.call-done = bf16[16,256,256]{2,1,0:T(8,128)(2,1)} async-done(((bf16[4,256,256]{2,1,0:T(8,128)(2,1)}), bf16[16,256,256]{2,1,0:T(8,128)(2,1)}) %all-gather.2.cloned.1.call-update) | async-done | bytes 2097168 | tf_op jit(solution)/shard_map/all_gather | solution.py:80
  79.9 3.2 %fusion.20 = bf16[16,4,128,256]{3,2,1,0:T(8,128)(2,1)S(1)} fusion(s32[16,4]{1,0:T(8,128)S(1)} %convert_element_type.133, s32[128]{0:T(128)S(1)} %iota_add_fusion, bf16[16,256,256]{2,1,0:T(8,128)(2,1)} %all-gather.2.cloned.1.call-done), kind=kOutput, calls=%fused_computation.29 | convolution fusion | flops 1080033280 | bytes 6292224 | tf_op jit(solution)/shard_map/sjiy,syx->sjix/dot_general | solution.py:89
  83.1 10.3 %fusion.8 = bf16[64,128,512]{2,1,0:T(8,128)(2,1)} fusion(bf16[64,128,256]{2,1,0:T(8,128)(2,1)S(1)} %bitcast.73, s32[64]{0:T(128)S(1)} %get-tuple-element.12), kind=kOutput, calls=%fused_computation.19 | convolution fusion | flops 2168455168 | bytes 12583168 | tf_op jit(solution)/shard_map/kyx,kxX->kyX/dot_general | solution.py:96
  93.4 11.7 %copy.39 = bf16[8,8,128,512]{3,1,2,0:T(8,128)(2,1)} copy(bf16[8,8,128,512]{3,2,1,0:T(8,128)(2,1)} %bitcast.68) | data formatting | bytes 16777216
  105.2 4.8 %convolution_convert_fusion = bf16[32,65536]{1,0:T(8,128)(2,1)S(1)} fusion(bf16[64,65536]{1,0:T(8,128)(2,1)} %bitcast.64, s32[64]{0:T(128)S(1)} %get-tuple-element.10, s32[32]{0:T(128)S(1)} %fusion.73), kind=kOutput, calls=%fused_computation | convolution fusion | flops 270534656 | bytes 12583296 | tf_op jit(solution)/shard_map/dot_general | solution.py:102
  110.0 0.3 collective-permute-start
  110.4 7.1 %collective-permute-done = bf16[32,65536]{1,0:T(8,128)(2,1)S(1)} collective-permute-done((bf16[32,65536]{1,0:T(8,128)(2,1)S(1)}, bf16[32,65536]{1,0:T(8,128)(2,1)S(1)}, u32[]{:S(2)}, u32[]{:S(2)}) %collective-permute-start) | collective-permute-done | bytes 4194336 | tf_op jit(solution)/shard_map/ppermute | solution.py:103
  117.5 1.3 add_convert_fusion
  118.8 3.5 %copy.40 = bf16[4,8,128,512]{3,2,1,0:T(8,128)(2,1)} copy(bf16[4,8,128,512]{3,1,2,0:T(8,128)(2,1)S(1)} %bitcast.66) | data formatting | bytes 8388608
  122.4 10.2 %all-to-all-start.2 = ((bf16[32,128,512]{2,1,0:T(8,128)(2,1)}), bf16[32,128,512]{2,1,0:T(8,128)(2,1)}, u32[]{:S(2)}, u32[]{:S(2)}) async-start(bf16[32,128,512]{2,1,0:T(8,128)(2,1)} %bitcast.67), calls=%async_computation.2 | async-start | bytes 8388608 | tf_op jit(solution)/shard_map/all_to_all | solution.py:108
  132.6 0.2 slice_reduce_fusion
  132.8 0.6 fusion.24
  133.4 4.4 %fusion.25 = (s32[4096]{0:T(1024)S(1)}, s32[4096]{0:T(1024)S(1)}, s32[4096]{0:T(1024)S(1)}, s32[4096]{0:T(1024)S(1)}, s32[4096]{0:T(1024)S(1)}) fusion(f32[4096,4]{1,0:T(8,128)S(1)} %reshape.76), kind=kLoop, calls=%fused_computation.43 | loop fusion | flops 20480 | bytes 131072 | tf_op jit(solution)/shard_map/convert_element_type | solution.py:110
  137.8 1.8 fusion.7
  139.7 3.9 %fusion.17 = f32[128,512]{1,0:T(8,128)S(1)} fusion(s32[4096]{0:T(1024)S(1)} %get-tuple-element.6, s32[4096]{0:T(1024)S(1)} %get-tuple-element.8, bf16[4096]{0:T(1024)(128)(2,1)S(1)} %broadcast_select_fusion, s32[128]{0:T(128)S(1)} %iota_add_fusion, s32[4096]{0:T(1024)S(1)} %get-tuple-element.7, s32[4096]{0:T(1024)S(1)} %get-tuple-element.5), kind=kOutput, calls=%fused_computation.27 | convolution fusion | flops 549453824 | bytes 336384 | tf_op jit(solution)/shard_map/my,mx->yx/dot_general | solution.py:126
  143.6 83.5 %all-to-all-done.2 = bf16[32,128,512]{2,1,0:T(8,128)(2,1)} async-done(((bf16[32,128,512]{2,1,0:T(8,128)(2,1)}), bf16[32,128,512]{2,1,0:T(8,128)(2,1)}, u32[]{:S(2)}, u32[]{:S(2)}) %all-to-all-start.2) | async-done | bytes 4194336 | tf_op jit(solution)/shard_map/all_to_all | solution.py:108
  227.1 2.8 %convert_reduce_fusion = f32[128,512]{1,0:T(8,128)S(1)} fusion(bf16[32,128,512]{2,1,0:T(8,128)(2,1)} %all-to-all-done.2), kind=kLoop, calls=%fused_computation.13 | loop fusion | flops 4128768 | bytes 4456448 | tf_op jit(solution)/shard_map/reduce_sum | solution.py:109
  229.9 0.7 divide_bitcast_fusion
  (17 shorter events, 0.2 us)
Async XLA Ops:
  6.5 37.6 %copy-start = (bf16[4,256,256]{2,1,0:T(8,128)(2,1)S(1)}, bf16[4,256,256]{2,1,0:T(8,128)(2,1)}, u32[]{:S(2)}) copy-start(bf16[4,256,256]{2,1,0:T(8,128)(2,1)} %param.8) | copy-start | bytes 1572868
  10.5 9.5 %all-to-all-start = ((f32[4,1,86]{2,1,0:T(1,128)}), f32[4,1,86]{2,1,0:T(1,128)S(1)}, u32[]{:S(2)}, u32[]{:S(2)}) async-start(f32[4,1,86]{2,1,0:T(1,128)} %broadcast_in_dim.14), calls=%async_computation | async-start | bytes 4096 | tf_op jit(solution)/shard_map/all_to_all | solution.py:50
  14.8 19.5 %copy-start.3 = (bf16[10,41]{1,0:T(8,128)(2,1)S(1)}, bf16[10,41]{1,0:T(8,128)(2,1)}, u32[]{:S(2)}) copy-start(bf16[10,41]{1,0:T(8,128)(2,1)} %param.15) | copy-start | bytes 2464
  21.9 21.3 %all-to-all-start.1 = ((f32[64,1,344]{2,1,0:T(1,128)}), f32[64,1,344]{2,1,0:T(1,128)S(1)}, u32[]{:S(2)}, u32[]{:S(2)}) async-start(f32[64,1,344]{2,1,0:T(1,128)} %broadcast_in_dim.16), calls=%async_computation.1 | async-start | bytes 196608 | tf_op jit(solution)/shard_map/all_to_all | solution.py:52
  34.0 9.7 %copy-start.2 = (s32[4]{0:T(128)S(1)}, s32[4]{0:T(128)}, u32[]{:S(2)}) copy-start(s32[4]{0:T(128)} %param.9) | copy-start | bytes 52
  34.0 45.8 %all-gather.2.cloned.1.call-start = ((), (), s32[]{:S(2)}) async-start(), calls=%async_computation.3 | async-start | bytes 2621440 | tf_op jit(solution)/shard_map/all_gather | solution.py:80
  105.2 12.3 %copy-start.1 = (bf16[8,8,128,512]{3,1,2,0:T(8,128)(2,1)S(1)}, bf16[8,8,128,512]{3,1,2,0:T(8,128)(2,1)}, u32[]{:S(2)}) copy-start(bf16[8,8,128,512]{3,1,2,0:T(8,128)(2,1)} %copy.39) | copy-start | bytes 25165828
  110.0 7.5 %collective-permute-start = (bf16[32,65536]{1,0:T(8,128)(2,1)S(1)}, bf16[32,65536]{1,0:T(8,128)(2,1)S(1)}, u32[]{:S(2)}, u32[]{:S(2)}) collective-permute-start(bf16[32,65536]{1,0:T(8,128)(2,1)S(1)} %convolution_convert_fusion), channel_id=1, source_target_pairs={{0,4},{4,0},{1,5},{5,1},{2,6},{6,2},{3,7},{7,3},{8,12},{12,8},{9,1... | collective-permute-start | bytes 12582920 | tf_op jit(solution)/shard_map/ppermute | solution.py:103
  122.4 104.8 %all-to-all-start.2 = ((bf16[32,128,512]{2,1,0:T(8,128)(2,1)}), bf16[32,128,512]{2,1,0:T(8,128)(2,1)}, u32[]{:S(2)}, u32[]{:S(2)}) async-start(bf16[32,128,512]{2,1,0:T(8,128)(2,1)} %bitcast.67), calls=%async_computation.2 | async-start | bytes 8388608 | tf_op jit(solution)/shard_map/all_to_all | solution.py:108
Sparse Core Ops, SparseCore 0:
  52.2 27.5 all-gather.1

commit v11 on v10

--- a/solution.py
+++ b/solution.py
@@ -59,6 +59,7 @@
     hband = band_matrix(horiz_taps, tile_side)
 
     rows_pass = jnp.einsum("tyk,bxk->tybx", tiles, hband, preferred_element_type=jnp.float32)
+    rows_pass = lax.optimization_barrier(rows_pass)
 
     exposures = packed.shape[0]
     picker = (tile_exposure[:, None] == jnp.arange(exposures, dtype=jnp.int32)[None, :]).astype(

time: 242 us -> 243 us (level); the launches traced: 238 us -> 242 us
  matrix products: 38.3 us -> 41.5 us
    dot_general x0 -> x1, matrix products: none -> 5.79 us  [per_device(): jnp.einsum('tyk,bxk->tybx', tiles, hband, preferred_element_type=jnp.floa...]
    all_to_all x1, waiting for transfers between devices: 2.56 us -> 0.01 us  [per_device(): lax.all_to_all(payload, 'grp', split_axis=0, concat_axis=0, tiled=True)]
  transfers between devices with their start and end apart: 5 -> 5, of which waited for: 5 -> 4; matrix products, arithmetic and copies ran while one was open for 8% -> 9% of each run, Pallas kernels for 0% -> 0%
where the time goes in v11:
time: 243 us; the launch traced here: 242 us
  waiting for transfers between devices  126 us (52%)
  matrix products  41.5 us (17%)
  starting transfers between devices  27 us (11%)
  local copies, waits for them, and re-layouts  22 us (9%)
  between operations  13.6 us (6%)
  other arithmetic  11.2 us (5%)
    all_to_all x1, waiting for transfers between devices, per_device(): lax.all_to_all(pair.astype(jnp.bfloat16), CHIP, split_axis=0, concat_axis...  83.4 us
    all_gather x1, waiting for transfers between devices, per_device(): row_tiles = lax.all_gather(weighted, 'grp', axis=0, tiled=True)  28.6 us
    unnamed x10, local copies, waits for them, and re-layouts  15.3 us
    all_to_all x1, starting transfers between devices, per_device(): lax.all_to_all(payload, EXP, split_axis=0, concat_axis=0, tiled=True)  12.1 us
    dot_general x1, matrix products, per_device(): jnp.einsum('kyx,kxX->kyX', got_slabs, shifter, preferred_element_type=jnp...  10.3 us
    all_to_all x1, starting transfers between devices, per_device(): lax.all_to_all(pair.astype(jnp.bfloat16), CHIP, split_axis=0, concat_axis...  10.2 us
    all_to_all x1, waiting for transfers between devices, per_device(): lax.all_to_all(payload, EXP, split_axis=0, concat_axis=0, tiled=True)  7.26 us
    ppermute x1, waiting for transfers between devices, per_device(): lax.ppermute(give.astype(jnp.bfloat16), 'ec', perm=[(0, 1), (1, 0)])  7.13 us
  transfers between devices with their start and end apart: 5, of which 4 were waited for; matrix products, arithmetic and copies ran while one was open for 9% of the time, Pallas kernels for 0%

profile of v11, /device:TPU:8, one launch (start us, length us, event | category | flops | bytes accessed | tf_op | source)
XLA Modules:
  0.0 241.7 jit_solution(1028108661394052426)
XLA Ops:
  6.5 0.8 copy.25
  7.4 0.7 maximum_convert_fusion
  8.1 0.1 reshape.79
  8.2 0.7 stack_broadcast_in_dim.2
  8.9 0.7 add_convert_fusion.1
  9.6 0.1 copy.27
  9.7 0.1 convert_element_type.129
  9.9 0.6 broadcast_in_dim.14
  10.5 4.3 %all-to-all-start = ((f32[4,1,86]{2,1,0:T(1,128)}), f32[4,1,86]{2,1,0:T(1,128)S(1)}, u32[]{:S(2)}, u32[]{:S(2)}) async-start(f32[4,1,86]{2,1,0:T(1,128)} %broadcast_in_dim.14), calls=%async_computation | async-start | bytes 4096 | tf_op jit(solution)/shard_map/all_to_all | solution.py:50
  14.8 2.6 %convert_bitcast_fusion.1 = bf16[10,256,256,1]{2,0,1,3:T(8,128)(2,1)S(1)} fusion(bf16[10,41]{1,0:T(8,128)(2,1)} %param.15), kind=kOutput, calls=%fused_computation.40 | convolution fusion | flops 62455808 | bytes 1311540 | tf_op jit(solution)/shard_map/bd,dij->bij/dot_general | solution.py:19
  17.4 5.8 %convolution_bitcast_fusion = f32[4,256,10,256]{1,3,0,2:T(8,128)} fusion(bf16[10,256,256,1]{2,0,1,3:T(8,128)(2,1)S(1)} %convert_bitcast_fusion.1, bf16[4,256,256]{2,1,0:T(8,128)(2,1)S(1)} %copy-done), kind=kOutput, calls=%fused_computation.27 | convolution fusion | flops 1342177280 | bytes 12320768 | tf_op jit(solution)/shard_map/tyk,bxk->tybx/dot_general | solution.py:61
  23.2 0.5 broadcast.86
  23.7 0.7 reduce.26
  24.4 0.1 broadcast_in_dim.15
  24.4 0.7 broadcast_in_dim.16
  25.1 12.1 %all-to-all-start.1 = ((f32[64,1,344]{2,1,0:T(1,128)}), f32[64,1,344]{2,1,0:T(1,128)S(1)}, u32[]{:S(2)}, u32[]{:S(2)}) async-start(f32[64,1,344]{2,1,0:T(1,128)} %broadcast_in_dim.16), calls=%async_computation.1 | async-start | bytes 196608 | tf_op jit(solution)/shard_map/all_to_all | solution.py:52
  37.3 1.9 convert_bitcast_fusion
  39.2 7.3 %all-to-all-done.1 = f32[64,1,344]{2,1,0:T(1,128)S(1)} async-done(((f32[64,1,344]{2,1,0:T(1,128)}), f32[64,1,344]{2,1,0:T(1,128)S(1)}, u32[]{:S(2)}, u32[]{:S(2)}) %all-to-all-start.1) | async-done | bytes 88096 | tf_op jit(solution)/shard_map/all_to_all | solution.py:52
  46.5 0.2 reduce.1
  46.7 0.1 reshape.75
  46.8 0.1 convert_element_type.134
  46.9 0.2 fusion.51
  47.1 0.2 slice_reduce_fusion.1
  47.3 0.1 copy.29
  47.4 5.7 %fusion.30 = bf16[4,256,256]{1,2,0:T(8,128)(2,1)S(1)} fusion(bf16[10,256,256,1]{2,0,1,3:T(8,128)(2,1)S(1)} %convert_bitcast_fusion, f32[4,256,10,256]{1,3,0,2:T(8,128)} %convolution_bitcast_fusion, f32[4,10]{0,1:T(8,128)S(1)} %copy.29, f32[4]{0:T(128)S(1)} %slice_reduce_fusion.1), kind=kOutput, calls=%fused_computation.49 | convolution fusion | flops 1347944448 | bytes 12320944 | tf_op jit(solution)/shard_map/byk,tkbx->tyx/dot_general | solution.py:73
  53.1 1.0 copy.31
  54.2 0.1 slice.52
  54.3 1.1 reshape.76
  55.4 0.2 fusion.41
  55.6 0.1 convert_element_type.133
  55.7 28.6 %all-gather.2.cloned.1.call-done = bf16[16,256,256]{2,1,0:T(8,128)(2,1)} async-done(((bf16[4,256,256]{2,1,0:T(8,128)(2,1)}), bf16[16,256,256]{2,1,0:T(8,128)(2,1)}) %all-gather.2.cloned.1.call-update) | async-done | bytes 2097168 | tf_op jit(solution)/shard_map/all_gather | solution.py:81
  84.3 3.2 %fusion.16 = bf16[16,4,128,256]{3,2,1,0:T(8,128)(2,1)S(1)} fusion(s32[16,4]{1,0:T(8,128)S(1)} %convert_element_type.133, s32[128]{0:T(128)S(1)} %iota_add_fusion, bf16[16,256,256]{2,1,0:T(8,128)(2,1)} %all-gather.2.cloned.1.call-done), kind=kOutput, calls=%fused_computation.28 | convolution fusion | flops 1080033280 | bytes 6292224 | tf_op jit(solution)/shard_map/sjiy,syx->sjix/dot_general | solution.py:90
  87.5 10.3 %fusion.7 = bf16[64,128,512]{2,1,0:T(8,128)(2,1)} fusion(bf16[64,128,256]{2,1,0:T(8,128)(2,1)S(1)} %bitcast.61, s32[64]{0:T(128)S(1)} %get-tuple-element.12), kind=kOutput, calls=%fused_computation.18 | convolution fusion | flops 2168455168 | bytes 12583168 | tf_op jit(solution)/shard_map/kyx,kxX->kyX/dot_general | solution.py:97
  97.8 11.7 %copy.39 = bf16[8,8,128,512]{3,1,2,0:T(8,128)(2,1)} copy(bf16[8,8,128,512]{3,2,1,0:T(8,128)(2,1)} %bitcast.56) | data formatting | bytes 16777216
  109.5 4.8 %convolution_convert_fusion = bf16[32,65536]{1,0:T(8,128)(2,1)S(1)} fusion(bf16[64,65536]{1,0:T(8,128)(2,1)} %bitcast.52, s32[64]{0:T(128)S(1)} %get-tuple-element.10, s32[32]{0:T(128)S(1)} %fusion.55), kind=kOutput, calls=%fused_computation | convolution fusion | flops 270534656 | bytes 12583296 | tf_op jit(solution)/shard_map/dot_general | solution.py:103
  114.4 0.3 collective-permute-start
  114.7 7.1 %collective-permute-done = bf16[32,65536]{1,0:T(8,128)(2,1)S(1)} collective-permute-done((bf16[32,65536]{1,0:T(8,128)(2,1)S(1)}, bf16[32,65536]{1,0:T(8,128)(2,1)S(1)}, u32[]{:S(2)}, u32[]{:S(2)}) %collective-permute-start) | collective-permute-done | bytes 4194336 | tf_op jit(solution)/shard_map/ppermute | solution.py:104
  121.8 1.3 add_convert_fusion
  123.1 3.5 %copy.40 = bf16[4,8,128,512]{3,2,1,0:T(8,128)(2,1)} copy(bf16[4,8,128,512]{3,1,2,0:T(8,128)(2,1)S(1)} %bitcast.54) | data formatting | bytes 8388608
  126.7 10.2 %all-to-all-start.2 = ((bf16[32,128,512]{2,1,0:T(8,128)(2,1)}), bf16[32,128,512]{2,1,0:T(8,128)(2,1)}, u32[]{:S(2)}, u32[]{:S(2)}) async-start(bf16[32,128,512]{2,1,0:T(8,128)(2,1)} %bitcast.55), calls=%async_computation.2 | async-start | bytes 8388608 | tf_op jit(solution)/shard_map/all_to_all | solution.py:109
  136.9 0.2 slice_reduce_fusion
  137.1 0.6 fusion.20
  137.7 4.4 %fusion.21 = (s32[4096]{0:T(1024)S(1)}, s32[4096]{0:T(1024)S(1)}, s32[4096]{0:T(1024)S(1)}, s32[4096]{0:T(1024)S(1)}, s32[4096]{0:T(1024)S(1)}) fusion(f32[4096,4]{1,0:T(8,128)S(1)} %reshape.76), kind=kLoop, calls=%fused_computation.42 | loop fusion | flops 20480 | bytes 131072 | tf_op jit(solution)/shard_map/convert_element_type | solution.py:111
  142.2 1.8 fusion.6
  144.0 3.9 %fusion.15 = f32[128,512]{1,0:T(8,128)S(1)} fusion(s32[4096]{0:T(1024)S(1)} %get-tuple-element.6, s32[4096]{0:T(1024)S(1)} %get-tuple-element.8, bf16[4096]{0:T(1024)(128)(2,1)S(1)} %broadcast_select_fusion, s32[128]{0:T(128)S(1)} %iota_add_fusion, s32[4096]{0:T(1024)S(1)} %get-tuple-element.7, s32[4096]{0:T(1024)S(1)} %get-tuple-element.5), kind=kOutput, calls=%fused_computation.26 | convolution fusion | flops 549453824 | bytes 336384 | tf_op jit(solution)/shard_map/my,mx->yx/dot_general | solution.py:127
  147.9 83.4 %all-to-all-done.2 = bf16[32,128,512]{2,1,0:T(8,128)(2,1)} async-done(((bf16[32,128,512]{2,1,0:T(8,128)(2,1)}), bf16[32,128,512]{2,1,0:T(8,128)(2,1)}, u32[]{:S(2)}, u32[]{:S(2)}) %all-to-all-start.2) | async-done | bytes 4194336 | tf_op jit(solution)/shard_map/all_to_all | solution.py:109
  231.3 2.8 %convert_reduce_fusion = f32[128,512]{1,0:T(8,128)S(1)} fusion(bf16[32,128,512]{2,1,0:T(8,128)(2,1)} %all-to-all-done.2), kind=kLoop, calls=%fused_computation.12 | loop fusion | flops 4128768 | bytes 4456448 | tf_op jit(solution)/shard_map/reduce_sum | solution.py:110
  234.1 0.7 divide_bitcast_fusion
  (18 shorter events, 0.2 us)
Async XLA Ops:
  6.5 10.8 %copy-start = (bf16[4,256,256]{2,1,0:T(8,128)(2,1)S(1)}, bf16[4,256,256]{2,1,0:T(8,128)(2,1)}, u32[]{:S(2)}) copy-start(bf16[4,256,256]{2,1,0:T(8,128)(2,1)} %param.8) | copy-start | bytes 1572868
  10.5 12.7 %all-to-all-start = ((f32[4,1,86]{2,1,0:T(1,128)}), f32[4,1,86]{2,1,0:T(1,128)S(1)}, u32[]{:S(2)}, u32[]{:S(2)}) async-start(f32[4,1,86]{2,1,0:T(1,128)} %broadcast_in_dim.14), calls=%async_computation | async-start | bytes 4096 | tf_op jit(solution)/shard_map/all_to_all | solution.py:50
  17.4 19.9 %copy-start.3 = (bf16[10,41]{1,0:T(8,128)(2,1)S(1)}, bf16[10,41]{1,0:T(8,128)(2,1)}, u32[]{:S(2)}) copy-start(bf16[10,41]{1,0:T(8,128)(2,1)} %param.14) | copy-start | bytes 2464
  25.1 21.3 %all-to-all-start.1 = ((f32[64,1,344]{2,1,0:T(1,128)}), f32[64,1,344]{2,1,0:T(1,128)S(1)}, u32[]{:S(2)}, u32[]{:S(2)}) async-start(f32[64,1,344]{2,1,0:T(1,128)} %broadcast_in_dim.16), calls=%async_computation.1 | async-start | bytes 196608 | tf_op jit(solution)/shard_map/all_to_all | solution.py:52
  37.3 9.7 %copy-start.2 = (s32[4]{0:T(128)S(1)}, s32[4]{0:T(128)}, u32[]{:S(2)}) copy-start(s32[4]{0:T(128)} %param.9) | copy-start | bytes 52
  37.3 47.0 %all-gather.2.cloned.1.call-start = ((), (), s32[]{:S(2)}) async-start(), calls=%async_computation.3 | async-start | bytes 2621440 | tf_op jit(solution)/shard_map/all_gather | solution.py:81
  109.5 12.3 %copy-start.1 = (bf16[8,8,128,512]{3,1,2,0:T(8,128)(2,1)S(1)}, bf16[8,8,128,512]{3,1,2,0:T(8,128)(2,1)}, u32[]{:S(2)}) copy-start(bf16[8,8,128,512]{3,1,2,0:T(8,128)(2,1)} %copy.39) | copy-start | bytes 25165828
  114.4 7.5 %collective-permute-start = (bf16[32,65536]{1,0:T(8,128)(2,1)S(1)}, bf16[32,65536]{1,0:T(8,128)(2,1)S(1)}, u32[]{:S(2)}, u32[]{:S(2)}) collective-permute-start(bf16[32,65536]{1,0:T(8,128)(2,1)S(1)} %convolution_convert_fusion), channel_id=1, source_target_pairs={{0,4},{4,0},{1,5},{5,1},{2,6},{6,2},{3,7},{7,3},{8,12},{12,8},{9,1... | collective-permute-start | bytes 12582920 | tf_op jit(solution)/shard_map/ppermute | solution.py:104
  126.7 104.6 %all-to-all-start.2 = ((bf16[32,128,512]{2,1,0:T(8,128)(2,1)}), bf16[32,128,512]{2,1,0:T(8,128)(2,1)}, u32[]{:S(2)}, u32[]{:S(2)}) async-start(bf16[32,128,512]{2,1,0:T(8,128)(2,1)} %bitcast.55), calls=%async_computation.2 | async-start | bytes 8388608 | tf_op jit(solution)/shard_map/all_to_all | solution.py:109
Sparse Core Ops, SparseCore 0:
  54.3 29.9 all-gather.1

commit v12 on v10

--- a/solution.py
+++ b/solution.py
@@ -99,10 +99,10 @@
     chip_patch = n_halves * jnp.arange(chips, dtype=jnp.int32)[:, None]
     flat_shifted = shifted.reshape(entries, band_rows * PS)
     give_of = (got_patch[None, :] == chip_patch + (1 - h)).astype(jnp.bfloat16)
-    give = jnp.dot(give_of, flat_shifted, preferred_element_type=jnp.float32)
+    give = jnp.einsum("pk,kyX->pyX", give_of, shifted, preferred_element_type=jnp.float32)
     got_give = lax.ppermute(give.astype(jnp.bfloat16), "ec", perm=[(0, 1), (1, 0)])
     keep_of = (got_patch[None, :] == chip_patch + h).astype(jnp.bfloat16)
-    keep = jnp.dot(keep_of, flat_shifted, preferred_element_type=jnp.float32)
+    keep = jnp.einsum("pk,kyX->pyX", keep_of, shifted, preferred_element_type=jnp.float32)
 
     pair = (keep + got_give.astype(jnp.float32)).reshape(chips, band_rows, PS)
     recv_bands = lax.all_to_all(pair.astype(jnp.bfloat16), CHIP, split_axis=0, concat_axis=0, tiled=True)

time: 242 us -> 243 us (level)
  matrix products: 38.3 us -> 51 us
  local copies, waits for them, and re-layouts: 22 us -> 11.1 us
    unnamed x10 -> x6, local copies, waits for them, and re-layouts: 15.3 us -> 0.01 us
    dot_general x2, matrix products: 6.13 us -> 16.4 us  [the longest x1 9.99 us: per_device(): jnp.einsum('pk,kyX->pyX', give_of, shifted, preferred_element_type=jnp.fl...]
    convert_element_type x0 -> x1, local copies, waits for them, and re-layouts: none -> 4.35 us  [per_device(): pair.astype(jnp.bfloat16)]
where the time goes in v12:
time: 243 us; the launch traced here: 239 us
  waiting for transfers between devices  125 us (51%)
  matrix products  51 us (21%)
  starting transfers between devices  26.9 us (11%)
  between operations  13.8 us (6%)
  other arithmetic  11.2 us (5%)
  local copies, waits for them, and re-layouts  11.1 us (5%)
    all_to_all x1, waiting for transfers between devices, per_device(): lax.all_to_all(pair.astype(jnp.bfloat16), CHIP, split_axis=0, concat_axis...  83.4 us
    all_gather x1, waiting for transfers between devices, per_device(): row_tiles = lax.all_gather(weighted, 'grp', axis=0, tiled=True)  26.2 us
    all_to_all x1, starting transfers between devices, per_device(): lax.all_to_all(payload, EXP, split_axis=0, concat_axis=0, tiled=True)  12.1 us
    dot_general x1, matrix products, per_device(): jnp.einsum('kyx,kxX->kyX', got_slabs, shifter, preferred_element_type=jnp...  10.9 us
    all_to_all x1, starting transfers between devices, per_device(): lax.all_to_all(pair.astype(jnp.bfloat16), CHIP, split_axis=0, concat_axis...  10.2 us
    dot_general x1, matrix products, per_device(): jnp.einsum('pk,kyX->pyX', give_of, shifted, preferred_element_type=jnp.fl...  9.99 us
    ppermute x1, waiting for transfers between devices, per_device(): lax.ppermute(give.astype(jnp.bfloat16), 'ec', perm=[(0, 1), (1, 0)])  7.13 us
    dot_general x1, matrix products, per_device(): jnp.einsum('byk,tkbx->tyx', vband, partial_value, preferred_element_type=...  6.72 us
  transfers between devices with their start and end apart: 5, of which 5 were waited for; matrix products, arithmetic and copies ran while one was open for 8% of the time, Pallas kernels for 0%

profile of v12, /device:TPU:8, one launch (start us, length us, event | category | flops | bytes accessed | tf_op | source)
XLA Modules:
  0.0 239.0 jit_solution(3704284645141947513)
XLA Ops:
  6.5 0.8 copy.31
  7.4 0.7 maximum_convert_fusion
  8.1 0.1 reshape.73
  8.2 0.7 stack_broadcast_in_dim.2
  8.9 0.7 add_convert_fusion.1
  9.6 0.1 copy.33
  9.7 0.1 convert_element_type.126
  9.9 0.6 broadcast_in_dim.14
  10.5 4.3 %all-to-all-start = ((f32[4,1,86]{2,1,0:T(1,128)}), f32[4,1,86]{2,1,0:T(1,128)S(1)}, u32[]{:S(2)}, u32[]{:S(2)}) async-start(f32[4,1,86]{2,1,0:T(1,128)} %broadcast_in_dim.14), calls=%async_computation | async-start | bytes 4096 | tf_op jit(solution)/shard_map/all_to_all | solution.py:50
  14.8 2.6 %convert_bitcast_fusion = bf16[10,256,256,1]{2,0,1,3:T(8,128)(2,1)S(1)} fusion(bf16[10,41]{1,0:T(8,128)(2,1)} %param.14), kind=kOutput, calls=%fused_computation.44 | convolution fusion | flops 62455808 | bytes 1311540 | tf_op jit(solution)/shard_map/bd,dij->bij/dot_general | solution.py:19
  17.4 2.6 %all-to-all-done = f32[4,1,86]{2,1,0:T(1,128)S(1)} async-done(((f32[4,1,86]{2,1,0:T(1,128)}), f32[4,1,86]{2,1,0:T(1,128)S(1)}, u32[]{:S(2)}, u32[]{:S(2)}) %all-to-all-start) | async-done | bytes 1408 | tf_op jit(solution)/shard_map/all_to_all | solution.py:50
  19.9 0.5 broadcast.86
  20.5 0.7 reduce.26
  21.1 0.1 broadcast_in_dim.15
  21.2 0.7 broadcast_in_dim.16
  21.9 12.1 %all-to-all-start.1 = ((f32[64,1,344]{2,1,0:T(1,128)}), f32[64,1,344]{2,1,0:T(1,128)S(1)}, u32[]{:S(2)}, u32[]{:S(2)}) async-start(f32[64,1,344]{2,1,0:T(1,128)} %broadcast_in_dim.16), calls=%async_computation.1 | async-start | bytes 196608 | tf_op jit(solution)/shard_map/all_to_all | solution.py:52
  34.0 0.2 all-gather.2.cloned.1.call-start
  34.3 3.3 %convert_bitcast_fusion.1 = bf16[10,256,256,1]{2,0,1,3:T(8,128)(2,1)} fusion(bf16[10,41]{1,0:T(8,128)(2,1)S(1)} %copy-done.2), kind=kOutput, calls=%fused_computation.45 | convolution fusion | flops 62455808 | bytes 1311540 | tf_op jit(solution)/shard_map/bd,dij->bij/dot_general | solution.py:19
  37.5 5.7 %all-to-all-done.1 = f32[64,1,344]{2,1,0:T(1,128)S(1)} async-done(((f32[64,1,344]{2,1,0:T(1,128)}), f32[64,1,344]{2,1,0:T(1,128)S(1)}, u32[]{:S(2)}, u32[]{:S(2)}) %all-to-all-start.1) | async-done | bytes 88096 | tf_op jit(solution)/shard_map/all_to_all | solution.py:52
  43.2 0.2 reduce.1
  43.5 0.1 reshape.70
  43.6 0.1 convert_element_type.131
  43.7 0.2 fusion.77
  43.9 0.2 slice_reduce_fusion.1
  44.1 0.1 copy.35
  44.2 6.7 %fusion.52 = bf16[4,256,256]{1,2,0:T(8,128)(2,1)S(1)} fusion(bf16[10,256,256,1]{2,0,1,3:T(8,128)(2,1)S(1)} %convert_bitcast_fusion, f32[4,10]{0,1:T(8,128)S(1)} %copy.35, bf16[10,256,256,1]{2,0,1,3:T(8,128)(2,1)} %convert_bitcast_fusion.1, bf16[4,256,256]{2,1,0:T(8,128)(2,1)S(1)} %copy-done, f32[4]{0:T(128)S(1)} %slice_reduce_fusion.1), kind=kOutput, calls=%fused_computation.54 | convolution fusion | flops 2690121728 | bytes 3670192 | tf_op jit(solution)/shard_map/byk,tkbx->tyx/dot_general | solution.py:72
  50.9 1.0 copy.37
  52.0 0.1 slice.52
  52.1 1.1 reshape.71
  53.2 0.2 fusion.68
  53.4 0.1 convert_element_type.130
  53.5 26.2 %all-gather.2.cloned.1.call-done = bf16[16,256,256]{2,1,0:T(8,128)(2,1)} async-done(((bf16[4,256,256]{2,1,0:T(8,128)(2,1)}), bf16[16,256,256]{2,1,0:T(8,128)(2,1)}) %all-gather.2.cloned.1.call-update) | async-done | bytes 2097168 | tf_op jit(solution)/shard_map/all_gather | solution.py:80
  79.7 5.2 %fusion.29 = bf16[16,4,128,256]{3,2,1,0:T(8,128)(2,1)} fusion(s32[16,4]{1,0:T(8,128)S(1)} %convert_element_type.130, s32[128]{0:T(128)S(1)} %iota_add_fusion, bf16[16,256,256]{2,1,0:T(8,128)(2,1)} %all-gather.2.cloned.1.call-done), kind=kOutput, calls=%fused_computation.33 | convolution fusion | flops 1080033280 | bytes 6292224 | tf_op jit(solution)/shard_map/sjiy,syx->sjix/dot_general | solution.py:89
  84.9 10.9 %fusion.12 = bf16[64,128,512]{2,1,0:T(8,128)(2,1)S(1)} fusion(bf16[64,128,256]{2,1,0:T(8,128)(2,1)} %bitcast.68, s32[64]{0:T(128)S(1)} %get-tuple-element.12), kind=kOutput, calls=%fused_computation.22 | convolution fusion | flops 2168455168 | bytes 12583168 | tf_op jit(solution)/shard_map/kyx,kxX->kyX/dot_general | solution.py:96
  95.7 10.0 %fusion.24 = bf16[32,128,512]{2,0,1:T(8,128)(2,1)S(1)} fusion(bf16[64,128,512]{2,1,0:T(8,128)(2,1)S(1)} %fusion.12, s32[64]{0:T(128)S(1)} %get-tuple-element.10, s32[32]{0:T(128)S(1)} %fusion.81), kind=kOutput, calls=%fused_computation.32 | convolution fusion | flops 270534656 | bytes 12583296 | tf_op jit(solution)/shard_map/pk,kyX->pyX/dot_general | solution.py:102
  105.7 0.1 collective-permute-start
  105.8 7.1 %collective-permute-done = bf16[32,128,512]{2,0,1:T(8,128)(2,1)S(1)} collective-permute-done((bf16[32,128,512]{2,0,1:T(8,128)(2,1)S(1)}, bf16[32,128,512]{2,0,1:T(8,128)(2,1)S(1)}, u32[]{:S(2)}, u32[]{:S(2)}) %collective-permute-start) | collective-permute-done | bytes 4194336 | tf_op jit(solution)/shard_map/ppermute | solution.py:103
  113.0 6.4 %add_convert_fusion = bf16[32,128,512]{2,0,1:T(8,128)(2,1)S(1)} fusion(bf16[32,128,512]{2,0,1:T(8,128)(2,1)S(1)} %collective-permute-done, bf16[64,128,512]{2,1,0:T(8,128)(2,1)S(1)} %fusion.12, s32[64]{0:T(128)S(1)} %get-tuple-element.10, s32[32]{0:T(128)S(1)} %fusion.82), kind=kOutput, calls=%fused_computation.13 | convolution fusion | flops 274728960 | bytes 16777600 | tf_op jit(solution)/shard_map/pk,kyX->pyX/dot_general | solution.py:105
  119.4 4.3 %copy.40 = bf16[32,128,512]{2,1,0:T(8,128)(2,1)} copy(bf16[32,128,512]{2,0,1:T(8,128)(2,1)S(1)} %add_convert_fusion) | data formatting | bytes 8388608 | tf_op jit(solution)/shard_map/convert_element_type | solution.py:108
  123.8 10.2 %all-to-all-start.2 = ((bf16[32,128,512]{2,1,0:T(8,128)(2,1)}), bf16[32,128,512]{2,1,0:T(8,128)(2,1)}, u32[]{:S(2)}, u32[]{:S(2)}) async-start(bf16[32,128,512]{2,1,0:T(8,128)(2,1)} %copy.40), calls=%async_computation.2 | async-start | bytes 8388608 | tf_op jit(solution)/shard_map/all_to_all | solution.py:108
  134.0 0.2 slice_reduce_fusion
  134.2 0.6 fusion.33
  134.8 4.4 %fusion.34 = (s32[4096]{0:T(1024)S(1)}, s32[4096]{0:T(1024)S(1)}, s32[4096]{0:T(1024)S(1)}, s32[4096]{0:T(1024)S(1)}, s32[4096]{0:T(1024)S(1)}) fusion(f32[4096,4]{1,0:T(8,128)S(1)} %reshape.71), kind=kLoop, calls=%fused_computation.47 | loop fusion | flops 20480 | bytes 131072 | tf_op jit(solution)/shard_map/convert_element_type | solution.py:110
  139.3 1.8 fusion.7
  141.1 3.9 %fusion.21 = f32[128,512]{1,0:T(8,128)S(1)} fusion(s32[4096]{0:T(1024)S(1)} %get-tuple-element.6, s32[4096]{0:T(1024)S(1)} %get-tuple-element.8, bf16[4096]{0:T(1024)(128)(2,1)S(1)} %broadcast_select_fusion, s32[128]{0:T(128)S(1)} %iota_add_fusion, s32[4096]{0:T(1024)S(1)} %get-tuple-element.7, s32[4096]{0:T(1024)S(1)} %get-tuple-element.5), kind=kOutput, calls=%fused_computation.30 | convolution fusion | flops 549453824 | bytes 336384 | tf_op jit(solution)/shard_map/my,mx->yx/dot_general | solution.py:126
  145.0 83.4 %all-to-all-done.2 = bf16[32,128,512]{2,1,0:T(8,128)(2,1)} async-done(((bf16[32,128,512]{2,1,0:T(8,128)(2,1)}), bf16[32,128,512]{2,1,0:T(8,128)(2,1)}, u32[]{:S(2)}, u32[]{:S(2)}) %all-to-all-start.2) | async-done | bytes 4194336 | tf_op jit(solution)/shard_map/all_to_all | solution.py:108
  228.4 2.8 %convert_reduce_fusion = f32[128,512]{1,0:T(8,128)S(1)} fusion(bf16[32,128,512]{2,1,0:T(8,128)(2,1)} %all-to-all-done.2), kind=kLoop, calls=%fused_computation.12 | loop fusion | flops 4128768 | bytes 4456448 | tf_op jit(solution)/shard_map/reduce_sum | solution.py:109
  231.2 0.7 divide_bitcast_fusion
  (14 shorter events, 0.1 us)
Async XLA Ops:
  6.5 37.6 %copy-start = (bf16[4,256,256]{2,1,0:T(8,128)(2,1)S(1)}, bf16[4,256,256]{2,1,0:T(8,128)(2,1)}, u32[]{:S(2)}) copy-start(bf16[4,256,256]{2,1,0:T(8,128)(2,1)} %param.8) | copy-start | bytes 1572868
  10.5 9.5 %all-to-all-start = ((f32[4,1,86]{2,1,0:T(1,128)}), f32[4,1,86]{2,1,0:T(1,128)S(1)}, u32[]{:S(2)}, u32[]{:S(2)}) async-start(f32[4,1,86]{2,1,0:T(1,128)} %broadcast_in_dim.14), calls=%async_computation | async-start | bytes 4096 | tf_op jit(solution)/shard_map/all_to_all | solution.py:50
  14.8 19.5 %copy-start.2 = (bf16[10,41]{1,0:T(8,128)(2,1)S(1)}, bf16[10,41]{1,0:T(8,128)(2,1)}, u32[]{:S(2)}) copy-start(bf16[10,41]{1,0:T(8,128)(2,1)} %param.15) | copy-start | bytes 2464
  21.9 21.3 %all-to-all-start.1 = ((f32[64,1,344]{2,1,0:T(1,128)}), f32[64,1,344]{2,1,0:T(1,128)S(1)}, u32[]{:S(2)}, u32[]{:S(2)}) async-start(f32[64,1,344]{2,1,0:T(1,128)} %broadcast_in_dim.16), calls=%async_computation.1 | async-start | bytes 196608 | tf_op jit(solution)/shard_map/all_to_all | solution.py:52
  34.0 9.7 %copy-start.1 = (s32[4]{0:T(128)S(1)}, s32[4]{0:T(128)}, u32[]{:S(2)}) copy-start(s32[4]{0:T(128)} %param.9) | copy-start | bytes 52
  34.0 45.7 %all-gather.2.cloned.1.call-start = ((), (), s32[]{:S(2)}) async-start(), calls=%async_computation.3 | async-start | bytes 2621440 | tf_op jit(solution)/shard_map/all_gather | solution.py:80
  105.7 7.2 %collective-permute-start = (bf16[32,128,512]{2,0,1:T(8,128)(2,1)S(1)}, bf16[32,128,512]{2,0,1:T(8,128)(2,1)S(1)}, u32[]{:S(2)}, u32[]{:S(2)}) collective-permute-start(bf16[32,128,512]{2,0,1:T(8,128)(2,1)S(1)} %fusion.24), channel_id=1, source_target_pairs={{0,4},{4,0},{1,5},{5,1},{2,6},{6,2},{3,7},{7,3},{8,12},{12,8},{9,1... | collective-permute-start | bytes 12582920 | tf_op jit(solution)/shard_map/ppermute | solution.py:103
  123.8 104.7 %all-to-all-start.2 = ((bf16[32,128,512]{2,1,0:T(8,128)(2,1)}), bf16[32,128,512]{2,1,0:T(8,128)(2,1)}, u32[]{:S(2)}, u32[]{:S(2)}) async-start(bf16[32,128,512]{2,1,0:T(8,128)(2,1)} %copy.40), calls=%async_computation.2 | async-start | bytes 8388608 | tf_op jit(solution)/shard_map/all_to_all | solution.py:108
Sparse Core Ops, SparseCore 0:
  52.1 27.5 all-gather.1
